TPU v7x, 256 devices: a whole 4x4x8 slice. The times are simulated.
256 devices in a mesh: gy: 8 (over z), gx: 32 (over y, x, core).
Axes of the slice: x: 4, y: 4, z: 8, core: 2. Of those that a mesh axis runs over, the one named last changes fastest.
Arguments:
- saved_thickness: bfloat16 [2, 512, 8192], P(None, 'gy', 'gx'), may hold values from 0.5 to 2
- saved_velocity: bfloat16 [2, 2, 512, 8192], P(None, None, 'gy', 'gx'), may hold values from -4 to 4
- surface_slope: bfloat16 [2, 512, 8192], P(None, 'gy', 'gx'), may hold values from -3 to 3
- basal_beta: float32 [512, 8192], P('gy', 'gx'), may hold values from 0.2 to 5
- cell_mask: int32 [512, 8192], P('gy', 'gx'), may hold values from 0 to 2
- upwind_flags: int32 [512, 8192], P('gy', 'gx'), may hold values from 0 to 3
- observed_velocity: bfloat16 [2, 2, 512, 8192], P(None, None, 'gy', 'gx'), may hold values from -60 to 60
- thickness_adjoint: float32 [512, 8192], P('gy', 'gx'), may hold values from -6 to 6
Outputs:
- beta_gradient: float32 [512, 8192], P('gy', 'gx')
- thickness_gradient: float32 [512, 8192], P('gy', 'gx')
- misfit: float32 [], replicated
All inputs are finite; a program needn't handle non-finite values.
Results may differ from a plain program's by a relative error of at most 0.0003.
Values sent between devices are 32-bit elements; how exact they have to be, the bound alone decides.
No kernel may reach another device: no remote copies, remote signals or barrier semaphores. Data moves between devices by JAX's collectives and lax.ppermute only.
A program may use at most 64 MiB of HBM per device.

v0:
```python
import jax
import jax.numpy as jnp
from jax import lax
from jax.experimental import pallas as pl
from jax.experimental.pallas import tpu as pltpu
from jax.sharding import PartitionSpec as P

EPSILON = 1e-06
HALO = 12
LANES = 128


def padded_2(block, sides, width):
    for axis, dim in sides:
        count = lax.axis_size(axis)
        forward = [(i, i + 1) for i in range(count - 1)]
        backward = [(target, source) for source, target in forward]
        low = lax.ppermute(
            lax.slice_in_dim(block, block.shape[dim] - width, None, axis=dim), axis, forward
        )
        high = lax.ppermute(lax.slice_in_dim(block, 0, width, axis=dim), axis, backward)
        block = jnp.concatenate([low, block, high], axis=dim)
    return block


def butterfly_sum(values, axes):
    for axis in axes:
        count = lax.axis_size(axis)
        if count & (count - 1):
            values = lax.psum(values, axis)
            continue
        stride = 1
        while stride < count:
            values = values + lax.ppermute(values, axis, [(i, i ^ stride) for i in range(count)])
            stride *= 2
    return values


SWEEPS = 3
RELAXATION = 0.8
TIME_STEP = 0.1


def make_nb(roll):
    def nb(x, dr, dc):
        if dr:
            x = roll(x, (-dr) % x.shape[0], 0)
        if dc:
            x = roll(x, (-dc) % x.shape[1], 1)
        return x

    return nb


def edges(nb, u, v, h, cov, dr, dc):
    du = nb(u, dr, dc) - u
    dv = nb(v, dr, dc) - v
    s = du * du + dv * dv
    p = jnp.exp(jnp.log(1.0 + s) * (-1.0 / 3.0))
    a = 0.5 * (h + nb(h, dr, dc)) * cov * nb(cov, dr, dc)
    return du, dv, s, p, a, a * p


def sweep_terms(nb, u, v, h, cov, fric, fu, fv):
    de = edges(nb, u, v, h, cov, 0, 1)
    ds = edges(nb, u, v, h, cov, 1, 0)
    ce, cs = de[5], ds[5]
    fe_u, fe_v = ce * de[0], ce * de[1]
    fs_u, fs_v = cs * ds[0], cs * ds[1]
    flux_u = fe_u + fs_u - nb(fe_u, 0, -1) - nb(fs_u, -1, 0)
    flux_v = fe_v + fs_v - nb(fe_v, 0, -1) - nb(fs_v, -1, 0)
    c_sum = ce + cs + nb(ce, 0, -1) + nb(cs, -1, 0)
    r_u = fu - fric * u + flux_u
    r_v = fv - fric * v + flux_v
    d = 1.0 + fric + c_sum
    return de, ds, r_u, r_v, d


def sweep_fwd(nb, u, v, h, cov, fric, fu, fv):
    de, ds, r_u, r_v, d = sweep_terms(nb, u, v, h, cov, fric, fu, fv)
    return cov * (u + RELAXATION * r_u / d), cov * (v + RELAXATION * r_v / d)


def sweep_bwd(nb, u, v, h, cov, fric, su, sv, bu, bv):
    de, ds, r_u, r_v, d = sweep_terms(nb, u, v, h, cov, fric, h * su, h * sv)
    qu, qv = cov * bu, cov * bv
    tu, tv = RELAXATION * qu / d, RELAXATION * qv / d
    d_bar = -(tu * r_u + tv * r_v) / d
    f_bar = d_bar - (tu * u + tv * v)
    h_bar = tu * su + tv * sv
    wu = qu - fric * tu
    wv = qv - fric * tv
    for (du, dv, s, p, a, c), (dr, dc) in ((de, (0, 1)), (ds, (1, 0))):
        big_u = tu - nb(tu, dr, dc)
        big_v = tv - nb(tv, dr, dc)
        c_bar = big_u * du + big_v * dv + d_bar + nb(d_bar, dr, dc)
        a_bar = c_bar * p
        s_bar = c_bar * a * (-1.0 / 3.0) * p / (1.0 + s)
        gu = big_u * c + 2.0 * s_bar * du
        gv = big_v * c + 2.0 * s_bar * dv
        wu = wu - gu + nb(gu, -dr, -dc)
        wv = wv - gv + nb(gv, -dr, -dc)
        k = 0.5 * cov * nb(cov, dr, dc) * a_bar
        h_bar = h_bar + k + nb(k, -dr, -dc)
    return wu, wv, h_bar, f_bar


def transport_bwd(nb, u, v, h, cov, don_e, don_s, g):
    q = cov * g
    h_bar = q
    div_bar = -TIME_STEP * q
    u_bar = None
    v_bar = None
    for vel, don, (dr, dc) in ((u, don_e, (0, 1)), (v, don_s, (1, 0))):
        f_bar = div_bar - nb(div_bar, dr, dc)
        kk = cov * nb(cov, dr, dc)
        speed = 0.5 * (vel + nb(vel, dr, dc))
        hh = don * h + (1.0 - don) * nb(h, dr, dc)
        x = 0.5 * f_bar * kk * hh
        vb = x + nb(x, -dr, -dc)
        y = f_bar * speed * kk
        h_bar = h_bar + y * don + nb(y * (1.0 - don), -dr, -dc)
        if u_bar is None:
            u_bar = vb
        else:
            v_bar = vb
    return u_bar, v_bar, h_bar


def statics(f):
    mask = f["mask"]
    cov = (mask > 0.5).astype(jnp.float32)
    grounded = (mask > 1.5).astype(jnp.float32)
    flags = f["flags"]
    don_s = (flags > 1.5).astype(jnp.float32)
    don_e = flags - 2.0 * don_s
    fric = f["beta"] * grounded
    return cov, grounded, don_e, don_s, fric


def forward_all(nb, f, steps):
    cov, grounded, don_e, don_s, fric = statics(f)
    out = []
    for n in range(steps):
        h = f["thick"][n]
        u, v = f["vel"][n]
        fu, fv = h * f["slope"][0], h * f["slope"][1]
        for _ in range(SWEEPS):
            u, v = sweep_fwd(nb, u, v, h, cov, fric, fu, fv)
        out.append((u, v))
    return out


def backward_all(nb, f, steps, scales, g):
    cov, grounded, don_e, don_s, fric = statics(f)
    su, sv = f["slope"][0], f["slope"][1]
    beta = jnp.zeros_like(g)
    for n in reversed(range(steps)):
        h = f["thick"][n]
        u, v = f["vel"][n]
        fu, fv = h * su, h * sv
        states = []
        for _ in range(SWEEPS):
            states.append((u, v))
            u, v = sweep_fwd(nb, u, v, h, cov, fric, fu, fv)
        ou, ov = f["obs"][n]
        inv = 1.0 / scales[n]
        bu, bv, h_bar = transport_bwd(nb, u, v, h, cov, don_e, don_s, g)
        bu = bu + grounded * (u - ou) * inv
        bv = bv + grounded * (v - ov) * inv
        f_tot = jnp.zeros_like(g)
        for k in reversed(range(SWEEPS)):
            wu, wv = states[k]
            bu, bv, hb, fb = sweep_bwd(nb, wu, wv, h, cov, fric, su, sv, bu, bv)
            h_bar = h_bar + hb
            f_tot = f_tot + fb
        beta = beta + grounded * f_tot
        g = h_bar
    return beta, g


def unpack(arr, steps):
    return {
        "mask": arr[0],
        "flags": arr[1],
        "beta": arr[2],
        "slope": (arr[3], arr[4]),
        "thick": [arr[5 + n] for n in range(steps)],
        "vel": [(arr[5 + steps + 2 * n], arr[6 + steps + 2 * n]) for n in range(steps)],
        "obs": [(arr[5 + 3 * steps + 2 * n], arr[6 + 3 * steps + 2 * n]) for n in range(steps)],
        "adj": arr[5 + 5 * steps],
    }


class RefLoader:
    def __init__(self, ref, steps):
        self.ref = ref
        self.steps = steps

    def __getitem__(self, key):
        r, steps = self.ref, self.steps
        if key == "mask":
            return r[0]
        if key == "flags":
            return r[1]
        if key == "beta":
            return r[2]
        if key == "slope":
            return (r[3], r[4])
        if key == "thick":
            return [r[5 + n] for n in range(steps)]
        if key == "vel":
            return [(r[5 + steps + 2 * n], r[6 + steps + 2 * n]) for n in range(steps)]
        if key == "obs":
            return [(r[5 + 3 * steps + 2 * n], r[6 + 3 * steps + 2 * n]) for n in range(steps)]
        if key == "adj":
            return r[5 + 5 * steps]
        raise KeyError(key)


def forward_kernel(steps):
    def kernel(f_ref, o_ref):
        nb = make_nb(pltpu.roll)
        out = forward_all(nb, RefLoader(f_ref, steps), steps)
        for n, (u, v) in enumerate(out):
            o_ref[2 * n] = u
            o_ref[2 * n + 1] = v

    return kernel


def backward_kernel(steps):
    def kernel(s_ref, f_ref, o_ref):
        nb = make_nb(pltpu.roll)
        loader = RefLoader(f_ref, steps)
        scales = [s_ref[n] for n in range(steps)]
        beta, g = backward_all(nb, loader, steps, scales, loader["adj"])
        o_ref[0] = beta
        o_ref[1] = g

    return kernel


def run_forward(fields, steps):
    _, r, c = fields.shape
    return pl.pallas_call(
        forward_kernel(steps),
        out_shape=jax.ShapeDtypeStruct((2 * steps, r, c), jnp.float32),
        in_specs=[pl.BlockSpec(memory_space=pltpu.VMEM)],
        out_specs=pl.BlockSpec(memory_space=pltpu.VMEM),
    )(fields)


def run_backward(scales, fields, steps):
    _, r, c = fields.shape
    return pl.pallas_call(
        backward_kernel(steps),
        out_shape=jax.ShapeDtypeStruct((2, r, c), jnp.float32),
        in_specs=[pl.BlockSpec(memory_space=pltpu.SMEM), pl.BlockSpec(memory_space=pltpu.VMEM)],
        out_specs=pl.BlockSpec(memory_space=pltpu.VMEM),
    )(scales, fields)


def on_device(
    saved_thickness,
    saved_velocity,
    surface_slope,
    basal_beta,
    cell_mask,
    upwind_flags,
    observed_velocity,
    thickness_adjoint,
):
    steps = saved_thickness.shape[0]
    rows, cols = basal_beta.shape
    f32 = jnp.float32
    obs_local = observed_velocity.astype(f32)
    grounded_local = (cell_mask == 2).astype(f32)
    scale_local = [
        jnp.sum(grounded_local * jnp.sum(obs_local[n] * obs_local[n], axis=0)) for n in range(steps)
    ]
    fields = jnp.concatenate(
        [
            jnp.stack([cell_mask.astype(f32), upwind_flags.astype(f32), basal_beta]),
            surface_slope.astype(f32),
            saved_thickness.astype(f32),
            saved_velocity.astype(f32).reshape(steps * 2, rows, cols),
            obs_local.reshape(steps * 2, rows, cols),
            thickness_adjoint[None],
        ],
        axis=0,
    )
    wide = padded_2(fields, (("gy", 1), ("gx", 2)), HALO)
    wide_cols = -(-wide.shape[2] // LANES) * LANES
    wide = jnp.pad(wide, ((0, 0), (0, 0), (0, wide_cols - wide.shape[2])))

    def centre(values):
        return values[..., HALO : HALO + rows, HALO : HALO + cols]

    velocities = run_forward(wide, steps)
    misfit_local = []
    for n in range(steps):
        difference = centre(velocities[2 * n : 2 * n + 2]) - obs_local[n]
        misfit_local.append(0.5 * jnp.sum(grounded_local * jnp.sum(difference * difference, axis=0)))
    totals = butterfly_sum(jnp.stack(scale_local + misfit_local), ("gx", "gy"))
    cell_count = rows * cols * lax.axis_size("gy") * lax.axis_size("gx")
    scales = totals[:steps] / cell_count + EPSILON
    misfit = jnp.zeros((), f32)
    for n in reversed(range(steps)):
        misfit = misfit + totals[steps + n] / cell_count / scales[n]
    grads = run_backward(scales, wide, steps)
    return (centre(grads[0]), centre(grads[1]), misfit)


def solution(mesh):
    in_specs = (
        P(None, "gy", "gx"),
        P(None, None, "gy", "gx"),
        P(None, "gy", "gx"),
        P("gy", "gx"),
        P("gy", "gx"),
        P("gy", "gx"),
        P(None, None, "gy", "gx"),
        P("gy", "gx"),
    )
    out_specs = (P("gy", "gx"), P("gy", "gx"), P())
    return jax.shard_map(
        on_device, mesh=mesh, in_specs=in_specs, out_specs=out_specs, check_vma=False
    )
```

profile of v0, /device:TPU:38, one launch (start us, length us, event | category | flops | bytes accessed | tf_op | source)
XLA Modules:
  0.0 100.8 jit_solution(4014860158874183590)
XLA Ops:
  0.6 0.9 convert_element_type.19
  1.6 0.8 bitcast_dynamic-update-slice_fusion.3
  2.4 0.8 bitcast_dynamic-update-slice_fusion.2
  3.3 0.8 bitcast_dynamic-update-slice_fusion.1
  4.1 0.8 convert_dynamic-update-slice_fusion.2
  4.9 0.9 convert_dynamic-update-slice_fusion.1
  5.8 0.9 convert_dynamic-update-slice_fusion
  6.8 0.8 bitcast_dynamic-update-slice_fusion
  7.7 3.8 %collective-permute-start = (f32[16,12,256]{2,1,0:T(8,128)S(1)}, f32[16,12,256]{2,1,0:T(8,128)S(1)}, u32[]{:S(2)}, u32[]{:S(2)}) collective-permute-start(f32[16,12,256]{2,1,0:T(8,128)S(1)} %get-tuple-element.13), channel_id=1, source_target_pairs={{0,32},{32,64},{64,96},{96,128},{128,160},{160,192},{192,224},{1,3... | collective-permute-start | bytes 589832 | tf_op jit(solution)/shard_map/ppermute | solution.py:18
  11.5 2.0 %collective-permute-start.1 = (f32[16,12,256]{2,1,0:T(8,128)S(1)}, f32[16,12,256]{2,1,0:T(8,128)S(1)}, u32[]{:S(2)}, u32[]{:S(2)}) collective-permute-start(f32[16,12,256]{2,1,0:T(8,128)S(1)} %get-tuple-element.14), channel_id=1, source_target_pairs={{32,0},{64,32},{96,64},{128,96},{160,128},{192,160},{224,192},{33,... | collective-permute-start | bytes 589832 | tf_op jit(solution)/shard_map/ppermute | solution.py:21
  13.5 4.1 %collective-permute-done = f32[16,12,256]{2,1,0:T(8,128)S(1)} collective-permute-done((f32[16,12,256]{2,1,0:T(8,128)S(1)}, f32[16,12,256]{2,1,0:T(8,128)S(1)}, u32[]{:S(2)}, u32[]{:S(2)}) %collective-permute-start) | collective-permute-done | bytes 196640 | tf_op jit(solution)/shard_map/ppermute | solution.py:18
  17.6 3.7 %collective-permute-done.1 = f32[16,12,256]{2,1,0:T(8,128)S(1)} collective-permute-done((f32[16,12,256]{2,1,0:T(8,128)S(1)}, f32[16,12,256]{2,1,0:T(8,128)S(1)}, u32[]{:S(2)}, u32[]{:S(2)}) %collective-permute-start.1) | collective-permute-done | bytes 196640 | tf_op jit(solution)/shard_map/ppermute | solution.py:21
  21.3 0.1 pad_maximum_fusion
  21.5 0.3 fusion.9
  21.7 0.3 copy.11
  22.0 1.9 %collective-permute-start.2 = (f32[16,88,12]{1,0,2:T(8,128)S(1)}, f32[16,88,12]{1,0,2:T(8,128)S(1)}, u32[]{:S(2)}, u32[]{:S(2)}) collective-permute-start(f32[16,88,12]{1,0,2:T(8,128)S(1)} %copy.11), channel_id=1, source_target_pairs={{0,1},{1,2},{2,3},{3,4},{4,5},{5,6},{6,7},{7,8},{8,9},{9,10},{10,1... | collective-permute-start | bytes 202760 | tf_op jit(solution)/shard_map/ppermute | solution.py:18
  23.9 0.3 copy.12
  24.2 3.6 %collective-permute-start.3 = (f32[16,88,12]{1,0,2:T(8,128)S(1)}, f32[16,88,12]{1,0,2:T(8,128)S(1)}, u32[]{:S(2)}, u32[]{:S(2)}) collective-permute-start(f32[16,88,12]{1,0,2:T(8,128)S(1)} %copy.12), channel_id=1, source_target_pairs={{1,0},{2,1},{3,2},{4,3},{5,4},{6,5},{7,6},{8,7},{9,8},{10,9},{11,1... | collective-permute-start | bytes 202760 | tf_op jit(solution)/shard_map/ppermute | solution.py:21
  27.8 0.1 collective-permute-done.2
  27.9 0.3 copy.13
  28.2 1.8 %collective-permute-done.3 = f32[16,88,12]{1,0,2:T(8,128)S(1)} collective-permute-done((f32[16,88,12]{1,0,2:T(8,128)S(1)}, f32[16,88,12]{1,0,2:T(8,128)S(1)}, u32[]{:S(2)}, u32[]{:S(2)}) %collective-permute-start.3) | collective-permute-done | bytes 67616 | tf_op jit(solution)/shard_map/ppermute | solution.py:21
  30.0 0.3 copy.14
  30.3 2.3 %select_maximum_fusion.f_ref = f32[16,88,384]{2,1,0:T(8,128)} fusion(f32[16,88,12]{2,1,0:T(8,128)S(1)} %copy.14, f32[16,88,12]{2,1,0:T(8,128)S(1)} %copy.13, f32[16,12,256]{2,1,0:T(8,128)S(1)} %collective-permute-done.1, f32[16,64,256]{2,1,0:T(8,128)S(1)} %bitcast_dynamic-update-slice_fusion, f32[16,12,256]{2,1,0:T(8,128)S(1)} %collective-permute-done), kind=kLoop, calls=%fused_computation | loop fusion | flops 5406720 | bytes 3739648 | tf_op jit(solution)/shard_map/concatenate | solution.py:22
  32.6 0.0 copy-start
  32.6 4.9 %shard_map.103 = f32[4,88,384]{2,1,0:T(8,128)} custom-call(f32[16,88,384]{2,1,0:T(8,128)} %select_maximum_fusion.f_ref), custom_call_target="tpu_custom_call" | custom-call | tf_op jit(solution)/shard_map/pallas_call | solution.py:246
  37.5 1.2 %fusion.8 = (f32[64,256]{1,0:T(8,128)S(1)}, f32[64,256]{1,0:T(8,128)S(1)}, f32[64,256]{1,0:T(8,128)S(1)}, f32[64,256]{1,0:T(8,128)S(1)}) fusion(f32[4,88,384]{2,1,0:T(8,128)} %shard_map.103, f32[2,2,64,256]{3,2,1,0:T(8,128)S(1)} %convert_element_type.19), kind=kLoop, calls=%fused_computation.17 | loop fusion | flops 262144 | bytes 786432 | tf_op jit(solution)/shard_map/reduce_sum | solution.py:304
  38.7 0.0 copy-done
  38.7 0.7 select_reduce_fusion.3
  40.7 1.3 %pad_maximum_fusion.1 = f32[4]{0:T(128)S(1)} fusion(f32[1]{0:T(128)} %bitcast.11, f32[1]{0:T(128)} %bitcast.10, f32[1]{0:T(128)} %bitcast.3, f32[1]{0:T(128)} %bitcast.1), kind=kLoop, calls=%fused_computation.34 | loop fusion | flops 12 | bytes 32 | tf_op jit(solution)/shard_map/stack | solution.py:305
  42.1 3.8 %collective-permute-start.4 = (f32[4]{0:T(128)S(1)}, f32[4]{0:T(128)S(1)}, u32[]{:S(2)}, u32[]{:S(2)}) collective-permute-start(f32[4]{0:T(128)S(1)} %pad_maximum_fusion.1), channel_id=1, source_target_pairs={{0,1},{1,0},{2,3},{3,2},{4,5},{5,4},{6,7},{7,6},{8,9},{9,8},{10,11... | collective-permute-start | bytes 56 | tf_op jit(solution)/shard_map/ppermute | solution.py:34
  45.9 0.8 collective-permute-done.4
  46.7 1.3 %fusion.13 = f32[4]{0:T(128)S(1)} fusion(f32[4]{0:T(128)S(1)} %collective-permute-done.4, f32[1]{0:T(128)} %bitcast.11, f32[1]{0:T(128)} %bitcast.10, f32[1]{0:T(128)} %bitcast.3, f32[1]{0:T(128)} %bitcast.1), kind=kLoop, calls=%fused_computation.40 | loop fusion | flops 16 | bytes 48 | tf_op jit(solution)/shard_map/add | solution.py:34
  48.1 0.0 collective-permute-start.5
  48.1 3.6 %collective-permute-done.5 = f32[4]{0:T(128)S(1)} collective-permute-done((f32[4]{0:T(128)S(1)}, f32[4]{0:T(128)S(1)}, u32[]{:S(2)}, u32[]{:S(2)}) %collective-permute-start.5) | collective-permute-done | bytes 48 | tf_op jit(solution)/shard_map/ppermute | solution.py:34
  51.6 1.3 %fusion.14 = f32[4]{0:T(128)S(1)} fusion(f32[4]{0:T(128)S(1)} %collective-permute-done.5, f32[4]{0:T(128)S(1)} %collective-permute-done.4, f32[1]{0:T(128)} %bitcast.11, f32[1]{0:T(128)} %bitcast.10, f32[1]{0:T(128)} %bitcast.3, f32[1]{0:T(128)} %bitcast.1), kind=kLoop, calls=%fused_computation.41 | loop fusion | flops 20 | bytes 64 | tf_op jit(solution)/shard_map/add | solution.py:34
  53.0 0.0 collective-permute-start.6
  53.0 5.1 %collective-permute-done.6 = f32[4]{0:T(128)S(1)} collective-permute-done((f32[4]{0:T(128)S(1)}, f32[4]{0:T(128)S(1)}, u32[]{:S(2)}, u32[]{:S(2)}) %collective-permute-start.6) | collective-permute-done | bytes 48 | tf_op jit(solution)/shard_map/ppermute | solution.py:34
  58.1 1.6 %collective-permute-start.7 = (f32[4]{0:T(128)S(1)}, f32[4]{0:T(128)S(1)}, u32[]{:S(2)}, u32[]{:S(2)}) collective-permute-start(f32[4]{0:T(128)S(1)} %add.37), channel_id=1, source_target_pairs={{0,8},{1,9},{2,10},{3,11},{4,12},{5,13},{6,14},{7,15},{8,0},{9,1},... | collective-permute-start | bytes 56 | tf_op jit(solution)/shard_map/ppermute | solution.py:34
  59.7 2.0 %collective-permute-done.7 = f32[4]{0:T(128)S(1)} collective-permute-done((f32[4]{0:T(128)S(1)}, f32[4]{0:T(128)S(1)}, u32[]{:S(2)}, u32[]{:S(2)}) %collective-permute-start.7) | collective-permute-done | bytes 48 | tf_op jit(solution)/shard_map/ppermute | solution.py:34
  61.7 2.9 %collective-permute-start.8 = (f32[4]{0:T(128)S(1)}, f32[4]{0:T(128)S(1)}, u32[]{:S(2)}, u32[]{:S(2)}) collective-permute-start(f32[4]{0:T(128)S(1)} %add.38), channel_id=1, source_target_pairs={{0,16},{1,17},{2,18},{3,19},{4,20},{5,21},{6,22},{7,23},{8,24},{9,... | collective-permute-start | bytes 56 | tf_op jit(solution)/shard_map/ppermute | solution.py:34
  64.6 2.2 %collective-permute-done.8 = f32[4]{0:T(128)S(1)} collective-permute-done((f32[4]{0:T(128)S(1)}, f32[4]{0:T(128)S(1)}, u32[]{:S(2)}, u32[]{:S(2)}) %collective-permute-start.8) | collective-permute-done | bytes 48 | tf_op jit(solution)/shard_map/ppermute | solution.py:34
  66.7 0.1 collective-permute-start.9
  66.9 3.5 %collective-permute-done.9 = f32[4]{0:T(128)S(1)} collective-permute-done((f32[4]{0:T(128)S(1)}, f32[4]{0:T(128)S(1)}, u32[]{:S(2)}, u32[]{:S(2)}) %collective-permute-start.9) | collective-permute-done | bytes 48 | tf_op jit(solution)/shard_map/ppermute | solution.py:34
  70.3 5.5 %collective-permute-start.10 = (f32[4]{0:T(128)S(1)}, f32[4]{0:T(128)S(1)}, u32[]{:S(2)}, u32[]{:S(2)}) collective-permute-start(f32[4]{0:T(128)S(1)} %add.40), channel_id=1, source_target_pairs={{0,64},{32,96},{64,0},{96,32},{128,192},{160,224},{192,128},{224,1... | collective-permute-start | bytes 56 | tf_op jit(solution)/shard_map/ppermute | solution.py:34
  75.8 1.5 %collective-permute-done.10 = f32[4]{0:T(128)S(1)} collective-permute-done((f32[4]{0:T(128)S(1)}, f32[4]{0:T(128)S(1)}, u32[]{:S(2)}, u32[]{:S(2)}) %collective-permute-start.10) | collective-permute-done | bytes 48 | tf_op jit(solution)/shard_map/ppermute | solution.py:34
  77.4 2.6 %collective-permute-start.11 = (f32[4]{0:T(128)S(1)}, f32[4]{0:T(128)S(1)}, u32[]{:S(2)}, u32[]{:S(2)}) collective-permute-start(f32[4]{0:T(128)S(1)} %add.41), channel_id=1, source_target_pairs={{0,128},{32,160},{64,192},{96,224},{128,0},{160,32},{192,64},{224,... | collective-permute-start | bytes 56 | tf_op jit(solution)/shard_map/ppermute | solution.py:34
  80.0 4.9 %collective-permute-done.11 = f32[4]{0:T(128)S(1)} collective-permute-done((f32[4]{0:T(128)S(1)}, f32[4]{0:T(128)S(1)}, u32[]{:S(2)}, u32[]{:S(2)}) %collective-permute-start.11) | collective-permute-done | bytes 48 | tf_op jit(solution)/shard_map/ppermute | solution.py:34
  84.9 0.5 multiply_add_fusion.s_ref
  85.4 0.0 copy-start.1
  85.4 8.0 %shard_map.104 = f32[2,88,384]{2,1,0:T(8,128)} custom-call(f32[2]{0:T(128)} %multiply_add_fusion.s_ref, f32[16,88,384]{2,1,0:T(8,128)} %select_maximum_fusion.f_ref), custom_call_target="tpu_custom_call" | custom-call | tf_op jit(solution)/shard_map/pallas_call | solution.py:256
  93.4 0.0 copy-done.1
  93.4 0.6 fusion.11
  94.0 0.6 fusion.12
  94.6 1.0 slice_bitcast_fusion
  95.6 0.7 slice.87
  97.6 0.7 slice.85
  (8 shorter events, 0.1 us)
Async XLA Ops:
  7.7 9.9 %collective-permute-start = (f32[16,12,256]{2,1,0:T(8,128)S(1)}, f32[16,12,256]{2,1,0:T(8,128)S(1)}, u32[]{:S(2)}, u32[]{:S(2)}) collective-permute-start(f32[16,12,256]{2,1,0:T(8,128)S(1)} %get-tuple-element.13), channel_id=1, source_target_pairs={{0,32},{32,64},{64,96},{96,128},{128,160},{160,192},{192,224},{1,3... | collective-permute-start | bytes 589832 | tf_op jit(solution)/shard_map/ppermute | solution.py:18
  11.5 9.8 %collective-permute-start.1 = (f32[16,12,256]{2,1,0:T(8,128)S(1)}, f32[16,12,256]{2,1,0:T(8,128)S(1)}, u32[]{:S(2)}, u32[]{:S(2)}) collective-permute-start(f32[16,12,256]{2,1,0:T(8,128)S(1)} %get-tuple-element.14), channel_id=1, source_target_pairs={{32,0},{64,32},{96,64},{128,96},{160,128},{192,160},{224,192},{33,... | collective-permute-start | bytes 589832 | tf_op jit(solution)/shard_map/ppermute | solution.py:21
  22.0 5.9 %collective-permute-start.2 = (f32[16,88,12]{1,0,2:T(8,128)S(1)}, f32[16,88,12]{1,0,2:T(8,128)S(1)}, u32[]{:S(2)}, u32[]{:S(2)}) collective-permute-start(f32[16,88,12]{1,0,2:T(8,128)S(1)} %copy.11), channel_id=1, source_target_pairs={{0,1},{1,2},{2,3},{3,4},{4,5},{5,6},{6,7},{7,8},{8,9},{9,10},{10,1... | collective-permute-start | bytes 202760 | tf_op jit(solution)/shard_map/ppermute | solution.py:18
  24.2 5.8 %collective-permute-start.3 = (f32[16,88,12]{1,0,2:T(8,128)S(1)}, f32[16,88,12]{1,0,2:T(8,128)S(1)}, u32[]{:S(2)}, u32[]{:S(2)}) collective-permute-start(f32[16,88,12]{1,0,2:T(8,128)S(1)} %copy.12), channel_id=1, source_target_pairs={{1,0},{2,1},{3,2},{4,3},{5,4},{6,5},{7,6},{8,7},{9,8},{10,9},{11,1... | collective-permute-start | bytes 202760 | tf_op jit(solution)/shard_map/ppermute | solution.py:21
  32.6 6.1 %copy-start = (s32[64,256]{1,0:T(8,128)S(1)}, s32[64,256]{1,0:T(8,128)}, u32[]{:S(2)}) copy-start(s32[64,256]{1,0:T(8,128)} %param.12) | copy-start | bytes 196612
  42.1 4.6 %collective-permute-start.4 = (f32[4]{0:T(128)S(1)}, f32[4]{0:T(128)S(1)}, u32[]{:S(2)}, u32[]{:S(2)}) collective-permute-start(f32[4]{0:T(128)S(1)} %pad_maximum_fusion.1), channel_id=1, source_target_pairs={{0,1},{1,0},{2,3},{3,2},{4,5},{5,4},{6,7},{7,6},{8,9},{9,8},{10,11... | collective-permute-start | bytes 56 | tf_op jit(solution)/shard_map/ppermute | solution.py:34
  48.1 3.6 %collective-permute-start.5 = (f32[4]{0:T(128)S(1)}, f32[4]{0:T(128)S(1)}, u32[]{:S(2)}, u32[]{:S(2)}) collective-permute-start(f32[4]{0:T(128)S(1)} %fusion.13), channel_id=1, source_target_pairs={{0,2},{1,3},{2,0},{3,1},{4,6},{5,7},{6,4},{7,5},{8,10},{9,11},{10,... | collective-permute-start | bytes 56 | tf_op jit(solution)/shard_map/ppermute | solution.py:34
  53.0 5.1 %collective-permute-start.6 = (f32[4]{0:T(128)S(1)}, f32[4]{0:T(128)S(1)}, u32[]{:S(2)}, u32[]{:S(2)}) collective-permute-start(f32[4]{0:T(128)S(1)} %fusion.14), channel_id=1, source_target_pairs={{0,4},{1,5},{2,6},{3,7},{4,0},{5,1},{6,2},{7,3},{8,12},{9,13},{10,... | collective-permute-start | bytes 56 | tf_op jit(solution)/shard_map/ppermute | solution.py:34
  58.1 3.6 %collective-permute-start.7 = (f32[4]{0:T(128)S(1)}, f32[4]{0:T(128)S(1)}, u32[]{:S(2)}, u32[]{:S(2)}) collective-permute-start(f32[4]{0:T(128)S(1)} %add.37), channel_id=1, source_target_pairs={{0,8},{1,9},{2,10},{3,11},{4,12},{5,13},{6,14},{7,15},{8,0},{9,1},... | collective-permute-start | bytes 56 | tf_op jit(solution)/shard_map/ppermute | solution.py:34
  61.7 5.1 %collective-permute-start.8 = (f32[4]{0:T(128)S(1)}, f32[4]{0:T(128)S(1)}, u32[]{:S(2)}, u32[]{:S(2)}) collective-permute-start(f32[4]{0:T(128)S(1)} %add.38), channel_id=1, source_target_pairs={{0,16},{1,17},{2,18},{3,19},{4,20},{5,21},{6,22},{7,23},{8,24},{9,... | collective-permute-start | bytes 56 | tf_op jit(solution)/shard_map/ppermute | solution.py:34
  66.7 3.6 %collective-permute-start.9 = (f32[4]{0:T(128)S(1)}, f32[4]{0:T(128)S(1)}, u32[]{:S(2)}, u32[]{:S(2)}) collective-permute-start(f32[4]{0:T(128)S(1)} %add.39), channel_id=1, source_target_pairs={{0,32},{32,0},{64,96},{96,64},{128,160},{160,128},{192,224},{224,1... | collective-permute-start | bytes 56 | tf_op jit(solution)/shard_map/ppermute | solution.py:34
  70.3 7.1 %collective-permute-start.10 = (f32[4]{0:T(128)S(1)}, f32[4]{0:T(128)S(1)}, u32[]{:S(2)}, u32[]{:S(2)}) collective-permute-start(f32[4]{0:T(128)S(1)} %add.40), channel_id=1, source_target_pairs={{0,64},{32,96},{64,0},{96,32},{128,192},{160,224},{192,128},{224,1... | collective-permute-start | bytes 56 | tf_op jit(solution)/shard_map/ppermute | solution.py:34
  77.4 7.5 %collective-permute-start.11 = (f32[4]{0:T(128)S(1)}, f32[4]{0:T(128)S(1)}, u32[]{:S(2)}, u32[]{:S(2)}) collective-permute-start(f32[4]{0:T(128)S(1)} %add.41), channel_id=1, source_target_pairs={{0,128},{32,160},{64,192},{96,224},{128,0},{160,32},{192,64},{224,... | collective-permute-start | bytes 56 | tf_op jit(solution)/shard_map/ppermute | solution.py:34
  85.4 8.1 %copy-start.1 = (f32[2]{0:T(128)S(1)}, f32[2]{0:T(128)}, u32[]{:S(2)}) copy-start(f32[2]{0:T(128)} %multiply_add_fusion.s_ref) | copy-start | bytes 28
where the time goes:
time: 102 us; the launch traced here: 101 us
  waiting for transfers between devices  33.2 us (33%)
  starting transfers between devices  28 us (27%)
  other arithmetic  14.1 us (14%)
  Pallas kernels  12.9 us (13%)
  local copies, waits for them, and re-layouts  6.69 us (7%)
  between operations  5.82 us (6%)
    ppermute x8, waiting for transfers between devices, butterfly_sum(): lax.ppermute(values, axis, [(i, i ^ stride) for i in range(count)])  23.5 us
    ppermute x8, starting transfers between devices, butterfly_sum(): lax.ppermute(values, axis, [(i, i ^ stride) for i in range(count)])  16.6 us
    pallas_call x1, Pallas kernels, run_backward(): pl.pallas_call(backward_kernel(steps), out_shape=jax.ShapeDtypeStruct((2,...  8.05 us
    ppermute x2, starting transfers between devices, padded_2(): lax.ppermute(lax.slice_in_dim(block, block.shape[dim] - width, None, axis...  5.75 us
    ppermute x2, starting transfers between devices, padded_2(): lax.ppermute(lax.slice_in_dim(block, 0, width, axis=dim), axis, backward)  5.68 us
    ppermute x2, waiting for transfers between devices, padded_2(): lax.ppermute(lax.slice_in_dim(block, 0, width, axis=dim), axis, backward)  5.54 us
    pallas_call x1, Pallas kernels, run_forward(): pl.pallas_call(forward_kernel(steps), out_shape=jax.ShapeDtypeStruct((2 *...  4.89 us
    unnamed x5, other arithmetic  4.32 us
  transfers between devices with their start and end apart: 12, of which 12 were waited for; matrix products, arithmetic and copies ran while one was open for 1% of the time, Pallas kernels for 0%

commit v1 on v0

--- a/solution.py
+++ b/solution.py
@@ -10,16 +10,22 @@
 LANES = 128
 
 
-def padded_2(block, sides, width):
-    for axis, dim in sides:
+def wrapped_patch(block, width):
+    pieces = {}
+    for axis, dim in (("gy", 1), ("gx", 2)):
         count = lax.axis_size(axis)
         forward = [(i, i + 1) for i in range(count - 1)]
         backward = [(target, source) for source, target in forward]
-        low = lax.ppermute(
+        before = lax.ppermute(
             lax.slice_in_dim(block, block.shape[dim] - width, None, axis=dim), axis, forward
         )
-        high = lax.ppermute(lax.slice_in_dim(block, 0, width, axis=dim), axis, backward)
-        block = jnp.concatenate([low, block, high], axis=dim)
+        after = lax.ppermute(lax.slice_in_dim(block, 0, width, axis=dim), axis, backward)
+        if dim == 1:
+            block = jnp.concatenate([block, after, before], axis=dim)
+        else:
+            lanes = -(-(block.shape[2] + 2 * width) // LANES) * LANES
+            gap = jnp.zeros(block.shape[:2] + (lanes - block.shape[2] - 2 * width,), block.dtype)
+            block = jnp.concatenate([block, after, gap, before], axis=dim)
     return block
 
 
@@ -218,44 +224,51 @@
         raise KeyError(key)
 
 
-def forward_kernel(steps):
+def forward_kernel(steps, rows, cols):
     def kernel(f_ref, o_ref):
         nb = make_nb(pltpu.roll)
-        out = forward_all(nb, RefLoader(f_ref, steps), steps)
+        loader = RefLoader(f_ref, steps)
+        out = forward_all(nb, loader, steps)
+        grounded = (loader["mask"][:rows, :cols] > 1.5).astype(jnp.float32)
+
+        def total(x):
+            return jnp.broadcast_to(jnp.sum(jnp.sum(x, axis=0, keepdims=True), axis=1, keepdims=True), o_ref.shape[1:])
+
         for n, (u, v) in enumerate(out):
-            o_ref[2 * n] = u
-            o_ref[2 * n + 1] = v
+            ou, ov = loader["obs"][n]
+            ou, ov = ou[:rows, :cols], ov[:rows, :cols]
+            du, dv = u[:rows, :cols] - ou, v[:rows, :cols] - ov
+            o_ref[n] = total(grounded * (ou * ou + ov * ov))
+            o_ref[steps + n] = total(0.5 * grounded * (du * du + dv * dv))
 
     return kernel
 
 
-def backward_kernel(steps):
+def backward_kernel(steps, rows, cols):
     def kernel(s_ref, f_ref, o_ref):
         nb = make_nb(pltpu.roll)
         loader = RefLoader(f_ref, steps)
         scales = [s_ref[n] for n in range(steps)]
         beta, g = backward_all(nb, loader, steps, scales, loader["adj"])
-        o_ref[0] = beta
-        o_ref[1] = g
+        o_ref[0] = beta[: o_ref.shape[1], : o_ref.shape[2]]
+        o_ref[1] = g[: o_ref.shape[1], : o_ref.shape[2]]
 
     return kernel
 
 
-def run_forward(fields, steps):
-    _, r, c = fields.shape
+def run_forward(fields, steps, rows, cols):
     return pl.pallas_call(
-        forward_kernel(steps),
-        out_shape=jax.ShapeDtypeStruct((2 * steps, r, c), jnp.float32),
+        forward_kernel(steps, rows, cols),
+        out_shape=jax.ShapeDtypeStruct((2 * steps, 8, LANES), jnp.float32),
         in_specs=[pl.BlockSpec(memory_space=pltpu.VMEM)],
         out_specs=pl.BlockSpec(memory_space=pltpu.VMEM),
     )(fields)
 
 
-def run_backward(scales, fields, steps):
-    _, r, c = fields.shape
+def run_backward(scales, fields, steps, rows, cols):
     return pl.pallas_call(
-        backward_kernel(steps),
-        out_shape=jax.ShapeDtypeStruct((2, r, c), jnp.float32),
+        backward_kernel(steps, rows, cols),
+        out_shape=jax.ShapeDtypeStruct((2, rows, cols), jnp.float32),
         in_specs=[pl.BlockSpec(memory_space=pltpu.SMEM), pl.BlockSpec(memory_space=pltpu.VMEM)],
         out_specs=pl.BlockSpec(memory_space=pltpu.VMEM),
     )(scales, fields)
@@ -274,42 +287,27 @@
     steps = saved_thickness.shape[0]
     rows, cols = basal_beta.shape
     f32 = jnp.float32
-    obs_local = observed_velocity.astype(f32)
-    grounded_local = (cell_mask == 2).astype(f32)
-    scale_local = [
-        jnp.sum(grounded_local * jnp.sum(obs_local[n] * obs_local[n], axis=0)) for n in range(steps)
-    ]
     fields = jnp.concatenate(
         [
             jnp.stack([cell_mask.astype(f32), upwind_flags.astype(f32), basal_beta]),
             surface_slope.astype(f32),
             saved_thickness.astype(f32),
             saved_velocity.astype(f32).reshape(steps * 2, rows, cols),
-            obs_local.reshape(steps * 2, rows, cols),
+            observed_velocity.astype(f32).reshape(steps * 2, rows, cols),
             thickness_adjoint[None],
         ],
         axis=0,
     )
-    wide = padded_2(fields, (("gy", 1), ("gx", 2)), HALO)
-    wide_cols = -(-wide.shape[2] // LANES) * LANES
-    wide = jnp.pad(wide, ((0, 0), (0, 0), (0, wide_cols - wide.shape[2])))
-
-    def centre(values):
-        return values[..., HALO : HALO + rows, HALO : HALO + cols]
-
-    velocities = run_forward(wide, steps)
-    misfit_local = []
-    for n in range(steps):
-        difference = centre(velocities[2 * n : 2 * n + 2]) - obs_local[n]
-        misfit_local.append(0.5 * jnp.sum(grounded_local * jnp.sum(difference * difference, axis=0)))
-    totals = butterfly_sum(jnp.stack(scale_local + misfit_local), ("gx", "gy"))
+    wide = wrapped_patch(fields, HALO)
+    local_sums = run_forward(wide, steps, rows, cols)[:, 0, 0]
+    totals = butterfly_sum(local_sums, ("gx", "gy"))
     cell_count = rows * cols * lax.axis_size("gy") * lax.axis_size("gx")
     scales = totals[:steps] / cell_count + EPSILON
     misfit = jnp.zeros((), f32)
     for n in reversed(range(steps)):
         misfit = misfit + totals[steps + n] / cell_count / scales[n]
-    grads = run_backward(scales, wide, steps)
-    return (centre(grads[0]), centre(grads[1]), misfit)
+    grads = run_backward(scales, wide, steps, rows, cols)
+    return (grads[0], grads[1], misfit)
 
 
 def solution(mesh):

time: 102 us -> 90.8 us (0.89)
  the two profiles are of different devices: /device:TPU:38 before, /device:TPU:24 now
where the time goes in v1:
time: 90.8 us; the launch traced here: 90.1 us
  waiting for transfers between devices  32.8 us (36%)
  starting transfers between devices  26.5 us (29%)
  Pallas kernels  12.1 us (13%)
  other arithmetic  7.61 us (8%)
  local copies, waits for them, and re-layouts  6.69 us (7%)
  between operations  4.4 us (5%)
    ppermute x8, waiting for transfers between devices, butterfly_sum(): lax.ppermute(values, axis, [(i, i ^ stride) for i in range(count)])  21.7 us
    ppermute x8, starting transfers between devices, butterfly_sum(): lax.ppermute(values, axis, [(i, i ^ stride) for i in range(count)])  15.4 us
    pallas_call x1, Pallas kernels, run_backward(): pl.pallas_call(backward_kernel(steps, rows, cols), out_shape=jax.ShapeDty...  7.66 us
    ppermute x2, waiting for transfers between devices, wrapped_patch(): lax.ppermute(lax.slice_in_dim(block, block.shape[dim] - width, None, axis...  6.92 us
    ppermute x2, starting transfers between devices, wrapped_patch(): lax.ppermute(lax.slice_in_dim(block, block.shape[dim] - width, None, axis...  6.49 us
    unnamed x6, other arithmetic  5.25 us
    ppermute x2, starting transfers between devices, wrapped_patch(): lax.ppermute(lax.slice_in_dim(block, 0, width, axis=dim), axis, backward)  4.63 us
    pallas_call x1, Pallas kernels, run_forward(): pl.pallas_call(forward_kernel(steps, rows, cols), out_shape=jax.ShapeDtyp...  4.4 us
  transfers between devices with their start and end apart: 12, of which 11 were waited for; matrix products, arithmetic and copies ran while one was open for 1% of the time, Pallas kernels for 0%

profile of v1, /device:TPU:24, one launch (start us, length us, event | category | flops | bytes accessed | tf_op | source)
XLA Modules:
  0.0 90.1 jit_solution(3423002116158701921)
XLA Ops:
  0.6 0.8 bitcast_dynamic-update-slice_fusion.3
  1.5 0.8 bitcast_dynamic-update-slice_fusion.2
  2.3 0.8 bitcast_dynamic-update-slice_fusion.1
  3.2 0.8 convert_dynamic-update-slice_fusion.3
  4.0 0.9 convert_dynamic-update-slice_fusion.2
  4.9 0.9 %convert_dynamic-update-slice_fusion.1 = f32[16,64,256]{2,1,0:T(8,128)S(1)} fusion(f32[16,64,256]{2,1,0:T(8,128)S(1)} %convert_dynamic-update-slice_fusion.2, bf16[4,64,256]{2,1,0:T(8,128)(2,1)} %bitcast.17), kind=kLoop, calls=%fused_computation.3 | loop fusion | flops 65536 | bytes 393216
  5.8 0.9 %convert_dynamic-update-slice_fusion = f32[16,64,256]{2,1,0:T(8,128)S(1)} fusion(f32[16,64,256]{2,1,0:T(8,128)S(1)} %convert_dynamic-update-slice_fusion.1, bf16[4,64,256]{2,1,0:T(8,128)(2,1)} %bitcast.18), kind=kLoop, calls=%fused_computation.2 | loop fusion | flops 65536 | bytes 393216
  6.7 0.8 bitcast_dynamic-update-slice_fusion
  7.6 1.3 %collective-permute-start = (f32[16,12,256]{2,1,0:T(8,128)S(1)}, f32[16,12,256]{2,1,0:T(8,128)S(1)}, u32[]{:S(2)}, u32[]{:S(2)}) collective-permute-start(f32[16,12,256]{2,1,0:T(8,128)S(1)} %get-tuple-element.5), channel_id=1, source_target_pairs={{32,0},{64,32},{96,64},{128,96},{160,128},{192,160},{224,192},{33,... | collective-permute-start | bytes 589832 | tf_op jit(solution)/shard_map/ppermute | solution.py:22
  8.9 4.6 %collective-permute-start.1 = (f32[16,12,256]{2,1,0:T(8,128)S(1)}, f32[16,12,256]{2,1,0:T(8,128)S(1)}, u32[]{:S(2)}, u32[]{:S(2)}) collective-permute-start(f32[16,12,256]{2,1,0:T(8,128)S(1)} %get-tuple-element.6), channel_id=1, source_target_pairs={{0,32},{32,64},{64,96},{96,128},{128,160},{160,192},{192,224},{1,3... | collective-permute-start | bytes 589832 | tf_op jit(solution)/shard_map/ppermute | solution.py:19
  13.5 4.3 %collective-permute-done = f32[16,12,256]{2,1,0:T(8,128)S(1)} collective-permute-done((f32[16,12,256]{2,1,0:T(8,128)S(1)}, f32[16,12,256]{2,1,0:T(8,128)S(1)}, u32[]{:S(2)}, u32[]{:S(2)}) %collective-permute-start) | collective-permute-done | bytes 196640 | tf_op jit(solution)/shard_map/ppermute | solution.py:22
  17.7 1.2 %collective-permute-done.1 = f32[16,12,256]{2,1,0:T(8,128)S(1)} collective-permute-done((f32[16,12,256]{2,1,0:T(8,128)S(1)}, f32[16,12,256]{2,1,0:T(8,128)S(1)}, u32[]{:S(2)}, u32[]{:S(2)}) %collective-permute-start.1) | collective-permute-done | bytes 196640 | tf_op jit(solution)/shard_map/ppermute | solution.py:19
  18.9 0.1 pad_maximum_fusion.1
  19.1 0.3 fusion
  19.3 0.3 copy.11
  19.6 3.3 %collective-permute-start.2 = (f32[16,88,12]{1,0,2:T(8,128)S(1)}, f32[16,88,12]{1,0,2:T(8,128)S(1)}, u32[]{:S(2)}, u32[]{:S(2)}) collective-permute-start(f32[16,88,12]{1,0,2:T(8,128)S(1)} %copy.11), channel_id=1, source_target_pairs={{1,0},{2,1},{3,2},{4,3},{5,4},{6,5},{7,6},{8,7},{9,8},{10,9},{11,1... | collective-permute-start | bytes 202760 | tf_op jit(solution)/shard_map/ppermute | solution.py:22
  22.9 0.3 copy.12
  23.2 1.9 %collective-permute-start.3 = (f32[16,88,12]{1,0,2:T(8,128)S(1)}, f32[16,88,12]{1,0,2:T(8,128)S(1)}, u32[]{:S(2)}, u32[]{:S(2)}) collective-permute-start(f32[16,88,12]{1,0,2:T(8,128)S(1)} %copy.12), channel_id=1, source_target_pairs={{0,1},{1,2},{2,3},{3,4},{4,5},{5,6},{6,7},{7,8},{8,9},{9,10},{10,1... | collective-permute-start | bytes 202760 | tf_op jit(solution)/shard_map/ppermute | solution.py:19
  25.1 0.1 pad.4.clone
  25.2 0.0 collective-permute-done.2
  25.2 0.3 copy.13
  25.5 5.7 %collective-permute-done.3 = f32[16,88,12]{1,0,2:T(8,128)S(1)} collective-permute-done((f32[16,88,12]{1,0,2:T(8,128)S(1)}, f32[16,88,12]{1,0,2:T(8,128)S(1)}, u32[]{:S(2)}, u32[]{:S(2)}) %collective-permute-start.3) | collective-permute-done | bytes 67616 | tf_op jit(solution)/shard_map/ppermute | solution.py:19
  31.2 0.3 copy.14
  31.5 1.7 %pad_maximum_fusion.f_ref = f32[16,88,384]{2,1,0:T(8,128)} fusion(f32[16,88,12]{2,1,0:T(8,128)S(1)} %copy.14, f32[16,88,12]{2,1,0:T(8,128)S(1)} %copy.13, f32[16,12,256]{2,1,0:T(8,128)S(1)} %collective-permute-done.1, f32[16,12,256]{2,1,0:T(8,128)S(1)} %collective-permute-done, f32[16,64,256]{2,1,0:T(8,128)S(1)} %bitcast_dynamic-update-slice_fusion, ...), kind=kLoop, calls=%fused_computation | loop fusion | flops 2703360 | bytes 3741184 | tf_op jit(solution)/shard_map/concatenate | solution.py:28
  33.2 4.4 %shard_map.103 = f32[4,8,128]{2,1,0:T(8,128)} custom-call(f32[16,88,384]{2,1,0:T(8,128)} %pad_maximum_fusion.f_ref), custom_call_target="tpu_custom_call" | custom-call | tf_op jit(solution)/shard_map/pallas_call | solution.py:260
  37.6 0.8 slice_reduce_fusion
  38.4 0.1 collective-permute-start.4
  38.5 1.1 %collective-permute-done.4 = f32[4]{0:T(128)S(1)} collective-permute-done((f32[4]{0:T(128)S(1)}, f32[4]{0:T(128)S(1)}, u32[]{:S(2)}, u32[]{:S(2)}) %collective-permute-start.4) | collective-permute-done | bytes 48 | tf_op jit(solution)/shard_map/ppermute | solution.py:40
  39.7 0.0 collective-permute-start.5
  39.7 3.6 %collective-permute-done.5 = f32[4]{0:T(128)S(1)} collective-permute-done((f32[4]{0:T(128)S(1)}, f32[4]{0:T(128)S(1)}, u32[]{:S(2)}, u32[]{:S(2)}) %collective-permute-start.5) | collective-permute-done | bytes 48 | tf_op jit(solution)/shard_map/ppermute | solution.py:40
  43.3 0.0 collective-permute-start.6
  43.3 5.1 %collective-permute-done.6 = f32[4]{0:T(128)S(1)} collective-permute-done((f32[4]{0:T(128)S(1)}, f32[4]{0:T(128)S(1)}, u32[]{:S(2)}, u32[]{:S(2)}) %collective-permute-start.6) | collective-permute-done | bytes 48 | tf_op jit(solution)/shard_map/ppermute | solution.py:40
  48.3 0.4 collective-permute-start.7
  48.8 3.1 %collective-permute-done.7 = f32[4]{0:T(128)S(1)} collective-permute-done((f32[4]{0:T(128)S(1)}, f32[4]{0:T(128)S(1)}, u32[]{:S(2)}, u32[]{:S(2)}) %collective-permute-start.7) | collective-permute-done | bytes 48 | tf_op jit(solution)/shard_map/ppermute | solution.py:40
  51.9 0.9 %collective-permute-start.8 = (f32[4]{0:T(128)S(1)}, f32[4]{0:T(128)S(1)}, u32[]{:S(2)}, u32[]{:S(2)}) collective-permute-start(f32[4]{0:T(128)S(1)} %add.36), channel_id=1, source_target_pairs={{0,16},{1,17},{2,18},{3,19},{4,20},{5,21},{6,22},{7,23},{8,24},{9,... | collective-permute-start | bytes 56 | tf_op jit(solution)/shard_map/ppermute | solution.py:40
  52.8 4.1 %collective-permute-done.8 = f32[4]{0:T(128)S(1)} collective-permute-done((f32[4]{0:T(128)S(1)}, f32[4]{0:T(128)S(1)}, u32[]{:S(2)}, u32[]{:S(2)}) %collective-permute-start.8) | collective-permute-done | bytes 48 | tf_op jit(solution)/shard_map/ppermute | solution.py:40
  57.0 2.5 %collective-permute-start.9 = (f32[4]{0:T(128)S(1)}, f32[4]{0:T(128)S(1)}, u32[]{:S(2)}, u32[]{:S(2)}) collective-permute-start(f32[4]{0:T(128)S(1)} %add.37), channel_id=1, source_target_pairs={{0,32},{32,0},{64,96},{96,64},{128,160},{160,128},{192,224},{224,1... | collective-permute-start | bytes 56 | tf_op jit(solution)/shard_map/ppermute | solution.py:40
  59.5 1.5 %collective-permute-done.9 = f32[4]{0:T(128)S(1)} collective-permute-done((f32[4]{0:T(128)S(1)}, f32[4]{0:T(128)S(1)}, u32[]{:S(2)}, u32[]{:S(2)}) %collective-permute-start.9) | collective-permute-done | bytes 48 | tf_op jit(solution)/shard_map/ppermute | solution.py:40
  61.0 3.9 %collective-permute-start.10 = (f32[4]{0:T(128)S(1)}, f32[4]{0:T(128)S(1)}, u32[]{:S(2)}, u32[]{:S(2)}) collective-permute-start(f32[4]{0:T(128)S(1)} %add.38), channel_id=1, source_target_pairs={{0,64},{32,96},{64,0},{96,32},{128,192},{160,224},{192,128},{224,1... | collective-permute-start | bytes 56 | tf_op jit(solution)/shard_map/ppermute | solution.py:40
  64.9 1.5 %collective-permute-done.10 = f32[4]{0:T(128)S(1)} collective-permute-done((f32[4]{0:T(128)S(1)}, f32[4]{0:T(128)S(1)}, u32[]{:S(2)}, u32[]{:S(2)}) %collective-permute-start.10) | collective-permute-done | bytes 48 | tf_op jit(solution)/shard_map/ppermute | solution.py:40
  66.5 7.5 %collective-permute-start.11 = (f32[4]{0:T(128)S(1)}, f32[4]{0:T(128)S(1)}, u32[]{:S(2)}, u32[]{:S(2)}) collective-permute-start(f32[4]{0:T(128)S(1)} %add.39), channel_id=1, source_target_pairs={{0,128},{32,160},{64,192},{96,224},{128,0},{160,32},{192,64},{224,... | collective-permute-start | bytes 56 | tf_op jit(solution)/shard_map/ppermute | solution.py:40
  74.0 1.5 %collective-permute-done.11 = f32[4]{0:T(128)S(1)} collective-permute-done((f32[4]{0:T(128)S(1)}, f32[4]{0:T(128)S(1)}, u32[]{:S(2)}, u32[]{:S(2)}) %collective-permute-start.11) | collective-permute-done | bytes 48 | tf_op jit(solution)/shard_map/ppermute | solution.py:40
  75.5 0.5 multiply_add_fusion.s_ref
  76.1 0.0 copy-start
  76.1 7.7 %shard_map.104 = f32[2,64,256]{2,1,0:T(8,128)} custom-call(f32[2]{0:T(128)} %multiply_add_fusion.s_ref, f32[16,88,384]{2,1,0:T(8,128)} %pad_maximum_fusion.f_ref), custom_call_target="tpu_custom_call" | custom-call | tf_op jit(solution)/shard_map/pallas_call | solution.py:269
  83.7 0.0 copy-done
  83.7 0.6 fusion.2
  84.3 0.6 fusion.3
  84.9 1.5 %slice_bitcast_fusion = (f32[64,256]{1,0:T(8,128)}, f32[64,256]{1,0:T(8,128)}) fusion(f32[2,64,256]{2,1,0:T(8,128)} %shard_map.104), kind=kLoop, calls=%fused_computation.6 | loop fusion | bytes 262144 | tf_op jit(solution)/shard_map/squeeze | solution.py:310
  (10 shorter events, 0.1 us)
Async XLA Ops:
  7.6 10.1 %collective-permute-start = (f32[16,12,256]{2,1,0:T(8,128)S(1)}, f32[16,12,256]{2,1,0:T(8,128)S(1)}, u32[]{:S(2)}, u32[]{:S(2)}) collective-permute-start(f32[16,12,256]{2,1,0:T(8,128)S(1)} %get-tuple-element.5), channel_id=1, source_target_pairs={{32,0},{64,32},{96,64},{128,96},{160,128},{192,160},{224,192},{33,... | collective-permute-start | bytes 589832 | tf_op jit(solution)/shard_map/ppermute | solution.py:22
  8.9 10.0 %collective-permute-start.1 = (f32[16,12,256]{2,1,0:T(8,128)S(1)}, f32[16,12,256]{2,1,0:T(8,128)S(1)}, u32[]{:S(2)}, u32[]{:S(2)}) collective-permute-start(f32[16,12,256]{2,1,0:T(8,128)S(1)} %get-tuple-element.6), channel_id=1, source_target_pairs={{0,32},{32,64},{64,96},{96,128},{128,160},{160,192},{192,224},{1,3... | collective-permute-start | bytes 589832 | tf_op jit(solution)/shard_map/ppermute | solution.py:19
  19.6 5.6 %collective-permute-start.2 = (f32[16,88,12]{1,0,2:T(8,128)S(1)}, f32[16,88,12]{1,0,2:T(8,128)S(1)}, u32[]{:S(2)}, u32[]{:S(2)}) collective-permute-start(f32[16,88,12]{1,0,2:T(8,128)S(1)} %copy.11), channel_id=1, source_target_pairs={{1,0},{2,1},{3,2},{4,3},{5,4},{6,5},{7,6},{8,7},{9,8},{10,9},{11,1... | collective-permute-start | bytes 202760 | tf_op jit(solution)/shard_map/ppermute | solution.py:22
  23.2 8.1 %collective-permute-start.3 = (f32[16,88,12]{1,0,2:T(8,128)S(1)}, f32[16,88,12]{1,0,2:T(8,128)S(1)}, u32[]{:S(2)}, u32[]{:S(2)}) collective-permute-start(f32[16,88,12]{1,0,2:T(8,128)S(1)} %copy.12), channel_id=1, source_target_pairs={{0,1},{1,2},{2,3},{3,4},{4,5},{5,6},{6,7},{7,8},{8,9},{9,10},{10,1... | collective-permute-start | bytes 202760 | tf_op jit(solution)/shard_map/ppermute | solution.py:19
  38.4 1.2 %collective-permute-start.4 = (f32[4]{0:T(128)S(1)}, f32[4]{0:T(128)S(1)}, u32[]{:S(2)}, u32[]{:S(2)}) collective-permute-start(f32[4]{0:T(128)S(1)} %slice_reduce_fusion), channel_id=1, source_target_pairs={{0,1},{1,0},{2,3},{3,2},{4,5},{5,4},{6,7},{7,6},{8,9},{9,8},{10,11... | collective-permute-start | bytes 56 | tf_op jit(solution)/shard_map/ppermute | solution.py:40
  39.7 3.6 %collective-permute-start.5 = (f32[4]{0:T(128)S(1)}, f32[4]{0:T(128)S(1)}, u32[]{:S(2)}, u32[]{:S(2)}) collective-permute-start(f32[4]{0:T(128)S(1)} %add.33), channel_id=1, source_target_pairs={{0,2},{1,3},{2,0},{3,1},{4,6},{5,7},{6,4},{7,5},{8,10},{9,11},{10,... | collective-permute-start | bytes 56 | tf_op jit(solution)/shard_map/ppermute | solution.py:40
  43.3 5.1 %collective-permute-start.6 = (f32[4]{0:T(128)S(1)}, f32[4]{0:T(128)S(1)}, u32[]{:S(2)}, u32[]{:S(2)}) collective-permute-start(f32[4]{0:T(128)S(1)} %add.34), channel_id=1, source_target_pairs={{0,4},{1,5},{2,6},{3,7},{4,0},{5,1},{6,2},{7,3},{8,12},{9,13},{10,... | collective-permute-start | bytes 56 | tf_op jit(solution)/shard_map/ppermute | solution.py:40
  48.3 3.6 %collective-permute-start.7 = (f32[4]{0:T(128)S(1)}, f32[4]{0:T(128)S(1)}, u32[]{:S(2)}, u32[]{:S(2)}) collective-permute-start(f32[4]{0:T(128)S(1)} %add.35), channel_id=1, source_target_pairs={{0,8},{1,9},{2,10},{3,11},{4,12},{5,13},{6,14},{7,15},{8,0},{9,1},... | collective-permute-start | bytes 56 | tf_op jit(solution)/shard_map/ppermute | solution.py:40
  51.9 5.1 %collective-permute-start.8 = (f32[4]{0:T(128)S(1)}, f32[4]{0:T(128)S(1)}, u32[]{:S(2)}, u32[]{:S(2)}) collective-permute-start(f32[4]{0:T(128)S(1)} %add.36), channel_id=1, source_target_pairs={{0,16},{1,17},{2,18},{3,19},{4,20},{5,21},{6,22},{7,23},{8,24},{9,... | collective-permute-start | bytes 56 | tf_op jit(solution)/shard_map/ppermute | solution.py:40
  57.0 4.0 %collective-permute-start.9 = (f32[4]{0:T(128)S(1)}, f32[4]{0:T(128)S(1)}, u32[]{:S(2)}, u32[]{:S(2)}) collective-permute-start(f32[4]{0:T(128)S(1)} %add.37), channel_id=1, source_target_pairs={{0,32},{32,0},{64,96},{96,64},{128,160},{160,128},{192,224},{224,1... | collective-permute-start | bytes 56 | tf_op jit(solution)/shard_map/ppermute | solution.py:40
  61.0 5.5 %collective-permute-start.10 = (f32[4]{0:T(128)S(1)}, f32[4]{0:T(128)S(1)}, u32[]{:S(2)}, u32[]{:S(2)}) collective-permute-start(f32[4]{0:T(128)S(1)} %add.38), channel_id=1, source_target_pairs={{0,64},{32,96},{64,0},{96,32},{128,192},{160,224},{192,128},{224,1... | collective-permute-start | bytes 56 | tf_op jit(solution)/shard_map/ppermute | solution.py:40
  66.5 9.1 %collective-permute-start.11 = (f32[4]{0:T(128)S(1)}, f32[4]{0:T(128)S(1)}, u32[]{:S(2)}, u32[]{:S(2)}) collective-permute-start(f32[4]{0:T(128)S(1)} %add.39), channel_id=1, source_target_pairs={{0,128},{32,160},{64,192},{96,224},{128,0},{160,32},{192,64},{224,... | collective-permute-start | bytes 56 | tf_op jit(solution)/shard_map/ppermute | solution.py:40
  76.1 7.7 %copy-start = (f32[2]{0:T(128)S(1)}, f32[2]{0:T(128)}, u32[]{:S(2)}) copy-start(f32[2]{0:T(128)} %multiply_add_fusion.s_ref) | copy-start | bytes 28

commit v2 on v1

--- a/solution.py
+++ b/solution.py
@@ -245,15 +245,43 @@
 
 
 def backward_kernel(steps, rows, cols):
-    def kernel(s_ref, f_ref, o_ref):
+    def kernel(s_ref, f_ref, beta_ref, g_ref):
         nb = make_nb(pltpu.roll)
         loader = RefLoader(f_ref, steps)
         scales = [s_ref[n] for n in range(steps)]
         beta, g = backward_all(nb, loader, steps, scales, loader["adj"])
-        o_ref[0] = beta[: o_ref.shape[1], : o_ref.shape[2]]
-        o_ref[1] = g[: o_ref.shape[1], : o_ref.shape[2]]
+        beta_ref[...] = beta[:rows, :cols]
+        g_ref[...] = g[:rows, :cols]
 
     return kernel
+
+
+def pack_kernel(steps):
+    def kernel(thick_ref, vel_ref, slope_ref, beta_ref, mask_ref, flags_ref, obs_ref, adj_ref, o_ref):
+        f32 = jnp.float32
+        o_ref[0] = mask_ref[...].astype(f32)
+        o_ref[1] = flags_ref[...].astype(f32)
+        o_ref[2] = beta_ref[...]
+        for c in range(2):
+            o_ref[3 + c] = slope_ref[c].astype(f32)
+        for n in range(steps):
+            o_ref[5 + n] = thick_ref[n].astype(f32)
+            for c in range(2):
+                o_ref[5 + steps + 2 * n + c] = vel_ref[n, c].astype(f32)
+                o_ref[5 + 3 * steps + 2 * n + c] = obs_ref[n, c].astype(f32)
+        o_ref[5 + 5 * steps] = adj_ref[...]
+
+    return kernel
+
+
+def run_pack(*arrays):
+    steps, rows, cols = arrays[0].shape
+    return pl.pallas_call(
+        pack_kernel(steps),
+        out_shape=jax.ShapeDtypeStruct((6 + 5 * steps, rows, cols), jnp.float32),
+        in_specs=[pl.BlockSpec(memory_space=pltpu.VMEM)] * len(arrays),
+        out_specs=pl.BlockSpec(memory_space=pltpu.VMEM),
+    )(*arrays)
 
 
 def run_forward(fields, steps, rows, cols):
@@ -268,9 +296,9 @@
 def run_backward(scales, fields, steps, rows, cols):
     return pl.pallas_call(
         backward_kernel(steps, rows, cols),
-        out_shape=jax.ShapeDtypeStruct((2, rows, cols), jnp.float32),
+        out_shape=(jax.ShapeDtypeStruct((rows, cols), jnp.float32),) * 2,
         in_specs=[pl.BlockSpec(memory_space=pltpu.SMEM), pl.BlockSpec(memory_space=pltpu.VMEM)],
-        out_specs=pl.BlockSpec(memory_space=pltpu.VMEM),
+        out_specs=(pl.BlockSpec(memory_space=pltpu.VMEM),) * 2,
     )(scales, fields)
 
 
@@ -287,16 +315,15 @@
     steps = saved_thickness.shape[0]
     rows, cols = basal_beta.shape
     f32 = jnp.float32
-    fields = jnp.concatenate(
-        [
-            jnp.stack([cell_mask.astype(f32), upwind_flags.astype(f32), basal_beta]),
-            surface_slope.astype(f32),
-            saved_thickness.astype(f32),
-            saved_velocity.astype(f32).reshape(steps * 2, rows, cols),
-            observed_velocity.astype(f32).reshape(steps * 2, rows, cols),
-            thickness_adjoint[None],
-        ],
-        axis=0,
+    fields = run_pack(
+        saved_thickness,
+        saved_velocity,
+        surface_slope,
+        basal_beta,
+        cell_mask,
+        upwind_flags,
+        observed_velocity,
+        thickness_adjoint,
     )
     wide = wrapped_patch(fields, HALO)
     local_sums = run_forward(wide, steps, rows, cols)[:, 0, 0]

time: 90.8 us -> 86.7 us (0.955)
  other arithmetic: 7.61 us -> 3.58 us
  local copies, waits for them, and re-layouts: 6.69 us -> 4.53 us
  Pallas kernels: 12.1 us -> 14.2 us
    unnamed x6 -> x0, other arithmetic: 5.25 us -> none
    pallas_call x1 -> x2, Pallas kernels: 7.66 us -> 9.82 us  [the longest x1 7.65 us: run_backward(): pl.pallas_call(backward_kernel(steps, rows, cols), out_shape=(jax.ShapeDt...]
    squeeze x1 -> x0, local copies, waits for them, and re-layouts: 1.53 us -> none  [on_device(): return (grads[0], grads[1], misfit)]
    concatenate x1, other arithmetic: 0.13 us -> 1.36 us  [wrapped_patch(): block = jnp.concatenate([block, after, before], axis=dim)]
    slice x3, local copies, waits for them, and re-layouts: 0.54 us -> 1.57 us  [wrapped_patch(): lax.slice_in_dim(block, 0, width, axis=dim)]
where the time goes in v2:
time: 86.7 us; the launch traced here: 86.3 us
  waiting for transfers between devices  32.8 us (38%)
  starting transfers between devices  26.6 us (31%)
  Pallas kernels  14.2 us (16%)
  local copies, waits for them, and re-layouts  4.53 us (5%)
  between operations  4.47 us (5%)
  other arithmetic  3.58 us (4%)
    ppermute x8, waiting for transfers between devices, butterfly_sum(): lax.ppermute(values, axis, [(i, i ^ stride) for i in range(count)])  21.7 us
    ppermute x8, starting transfers between devices, butterfly_sum(): lax.ppermute(values, axis, [(i, i ^ stride) for i in range(count)])  15.4 us
    pallas_call x1, Pallas kernels, run_backward(): pl.pallas_call(backward_kernel(steps, rows, cols), out_shape=(jax.ShapeDt...  7.65 us
    ppermute x2, waiting for transfers between devices, wrapped_patch(): lax.ppermute(lax.slice_in_dim(block, block.shape[dim] - width, None, axis...  6.92 us
    ppermute x2, starting transfers between devices, wrapped_patch(): lax.ppermute(lax.slice_in_dim(block, block.shape[dim] - width, None, axis...  6.49 us
    ppermute x2, starting transfers between devices, wrapped_patch(): lax.ppermute(lax.slice_in_dim(block, 0, width, axis=dim), axis, backward)  4.76 us
    pallas_call x1, Pallas kernels, run_forward(): pl.pallas_call(forward_kernel(steps, rows, cols), out_shape=jax.ShapeDtyp...  4.4 us
    ppermute x2, waiting for transfers between devices, wrapped_patch(): lax.ppermute(lax.slice_in_dim(block, 0, width, axis=dim), axis, backward)  4.26 us
  transfers between devices with their start and end apart: 12, of which 11 were waited for; matrix products, arithmetic and copies ran while one was open for 1% of the time, Pallas kernels for 0%

profile of v2, /device:TPU:24, one launch (start us, length us, event | category | flops | bytes accessed | tf_op | source)
XLA Modules:
  0.0 86.3 jit_solution(5900091729068597578)
XLA Ops:
  0.6 2.2 %shard_map.103 = f32[16,64,256]{2,1,0:T(8,128)} custom-call(bf16[2,64,256]{2,1,0:T(8,128)(2,1)} %thick_ref.1, bf16[2,2,64,256]{3,2,1,0:T(8,128)(2,1)} %vel_ref.1, bf16[2,64,256]{2,1,0:T(8,128)(2,1)} %slope_ref.1, f32[64,256]{1,0:T(8,128)} %beta_ref.1, s32[64,256]{1,0:T(8,128)} %mask_ref.1, s32[64,256]{1,0:T(8,128)} %flags_ref.1, ...), custom_call_target="tpu_custom_call" | custom-call | tf_op jit(solution)/shard_map/pallas_call | solution.py:279
  2.8 1.1 %fusion.1 = (f32[16,12,256]{2,1,0:T(8,128)S(1)}, f32[16,12,256]{2,1,0:T(8,128)S(1)}) fusion(f32[16,64,256]{2,1,0:T(8,128)} %shard_map.103), kind=kLoop, calls=%fused_computation.5 | loop fusion | bytes 786432 | tf_op jit(solution)/shard_map/slice | solution.py:22
  3.9 1.3 %collective-permute-start = (f32[16,12,256]{2,1,0:T(8,128)S(1)}, f32[16,12,256]{2,1,0:T(8,128)S(1)}, u32[]{:S(2)}, u32[]{:S(2)}) collective-permute-start(f32[16,12,256]{2,1,0:T(8,128)S(1)} %get-tuple-element.9), channel_id=1, source_target_pairs={{32,0},{64,32},{96,64},{128,96},{160,128},{192,160},{224,192},{33,... | collective-permute-start | bytes 589832 | tf_op jit(solution)/shard_map/ppermute | solution.py:22
  5.2 4.6 %collective-permute-start.1 = (f32[16,12,256]{2,1,0:T(8,128)S(1)}, f32[16,12,256]{2,1,0:T(8,128)S(1)}, u32[]{:S(2)}, u32[]{:S(2)}) collective-permute-start(f32[16,12,256]{2,1,0:T(8,128)S(1)} %get-tuple-element.10), channel_id=1, source_target_pairs={{0,32},{32,64},{64,96},{96,128},{128,160},{160,192},{192,224},{1,3... | collective-permute-start | bytes 589832 | tf_op jit(solution)/shard_map/ppermute | solution.py:19
  9.8 4.3 %collective-permute-done = f32[16,12,256]{2,1,0:T(8,128)S(1)} collective-permute-done((f32[16,12,256]{2,1,0:T(8,128)S(1)}, f32[16,12,256]{2,1,0:T(8,128)S(1)}, u32[]{:S(2)}, u32[]{:S(2)}) %collective-permute-start) | collective-permute-done | bytes 196640 | tf_op jit(solution)/shard_map/ppermute | solution.py:22
  14.0 1.2 %collective-permute-done.1 = f32[16,12,256]{2,1,0:T(8,128)S(1)} collective-permute-done((f32[16,12,256]{2,1,0:T(8,128)S(1)}, f32[16,12,256]{2,1,0:T(8,128)S(1)}, u32[]{:S(2)}, u32[]{:S(2)}) %collective-permute-start.1) | collective-permute-done | bytes 196640 | tf_op jit(solution)/shard_map/ppermute | solution.py:19
  15.2 1.4 %pad_maximum_fusion.1 = f32[16,88,256]{2,1,0:T(8,128)S(1)} fusion(f32[16,12,256]{2,1,0:T(8,128)S(1)} %collective-permute-done.1, f32[16,12,256]{2,1,0:T(8,128)S(1)} %collective-permute-done, f32[16,64,256]{2,1,0:T(8,128)} %shard_map.103), kind=kLoop, calls=%fused_computation.1 | loop fusion | flops 720896 | bytes 2883584 | tf_op jit(solution)/shard_map/concatenate | solution.py:24
  16.6 0.3 fusion
  16.8 0.0 copy-start
  16.8 0.3 copy.11
  17.1 3.5 %collective-permute-start.2 = (f32[16,88,12]{1,0,2:T(8,128)S(1)}, f32[16,88,12]{1,0,2:T(8,128)S(1)}, u32[]{:S(2)}, u32[]{:S(2)}) collective-permute-start(f32[16,88,12]{1,0,2:T(8,128)S(1)} %copy.11), channel_id=1, source_target_pairs={{1,0},{2,1},{3,2},{4,3},{5,4},{6,5},{7,6},{8,7},{9,8},{10,9},{11,1... | collective-permute-start | bytes 202760 | tf_op jit(solution)/shard_map/ppermute | solution.py:22
  20.5 0.3 copy.12
  20.8 1.9 %collective-permute-start.3 = (f32[16,88,12]{1,0,2:T(8,128)S(1)}, f32[16,88,12]{1,0,2:T(8,128)S(1)}, u32[]{:S(2)}, u32[]{:S(2)}) collective-permute-start(f32[16,88,12]{1,0,2:T(8,128)S(1)} %copy.12), channel_id=1, source_target_pairs={{0,1},{1,2},{2,3},{3,4},{4,5},{5,6},{6,7},{7,8},{8,9},{9,10},{10,1... | collective-permute-start | bytes 202760 | tf_op jit(solution)/shard_map/ppermute | solution.py:19
  22.7 0.1 pad.4.clone
  22.8 0.0 collective-permute-done.2
  22.8 0.3 copy.13
  23.1 5.7 %collective-permute-done.3 = f32[16,88,12]{1,0,2:T(8,128)S(1)} collective-permute-done((f32[16,88,12]{1,0,2:T(8,128)S(1)}, f32[16,88,12]{1,0,2:T(8,128)S(1)}, u32[]{:S(2)}, u32[]{:S(2)}) %collective-permute-start.3) | collective-permute-done | bytes 67616 | tf_op jit(solution)/shard_map/ppermute | solution.py:19
  28.9 0.3 copy.14
  29.1 0.0 copy-done
  29.2 1.7 %pad_maximum_fusion.f_ref = f32[16,88,384]{2,1,0:T(8,128)} fusion(f32[16,88,12]{2,1,0:T(8,128)S(1)} %copy.14, f32[16,88,12]{2,1,0:T(8,128)S(1)} %copy.13, f32[16,12,256]{2,1,0:T(8,128)S(1)} %collective-permute-done.1, f32[16,12,256]{2,1,0:T(8,128)S(1)} %collective-permute-done, f32[16,64,256]{2,1,0:T(8,128)S(1)} %copy-done, f32[384]{0:T(512)S(1)} %pad.4.clone), kind=kLoop, calls=%fused_computation | loop fusion | flops 2703360 | bytes 3741184 | tf_op jit(solution)/shard_map/concatenate | solution.py:28
  30.8 4.4 %shard_map.104 = f32[4,8,128]{2,1,0:T(8,128)} custom-call(f32[16,88,384]{2,1,0:T(8,128)} %pad_maximum_fusion.f_ref), custom_call_target="tpu_custom_call" | custom-call | tf_op jit(solution)/shard_map/pallas_call | solution.py:288
  35.2 0.8 slice_reduce_fusion
  36.1 0.1 collective-permute-start.4
  36.1 1.1 %collective-permute-done.4 = f32[4]{0:T(128)S(1)} collective-permute-done((f32[4]{0:T(128)S(1)}, f32[4]{0:T(128)S(1)}, u32[]{:S(2)}, u32[]{:S(2)}) %collective-permute-start.4) | collective-permute-done | bytes 48 | tf_op jit(solution)/shard_map/ppermute | solution.py:40
  37.3 0.0 collective-permute-start.5
  37.3 3.6 %collective-permute-done.5 = f32[4]{0:T(128)S(1)} collective-permute-done((f32[4]{0:T(128)S(1)}, f32[4]{0:T(128)S(1)}, u32[]{:S(2)}, u32[]{:S(2)}) %collective-permute-start.5) | collective-permute-done | bytes 48 | tf_op jit(solution)/shard_map/ppermute | solution.py:40
  40.9 0.0 collective-permute-start.6
  40.9 5.1 %collective-permute-done.6 = f32[4]{0:T(128)S(1)} collective-permute-done((f32[4]{0:T(128)S(1)}, f32[4]{0:T(128)S(1)}, u32[]{:S(2)}, u32[]{:S(2)}) %collective-permute-start.6) | collective-permute-done | bytes 48 | tf_op jit(solution)/shard_map/ppermute | solution.py:40
  46.0 0.4 collective-permute-start.7
  46.4 3.1 %collective-permute-done.7 = f32[4]{0:T(128)S(1)} collective-permute-done((f32[4]{0:T(128)S(1)}, f32[4]{0:T(128)S(1)}, u32[]{:S(2)}, u32[]{:S(2)}) %collective-permute-start.7) | collective-permute-done | bytes 48 | tf_op jit(solution)/shard_map/ppermute | solution.py:40
  49.5 0.9 %collective-permute-start.8 = (f32[4]{0:T(128)S(1)}, f32[4]{0:T(128)S(1)}, u32[]{:S(2)}, u32[]{:S(2)}) collective-permute-start(f32[4]{0:T(128)S(1)} %add.36), channel_id=1, source_target_pairs={{0,16},{1,17},{2,18},{3,19},{4,20},{5,21},{6,22},{7,23},{8,24},{9,... | collective-permute-start | bytes 56 | tf_op jit(solution)/shard_map/ppermute | solution.py:40
  50.5 4.1 %collective-permute-done.8 = f32[4]{0:T(128)S(1)} collective-permute-done((f32[4]{0:T(128)S(1)}, f32[4]{0:T(128)S(1)}, u32[]{:S(2)}, u32[]{:S(2)}) %collective-permute-start.8) | collective-permute-done | bytes 48 | tf_op jit(solution)/shard_map/ppermute | solution.py:40
  54.6 2.5 %collective-permute-start.9 = (f32[4]{0:T(128)S(1)}, f32[4]{0:T(128)S(1)}, u32[]{:S(2)}, u32[]{:S(2)}) collective-permute-start(f32[4]{0:T(128)S(1)} %add.37), channel_id=1, source_target_pairs={{0,32},{32,0},{64,96},{96,64},{128,160},{160,128},{192,224},{224,1... | collective-permute-start | bytes 56 | tf_op jit(solution)/shard_map/ppermute | solution.py:40
  57.1 1.5 %collective-permute-done.9 = f32[4]{0:T(128)S(1)} collective-permute-done((f32[4]{0:T(128)S(1)}, f32[4]{0:T(128)S(1)}, u32[]{:S(2)}, u32[]{:S(2)}) %collective-permute-start.9) | collective-permute-done | bytes 48 | tf_op jit(solution)/shard_map/ppermute | solution.py:40
  58.6 3.9 %collective-permute-start.10 = (f32[4]{0:T(128)S(1)}, f32[4]{0:T(128)S(1)}, u32[]{:S(2)}, u32[]{:S(2)}) collective-permute-start(f32[4]{0:T(128)S(1)} %add.38), channel_id=1, source_target_pairs={{0,64},{32,96},{64,0},{96,32},{128,192},{160,224},{192,128},{224,1... | collective-permute-start | bytes 56 | tf_op jit(solution)/shard_map/ppermute | solution.py:40
  62.6 1.5 %collective-permute-done.10 = f32[4]{0:T(128)S(1)} collective-permute-done((f32[4]{0:T(128)S(1)}, f32[4]{0:T(128)S(1)}, u32[]{:S(2)}, u32[]{:S(2)}) %collective-permute-start.10) | collective-permute-done | bytes 48 | tf_op jit(solution)/shard_map/ppermute | solution.py:40
  64.1 7.5 %collective-permute-start.11 = (f32[4]{0:T(128)S(1)}, f32[4]{0:T(128)S(1)}, u32[]{:S(2)}, u32[]{:S(2)}) collective-permute-start(f32[4]{0:T(128)S(1)} %add.39), channel_id=1, source_target_pairs={{0,128},{32,160},{64,192},{96,224},{128,0},{160,32},{192,64},{224,... | collective-permute-start | bytes 56 | tf_op jit(solution)/shard_map/ppermute | solution.py:40
  71.6 1.5 %collective-permute-done.11 = f32[4]{0:T(128)S(1)} collective-permute-done((f32[4]{0:T(128)S(1)}, f32[4]{0:T(128)S(1)}, u32[]{:S(2)}, u32[]{:S(2)}) %collective-permute-start.11) | collective-permute-done | bytes 48 | tf_op jit(solution)/shard_map/ppermute | solution.py:40
  73.2 0.5 multiply_add_fusion.s_ref
  73.7 0.0 copy-start.1
  73.7 7.6 %shard_map.105 = (f32[64,256]{1,0:T(8,128)}, f32[64,256]{1,0:T(8,128)}) custom-call(f32[2]{0:T(128)} %multiply_add_fusion.s_ref, f32[16,88,384]{2,1,0:T(8,128)} %pad_maximum_fusion.f_ref), custom_call_target="tpu_custom_call" | custom-call | tf_op jit(solution)/shard_map/pallas_call | solution.py:297
  81.3 0.0 copy-done.1
  81.3 0.6 fusion.2
  81.9 0.7 fusion.3
  (9 shorter events, 0.0 us)
Async XLA Ops:
  3.9 10.1 %collective-permute-start = (f32[16,12,256]{2,1,0:T(8,128)S(1)}, f32[16,12,256]{2,1,0:T(8,128)S(1)}, u32[]{:S(2)}, u32[]{:S(2)}) collective-permute-start(f32[16,12,256]{2,1,0:T(8,128)S(1)} %get-tuple-element.9), channel_id=1, source_target_pairs={{32,0},{64,32},{96,64},{128,96},{160,128},{192,160},{224,192},{33,... | collective-permute-start | bytes 589832 | tf_op jit(solution)/shard_map/ppermute | solution.py:22
  5.2 10.0 %collective-permute-start.1 = (f32[16,12,256]{2,1,0:T(8,128)S(1)}, f32[16,12,256]{2,1,0:T(8,128)S(1)}, u32[]{:S(2)}, u32[]{:S(2)}) collective-permute-start(f32[16,12,256]{2,1,0:T(8,128)S(1)} %get-tuple-element.10), channel_id=1, source_target_pairs={{0,32},{32,64},{64,96},{96,128},{128,160},{160,192},{192,224},{1,3... | collective-permute-start | bytes 589832 | tf_op jit(solution)/shard_map/ppermute | solution.py:19
  16.8 12.3 %copy-start = (f32[16,64,256]{2,1,0:T(8,128)S(1)}, f32[16,64,256]{2,1,0:T(8,128)}, u32[]{:S(2)}) copy-start(f32[16,64,256]{2,1,0:T(8,128)} %shard_map.103) | copy-start | bytes 3145732
  17.1 5.8 %collective-permute-start.2 = (f32[16,88,12]{1,0,2:T(8,128)S(1)}, f32[16,88,12]{1,0,2:T(8,128)S(1)}, u32[]{:S(2)}, u32[]{:S(2)}) collective-permute-start(f32[16,88,12]{1,0,2:T(8,128)S(1)} %copy.11), channel_id=1, source_target_pairs={{1,0},{2,1},{3,2},{4,3},{5,4},{6,5},{7,6},{8,7},{9,8},{10,9},{11,1... | collective-permute-start | bytes 202760 | tf_op jit(solution)/shard_map/ppermute | solution.py:22
  20.8 8.1 %collective-permute-start.3 = (f32[16,88,12]{1,0,2:T(8,128)S(1)}, f32[16,88,12]{1,0,2:T(8,128)S(1)}, u32[]{:S(2)}, u32[]{:S(2)}) collective-permute-start(f32[16,88,12]{1,0,2:T(8,128)S(1)} %copy.12), channel_id=1, source_target_pairs={{0,1},{1,2},{2,3},{3,4},{4,5},{5,6},{6,7},{7,8},{8,9},{9,10},{10,1... | collective-permute-start | bytes 202760 | tf_op jit(solution)/shard_map/ppermute | solution.py:19
  36.1 1.2 %collective-permute-start.4 = (f32[4]{0:T(128)S(1)}, f32[4]{0:T(128)S(1)}, u32[]{:S(2)}, u32[]{:S(2)}) collective-permute-start(f32[4]{0:T(128)S(1)} %slice_reduce_fusion), channel_id=1, source_target_pairs={{0,1},{1,0},{2,3},{3,2},{4,5},{5,4},{6,7},{7,6},{8,9},{9,8},{10,11... | collective-permute-start | bytes 56 | tf_op jit(solution)/shard_map/ppermute | solution.py:40
  37.3 3.6 %collective-permute-start.5 = (f32[4]{0:T(128)S(1)}, f32[4]{0:T(128)S(1)}, u32[]{:S(2)}, u32[]{:S(2)}) collective-permute-start(f32[4]{0:T(128)S(1)} %add.33), channel_id=1, source_target_pairs={{0,2},{1,3},{2,0},{3,1},{4,6},{5,7},{6,4},{7,5},{8,10},{9,11},{10,... | collective-permute-start | bytes 56 | tf_op jit(solution)/shard_map/ppermute | solution.py:40
  40.9 5.1 %collective-permute-start.6 = (f32[4]{0:T(128)S(1)}, f32[4]{0:T(128)S(1)}, u32[]{:S(2)}, u32[]{:S(2)}) collective-permute-start(f32[4]{0:T(128)S(1)} %add.34), channel_id=1, source_target_pairs={{0,4},{1,5},{2,6},{3,7},{4,0},{5,1},{6,2},{7,3},{8,12},{9,13},{10,... | collective-permute-start | bytes 56 | tf_op jit(solution)/shard_map/ppermute | solution.py:40
  46.0 3.6 %collective-permute-start.7 = (f32[4]{0:T(128)S(1)}, f32[4]{0:T(128)S(1)}, u32[]{:S(2)}, u32[]{:S(2)}) collective-permute-start(f32[4]{0:T(128)S(1)} %add.35), channel_id=1, source_target_pairs={{0,8},{1,9},{2,10},{3,11},{4,12},{5,13},{6,14},{7,15},{8,0},{9,1},... | collective-permute-start | bytes 56 | tf_op jit(solution)/shard_map/ppermute | solution.py:40
  49.5 5.1 %collective-permute-start.8 = (f32[4]{0:T(128)S(1)}, f32[4]{0:T(128)S(1)}, u32[]{:S(2)}, u32[]{:S(2)}) collective-permute-start(f32[4]{0:T(128)S(1)} %add.36), channel_id=1, source_target_pairs={{0,16},{1,17},{2,18},{3,19},{4,20},{5,21},{6,22},{7,23},{8,24},{9,... | collective-permute-start | bytes 56 | tf_op jit(solution)/shard_map/ppermute | solution.py:40
  54.6 4.0 %collective-permute-start.9 = (f32[4]{0:T(128)S(1)}, f32[4]{0:T(128)S(1)}, u32[]{:S(2)}, u32[]{:S(2)}) collective-permute-start(f32[4]{0:T(128)S(1)} %add.37), channel_id=1, source_target_pairs={{0,32},{32,0},{64,96},{96,64},{128,160},{160,128},{192,224},{224,1... | collective-permute-start | bytes 56 | tf_op jit(solution)/shard_map/ppermute | solution.py:40
  58.6 5.5 %collective-permute-start.10 = (f32[4]{0:T(128)S(1)}, f32[4]{0:T(128)S(1)}, u32[]{:S(2)}, u32[]{:S(2)}) collective-permute-start(f32[4]{0:T(128)S(1)} %add.38), channel_id=1, source_target_pairs={{0,64},{32,96},{64,0},{96,32},{128,192},{160,224},{192,128},{224,1... | collective-permute-start | bytes 56 | tf_op jit(solution)/shard_map/ppermute | solution.py:40
  64.1 9.1 %collective-permute-start.11 = (f32[4]{0:T(128)S(1)}, f32[4]{0:T(128)S(1)}, u32[]{:S(2)}, u32[]{:S(2)}) collective-permute-start(f32[4]{0:T(128)S(1)} %add.39), channel_id=1, source_target_pairs={{0,128},{32,160},{64,192},{96,224},{128,0},{160,32},{192,64},{224,... | collective-permute-start | bytes 56 | tf_op jit(solution)/shard_map/ppermute | solution.py:40
  73.7 7.7 %copy-start.1 = (f32[2]{0:T(128)S(1)}, f32[2]{0:T(128)}, u32[]{:S(2)}) copy-start(f32[2]{0:T(128)} %multiply_add_fusion.s_ref) | copy-start | bytes 28

commit v3 on v2

--- a/solution.py
+++ b/solution.py
@@ -11,22 +11,40 @@
 
 
 def wrapped_patch(block, width):
-    pieces = {}
-    for axis, dim in (("gy", 1), ("gx", 2)):
-        count = lax.axis_size(axis)
-        forward = [(i, i + 1) for i in range(count - 1)]
-        backward = [(target, source) for source, target in forward]
-        before = lax.ppermute(
-            lax.slice_in_dim(block, block.shape[dim] - width, None, axis=dim), axis, forward
-        )
-        after = lax.ppermute(lax.slice_in_dim(block, 0, width, axis=dim), axis, backward)
-        if dim == 1:
-            block = jnp.concatenate([block, after, before], axis=dim)
-        else:
-            lanes = -(-(block.shape[2] + 2 * width) // LANES) * LANES
-            gap = jnp.zeros(block.shape[:2] + (lanes - block.shape[2] - 2 * width,), block.dtype)
-            block = jnp.concatenate([block, after, gap, before], axis=dim)
-    return block
+    ny, nx = lax.axis_size("gy"), lax.axis_size("gx")
+    rows, cols = block.shape[1], block.shape[2]
+    first, last = slice(0, width), slice(rows - width, rows)
+    first_c, last_c = slice(0, width), slice(cols - width, cols)
+    whole_r, whole_c = slice(0, rows), slice(0, cols)
+
+    def take(dy, dx, row_part, col_part):
+        pairs = []
+        for iy in range(ny):
+            for ix in range(nx):
+                ty, tx = iy + dy, ix + dx
+                if 0 <= ty < ny and 0 <= tx < nx:
+                    pairs.append((iy * nx + ix, ty * nx + tx))
+        return lax.ppermute(block[:, row_part, col_part], ("gy", "gx"), pairs)
+
+    north = take(1, 0, last, whole_c)
+    south = take(-1, 0, first, whole_c)
+    west = take(0, 1, whole_r, last_c)
+    east = take(0, -1, whole_r, first_c)
+    north_west = take(1, 1, last, last_c)
+    north_east = take(1, -1, last, first_c)
+    south_west = take(-1, 1, first, last_c)
+    south_east = take(-1, -1, first, first_c)
+    lanes = -(-(cols + 2 * width) // LANES) * LANES
+    gap_width = lanes - cols - 2 * width
+
+    def band(main, after, before):
+        gap = jnp.zeros(main.shape[:2] + (gap_width,), main.dtype)
+        return jnp.concatenate([main, after, gap, before], axis=2)
+
+    return jnp.concatenate(
+        [band(block, east, west), band(south, south_east, south_west), band(north, north_east, north_west)],
+        axis=1,
+    )
 
 
 def butterfly_sum(values, axes):

time: 86.7 us -> 113 us (1.30)
  starting transfers between devices: 26.6 us -> 44.6 us
  waiting for transfers between devices: 32.8 us -> 41.3 us
    ppermute x4 -> x8, starting transfers between devices: 11.3 us -> 27.4 us  [take(): return lax.ppermute(block[:, row_part, col_part], ('gy', 'gx'), pairs)]
    ppermute x4 -> x8, waiting for transfers between devices: 11.2 us -> 18.8 us  [take(): return lax.ppermute(block[:, row_part, col_part], ('gy', 'gx'), pairs)]
    ppermute x8, starting transfers between devices: 15.4 us -> 17.1 us  [butterfly_sum(): lax.ppermute(values, axis, [(i, i ^ stride) for i in range(count)])]
    slice x4 -> x3, local copies, waits for them, and re-layouts: 1.83 us -> 2.7 us  [take(): return lax.ppermute(block[:, row_part, col_part], ('gy', 'gx'), pairs)]
    concatenate x2 -> x1, other arithmetic: 3.04 us -> 2.55 us  [wrapped_patch(): jnp.concatenate([band(block, east, west), band(south, south_east, south_w...]
  transfers between devices with their start and end apart: 12 -> 16, of which waited for: 11 -> 12; matrix products, arithmetic and copies ran while one was open for 1% -> 1% of each run, Pallas kernels for 0% -> 0%
where the time goes in v3:
time: 113 us
  starting transfers between devices  44.6 us (39%)
  waiting for transfers between devices  41.3 us (37%)
  Pallas kernels  14.2 us (13%)
  local copies, waits for them, and re-layouts  4.89 us (4%)
  between operations  4.5 us (4%)
  other arithmetic  3.1 us (3%)
    ppermute x8, starting transfers between devices, take(): return lax.ppermute(block[:, row_part, col_part], ('gy', 'gx'), pairs)  27.4 us
    ppermute x8, waiting for transfers between devices, butterfly_sum(): lax.ppermute(values, axis, [(i, i ^ stride) for i in range(count)])  22.5 us
    ppermute x8, waiting for transfers between devices, take(): return lax.ppermute(block[:, row_part, col_part], ('gy', 'gx'), pairs)  18.8 us
    ppermute x8, starting transfers between devices, butterfly_sum(): lax.ppermute(values, axis, [(i, i ^ stride) for i in range(count)])  17.1 us
    pallas_call x1, Pallas kernels, run_backward(): pl.pallas_call(backward_kernel(steps, rows, cols), out_shape=(jax.ShapeDt...  7.65 us
    pallas_call x1, Pallas kernels, run_forward(): pl.pallas_call(forward_kernel(steps, rows, cols), out_shape=jax.ShapeDtyp...  4.4 us
    slice x3, local copies, waits for them, and re-layouts, take(): return lax.ppermute(block[:, row_part, col_part], ('gy', 'gx'), pairs)  2.7 us
    concatenate x1, other arithmetic, wrapped_patch(): jnp.concatenate([band(block, east, west), band(south, south_east, south_w...  2.55 us
  transfers between devices with their start and end apart: 16, of which 12 were waited for; matrix products, arithmetic and copies ran while one was open for 1% of the time, Pallas kernels for 0%

profile of v3, /device:TPU:24, one launch (start us, length us, event | category | flops | bytes accessed | tf_op | source)
XLA Modules:
  0.0 112.6 jit_solution(16080789443785919617)
XLA Ops:
  0.6 2.2 %shard_map.103 = f32[16,64,256]{2,1,0:T(8,128)} custom-call(bf16[2,64,256]{2,1,0:T(8,128)(2,1)} %thick_ref.1, bf16[2,2,64,256]{3,2,1,0:T(8,128)(2,1)} %vel_ref.1, bf16[2,64,256]{2,1,0:T(8,128)(2,1)} %slope_ref.1, f32[64,256]{1,0:T(8,128)} %beta_ref.1, s32[64,256]{1,0:T(8,128)} %mask_ref.1, s32[64,256]{1,0:T(8,128)} %flags_ref.1, ...), custom_call_target="tpu_custom_call" | custom-call | tf_op jit(solution)/shard_map/pallas_call | solution.py:297
  2.8 0.0 copy-start
  2.8 1.2 %fusion.1 = (f32[16,12,256]{2,1,0:T(8,128)S(1)}, f32[16,12,256]{2,1,0:T(8,128)S(1)}) fusion(f32[16,64,256]{2,1,0:T(8,128)} %shard_map.103), kind=kLoop, calls=%fused_computation.4 | loop fusion | bytes 786432 | tf_op jit(solution)/shard_map/slice | solution.py:27
  4.0 1.3 %collective-permute-start.2 = (f32[16,12,256]{2,1,0:T(8,128)S(1)}, f32[16,12,256]{2,1,0:T(8,128)S(1)}, u32[]{:S(2)}, u32[]{:S(2)}) collective-permute-start(f32[16,12,256]{2,1,0:T(8,128)S(1)} %get-tuple-element.9), channel_id=1, source_target_pairs={{32,0},{33,1},{34,2},{35,3},{36,4},{37,5},{38,6},{39,7},{40,8},{41... | collective-permute-start | bytes 589832 | tf_op jit(solution)/shard_map/ppermute | solution.py:27
  5.3 4.6 %collective-permute-start.5 = (f32[16,12,256]{2,1,0:T(8,128)S(1)}, f32[16,12,256]{2,1,0:T(8,128)S(1)}, u32[]{:S(2)}, u32[]{:S(2)}) collective-permute-start(f32[16,12,256]{2,1,0:T(8,128)S(1)} %get-tuple-element.10), channel_id=1, source_target_pairs={{0,32},{1,33},{2,34},{3,35},{4,36},{5,37},{6,38},{7,39},{8,40},{9,... | collective-permute-start | bytes 589832 | tf_op jit(solution)/shard_map/ppermute | solution.py:27
  9.9 1.4 %fusion = (f32[16,64,12]{2,1,0:T(8,128)S(1)}, f32[16,64,12]{2,1,0:T(8,128)S(1)}) fusion(f32[16,64,256]{2,1,0:T(8,128)} %shard_map.103), kind=kLoop, calls=%fused_computation.3 | loop fusion | bytes 196608 | tf_op jit(solution)/shard_map/slice | solution.py:27
  11.3 3.9 %collective-permute-start = (f32[16,64,12]{2,1,0:T(8,128)S(1)}, f32[16,64,12]{2,1,0:T(8,128)S(1)}, u32[]{:S(2)}, u32[]{:S(2)}) collective-permute-start(f32[16,64,12]{2,1,0:T(8,128)S(1)} %get-tuple-element.7), channel_id=1, source_target_pairs={{1,0},{2,1},{3,2},{4,3},{5,4},{6,5},{7,6},{8,7},{9,8},{10,9},{11,1... | collective-permute-start | bytes 147464 | tf_op jit(solution)/shard_map/ppermute | solution.py:27
  15.2 1.9 %collective-permute-start.1 = (f32[16,64,12]{2,1,0:T(8,128)S(1)}, f32[16,64,12]{2,1,0:T(8,128)S(1)}, u32[]{:S(2)}, u32[]{:S(2)}) collective-permute-start(f32[16,64,12]{2,1,0:T(8,128)S(1)} %get-tuple-element.8), channel_id=1, source_target_pairs={{0,1},{1,2},{2,3},{3,4},{4,5},{5,6},{6,7},{7,8},{8,9},{9,10},{10,1... | collective-permute-start | bytes 147464 | tf_op jit(solution)/shard_map/ppermute | solution.py:27
  17.1 0.0 copy-done
  17.1 0.1 fusion.2
  17.3 1.3 %collective-permute-start.3 = (f32[16,12,12]{2,1,0:T(8,128)S(1)}, f32[16,12,12]{2,1,0:T(8,128)S(1)}, u32[]{:S(2)}, u32[]{:S(2)}) collective-permute-start(f32[16,12,12]{2,1,0:T(8,128)S(1)} %get-tuple-element.11), channel_id=1, source_target_pairs={{33,0},{34,1},{35,2},{36,3},{37,4},{38,5},{39,6},{40,7},{41,8},{42... | collective-permute-start | bytes 27656 | tf_op jit(solution)/shard_map/ppermute | solution.py:27
  18.6 5.0 %collective-permute-done.3 = f32[16,12,12]{2,1,0:T(8,128)S(1)} collective-permute-done((f32[16,12,12]{2,1,0:T(8,128)S(1)}, f32[16,12,12]{2,1,0:T(8,128)S(1)}, u32[]{:S(2)}, u32[]{:S(2)}) %collective-permute-start.3) | collective-permute-done | bytes 9248 | tf_op jit(solution)/shard_map/ppermute | solution.py:27
  23.5 5.3 %collective-permute-start.7 = (f32[16,12,12]{2,1,0:T(8,128)S(1)}, f32[16,12,12]{2,1,0:T(8,128)S(1)}, u32[]{:S(2)}, u32[]{:S(2)}) collective-permute-start(f32[16,12,12]{2,1,0:T(8,128)S(1)} %get-tuple-element.12), channel_id=1, source_target_pairs={{0,33},{1,34},{2,35},{3,36},{4,37},{5,38},{6,39},{7,40},{8,41},{9,... | collective-permute-start | bytes 27656 | tf_op jit(solution)/shard_map/ppermute | solution.py:27
  28.8 3.2 %collective-permute-done.7 = f32[16,12,12]{2,1,0:T(8,128)S(1)} collective-permute-done((f32[16,12,12]{2,1,0:T(8,128)S(1)}, f32[16,12,12]{2,1,0:T(8,128)S(1)}, u32[]{:S(2)}, u32[]{:S(2)}) %collective-permute-start.7) | collective-permute-done | bytes 9248 | tf_op jit(solution)/shard_map/ppermute | solution.py:27
  32.0 7.9 %collective-permute-start.6 = (f32[16,12,12]{2,1,0:T(8,128)S(1)}, f32[16,12,12]{2,1,0:T(8,128)S(1)}, u32[]{:S(2)}, u32[]{:S(2)}) collective-permute-start(f32[16,12,12]{2,1,0:T(8,128)S(1)} %get-tuple-element.13), channel_id=1, source_target_pairs={{1,32},{2,33},{3,34},{4,35},{5,36},{6,37},{7,38},{8,39},{9,40},{10... | collective-permute-start | bytes 27656 | tf_op jit(solution)/shard_map/ppermute | solution.py:27
  39.9 2.5 %collective-permute-done.6 = f32[16,12,12]{2,1,0:T(8,128)S(1)} collective-permute-done((f32[16,12,12]{2,1,0:T(8,128)S(1)}, f32[16,12,12]{2,1,0:T(8,128)S(1)}, u32[]{:S(2)}, u32[]{:S(2)}) %collective-permute-start.6) | collective-permute-done | bytes 9248 | tf_op jit(solution)/shard_map/ppermute | solution.py:27
  42.4 1.3 %collective-permute-start.4 = (f32[16,12,12]{2,1,0:T(8,128)S(1)}, f32[16,12,12]{2,1,0:T(8,128)S(1)}, u32[]{:S(2)}, u32[]{:S(2)}) collective-permute-start(f32[16,12,12]{2,1,0:T(8,128)S(1)} %get-tuple-element.14), channel_id=1, source_target_pairs={{32,1},{33,2},{34,3},{35,4},{36,5},{37,6},{38,7},{39,8},{40,9},{41... | collective-permute-start | bytes 27656 | tf_op jit(solution)/shard_map/ppermute | solution.py:27
  43.7 0.1 pad.2.clone
  43.8 8.1 %collective-permute-done.4 = f32[16,12,12]{2,1,0:T(8,128)S(1)} collective-permute-done((f32[16,12,12]{2,1,0:T(8,128)S(1)}, f32[16,12,12]{2,1,0:T(8,128)S(1)}, u32[]{:S(2)}, u32[]{:S(2)}) %collective-permute-start.4) | collective-permute-done | bytes 9248 | tf_op jit(solution)/shard_map/ppermute | solution.py:27
  51.9 0.0 collective-permute-done
  51.9 0.0 collective-permute-done.1
  51.9 0.0 collective-permute-done.2
  51.9 0.0 collective-permute-done.5
  52.0 2.6 %maximum_maximum_fusion.f_ref = f32[16,88,384]{2,1,0:T(8,128)} fusion(f32[16,12,12]{2,1,0:T(8,128)S(1)} %collective-permute-done.7, f32[16,12,104]{2,1,0:T(8,128)S(1)} %broadcast.10, f32[16,12,12]{2,1,0:T(8,128)S(1)} %collective-permute-done.6, f32[16,12,256]{2,1,0:T(8,128)S(1)} %collective-permute-done.5, f32[16,12,12]{2,1,0:T(8,128)S(1)} %collective-permute-done.4, ...), kind=kLoop, calls=%fused_computation | loop fusion | flops 5947392 | bytes 3954688 | tf_op jit(solution)/shard_map/concatenate | solution.py:44
  54.5 4.4 %shard_map.104 = f32[4,8,128]{2,1,0:T(8,128)} custom-call(f32[16,88,384]{2,1,0:T(8,128)} %maximum_maximum_fusion.f_ref), custom_call_target="tpu_custom_call" | custom-call | tf_op jit(solution)/shard_map/pallas_call | solution.py:306
  58.9 0.8 slice_reduce_fusion
  59.7 0.1 collective-permute-start.8
  59.8 1.1 %collective-permute-done.8 = f32[4]{0:T(128)S(1)} collective-permute-done((f32[4]{0:T(128)S(1)}, f32[4]{0:T(128)S(1)}, u32[]{:S(2)}, u32[]{:S(2)}) %collective-permute-start.8) | collective-permute-done | bytes 48 | tf_op jit(solution)/shard_map/ppermute | solution.py:58
  61.0 0.0 collective-permute-start.9
  61.0 3.6 %collective-permute-done.9 = f32[4]{0:T(128)S(1)} collective-permute-done((f32[4]{0:T(128)S(1)}, f32[4]{0:T(128)S(1)}, u32[]{:S(2)}, u32[]{:S(2)}) %collective-permute-start.9) | collective-permute-done | bytes 48 | tf_op jit(solution)/shard_map/ppermute | solution.py:58
  64.5 0.0 collective-permute-start.10
  64.6 5.1 %collective-permute-done.10 = f32[4]{0:T(128)S(1)} collective-permute-done((f32[4]{0:T(128)S(1)}, f32[4]{0:T(128)S(1)}, u32[]{:S(2)}, u32[]{:S(2)}) %collective-permute-start.10) | collective-permute-done | bytes 48 | tf_op jit(solution)/shard_map/ppermute | solution.py:58
  69.6 0.4 collective-permute-start.11
  70.1 3.1 %collective-permute-done.11 = f32[4]{0:T(128)S(1)} collective-permute-done((f32[4]{0:T(128)S(1)}, f32[4]{0:T(128)S(1)}, u32[]{:S(2)}, u32[]{:S(2)}) %collective-permute-start.11) | collective-permute-done | bytes 48 | tf_op jit(solution)/shard_map/ppermute | solution.py:58
  73.2 0.9 collective-permute-start.12
  74.1 4.1 %collective-permute-done.12 = f32[4]{0:T(128)S(1)} collective-permute-done((f32[4]{0:T(128)S(1)}, f32[4]{0:T(128)S(1)}, u32[]{:S(2)}, u32[]{:S(2)}) %collective-permute-start.12) | collective-permute-done | bytes 48 | tf_op jit(solution)/shard_map/ppermute | solution.py:58
  78.3 2.8 %collective-permute-start.13 = (f32[4]{0:T(128)S(1)}, f32[4]{0:T(128)S(1)}, u32[]{:S(2)}, u32[]{:S(2)}) collective-permute-start(f32[4]{0:T(128)S(1)} %add.37), channel_id=1, source_target_pairs={{0,32},{32,0},{64,96},{96,64},{128,160},{160,128},{192,224},{224,1... | collective-permute-start | bytes 56 | tf_op jit(solution)/shard_map/ppermute | solution.py:58
  81.1 1.5 %collective-permute-done.13 = f32[4]{0:T(128)S(1)} collective-permute-done((f32[4]{0:T(128)S(1)}, f32[4]{0:T(128)S(1)}, u32[]{:S(2)}, u32[]{:S(2)}) %collective-permute-start.13) | collective-permute-done | bytes 48 | tf_op jit(solution)/shard_map/ppermute | solution.py:58
  82.7 7.7 %collective-permute-start.14 = (f32[4]{0:T(128)S(1)}, f32[4]{0:T(128)S(1)}, u32[]{:S(2)}, u32[]{:S(2)}) collective-permute-start(f32[4]{0:T(128)S(1)} %add.38), channel_id=1, source_target_pairs={{0,64},{32,96},{64,0},{96,32},{128,192},{160,224},{192,128},{224,1... | collective-permute-start | bytes 56 | tf_op jit(solution)/shard_map/ppermute | solution.py:58
  90.4 1.5 %collective-permute-done.14 = f32[4]{0:T(128)S(1)} collective-permute-done((f32[4]{0:T(128)S(1)}, f32[4]{0:T(128)S(1)}, u32[]{:S(2)}, u32[]{:S(2)}) %collective-permute-start.14) | collective-permute-done | bytes 48 | tf_op jit(solution)/shard_map/ppermute | solution.py:58
  91.9 5.1 %collective-permute-start.15 = (f32[4]{0:T(128)S(1)}, f32[4]{0:T(128)S(1)}, u32[]{:S(2)}, u32[]{:S(2)}) collective-permute-start(f32[4]{0:T(128)S(1)} %add.39), channel_id=1, source_target_pairs={{0,128},{32,160},{64,192},{96,224},{128,0},{160,32},{192,64},{224,... | collective-permute-start | bytes 56 | tf_op jit(solution)/shard_map/ppermute | solution.py:58
  97.0 2.3 %collective-permute-done.15 = f32[4]{0:T(128)S(1)} collective-permute-done((f32[4]{0:T(128)S(1)}, f32[4]{0:T(128)S(1)}, u32[]{:S(2)}, u32[]{:S(2)}) %collective-permute-start.15) | collective-permute-done | bytes 48 | tf_op jit(solution)/shard_map/ppermute | solution.py:58
  99.4 0.5 multiply_add_fusion.s_ref
  99.9 0.0 copy-start.1
  99.9 7.6 %shard_map.105 = (f32[64,256]{1,0:T(8,128)}, f32[64,256]{1,0:T(8,128)}) custom-call(f32[2]{0:T(128)} %multiply_add_fusion.s_ref, f32[16,88,384]{2,1,0:T(8,128)} %maximum_maximum_fusion.f_ref), custom_call_target="tpu_custom_call" | custom-call | tf_op jit(solution)/shard_map/pallas_call | solution.py:315
  107.6 0.0 copy-done.1
  107.6 0.6 fusion.3
  108.2 0.6 fusion.4
  (10 shorter events, 0.0 us)
Async XLA Ops:
  2.8 14.3 %copy-start = (f32[16,64,256]{2,1,0:T(8,128)S(1)}, f32[16,64,256]{2,1,0:T(8,128)}, u32[]{:S(2)}) copy-start(f32[16,64,256]{2,1,0:T(8,128)} %shard_map.103) | copy-start | bytes 3145732
  4.0 47.9 %collective-permute-start.2 = (f32[16,12,256]{2,1,0:T(8,128)S(1)}, f32[16,12,256]{2,1,0:T(8,128)S(1)}, u32[]{:S(2)}, u32[]{:S(2)}) collective-permute-start(f32[16,12,256]{2,1,0:T(8,128)S(1)} %get-tuple-element.9), channel_id=1, source_target_pairs={{32,0},{33,1},{34,2},{35,3},{36,4},{37,5},{38,6},{39,7},{40,8},{41... | collective-permute-start | bytes 589832 | tf_op jit(solution)/shard_map/ppermute | solution.py:27
  5.3 46.6 %collective-permute-start.5 = (f32[16,12,256]{2,1,0:T(8,128)S(1)}, f32[16,12,256]{2,1,0:T(8,128)S(1)}, u32[]{:S(2)}, u32[]{:S(2)}) collective-permute-start(f32[16,12,256]{2,1,0:T(8,128)S(1)} %get-tuple-element.10), channel_id=1, source_target_pairs={{0,32},{1,33},{2,34},{3,35},{4,36},{5,37},{6,38},{7,39},{8,40},{9,... | collective-permute-start | bytes 589832 | tf_op jit(solution)/shard_map/ppermute | solution.py:27
  11.3 40.7 %collective-permute-start = (f32[16,64,12]{2,1,0:T(8,128)S(1)}, f32[16,64,12]{2,1,0:T(8,128)S(1)}, u32[]{:S(2)}, u32[]{:S(2)}) collective-permute-start(f32[16,64,12]{2,1,0:T(8,128)S(1)} %get-tuple-element.7), channel_id=1, source_target_pairs={{1,0},{2,1},{3,2},{4,3},{5,4},{6,5},{7,6},{8,7},{9,8},{10,9},{11,1... | collective-permute-start | bytes 147464 | tf_op jit(solution)/shard_map/ppermute | solution.py:27
  15.2 36.7 %collective-permute-start.1 = (f32[16,64,12]{2,1,0:T(8,128)S(1)}, f32[16,64,12]{2,1,0:T(8,128)S(1)}, u32[]{:S(2)}, u32[]{:S(2)}) collective-permute-start(f32[16,64,12]{2,1,0:T(8,128)S(1)} %get-tuple-element.8), channel_id=1, source_target_pairs={{0,1},{1,2},{2,3},{3,4},{4,5},{5,6},{6,7},{7,8},{8,9},{9,10},{10,1... | collective-permute-start | bytes 147464 | tf_op jit(solution)/shard_map/ppermute | solution.py:27
  17.3 6.3 %collective-permute-start.3 = (f32[16,12,12]{2,1,0:T(8,128)S(1)}, f32[16,12,12]{2,1,0:T(8,128)S(1)}, u32[]{:S(2)}, u32[]{:S(2)}) collective-permute-start(f32[16,12,12]{2,1,0:T(8,128)S(1)} %get-tuple-element.11), channel_id=1, source_target_pairs={{33,0},{34,1},{35,2},{36,3},{37,4},{38,5},{39,6},{40,7},{41,8},{42... | collective-permute-start | bytes 27656 | tf_op jit(solution)/shard_map/ppermute | solution.py:27
  23.5 8.5 %collective-permute-start.7 = (f32[16,12,12]{2,1,0:T(8,128)S(1)}, f32[16,12,12]{2,1,0:T(8,128)S(1)}, u32[]{:S(2)}, u32[]{:S(2)}) collective-permute-start(f32[16,12,12]{2,1,0:T(8,128)S(1)} %get-tuple-element.12), channel_id=1, source_target_pairs={{0,33},{1,34},{2,35},{3,36},{4,37},{5,38},{6,39},{7,40},{8,41},{9,... | collective-permute-start | bytes 27656 | tf_op jit(solution)/shard_map/ppermute | solution.py:27
  32.0 10.4 %collective-permute-start.6 = (f32[16,12,12]{2,1,0:T(8,128)S(1)}, f32[16,12,12]{2,1,0:T(8,128)S(1)}, u32[]{:S(2)}, u32[]{:S(2)}) collective-permute-start(f32[16,12,12]{2,1,0:T(8,128)S(1)} %get-tuple-element.13), channel_id=1, source_target_pairs={{1,32},{2,33},{3,34},{4,35},{5,36},{6,37},{7,38},{8,39},{9,40},{10... | collective-permute-start | bytes 27656 | tf_op jit(solution)/shard_map/ppermute | solution.py:27
  42.4 9.5 %collective-permute-start.4 = (f32[16,12,12]{2,1,0:T(8,128)S(1)}, f32[16,12,12]{2,1,0:T(8,128)S(1)}, u32[]{:S(2)}, u32[]{:S(2)}) collective-permute-start(f32[16,12,12]{2,1,0:T(8,128)S(1)} %get-tuple-element.14), channel_id=1, source_target_pairs={{32,1},{33,2},{34,3},{35,4},{36,5},{37,6},{38,7},{39,8},{40,9},{41... | collective-permute-start | bytes 27656 | tf_op jit(solution)/shard_map/ppermute | solution.py:27
  59.7 1.2 %collective-permute-start.8 = (f32[4]{0:T(128)S(1)}, f32[4]{0:T(128)S(1)}, u32[]{:S(2)}, u32[]{:S(2)}) collective-permute-start(f32[4]{0:T(128)S(1)} %slice_reduce_fusion), channel_id=1, source_target_pairs={{0,1},{1,0},{2,3},{3,2},{4,5},{5,4},{6,7},{7,6},{8,9},{9,8},{10,11... | collective-permute-start | bytes 56 | tf_op jit(solution)/shard_map/ppermute | solution.py:58
  61.0 3.6 %collective-permute-start.9 = (f32[4]{0:T(128)S(1)}, f32[4]{0:T(128)S(1)}, u32[]{:S(2)}, u32[]{:S(2)}) collective-permute-start(f32[4]{0:T(128)S(1)} %add.33), channel_id=1, source_target_pairs={{0,2},{1,3},{2,0},{3,1},{4,6},{5,7},{6,4},{7,5},{8,10},{9,11},{10,... | collective-permute-start | bytes 56 | tf_op jit(solution)/shard_map/ppermute | solution.py:58
  64.5 5.1 %collective-permute-start.10 = (f32[4]{0:T(128)S(1)}, f32[4]{0:T(128)S(1)}, u32[]{:S(2)}, u32[]{:S(2)}) collective-permute-start(f32[4]{0:T(128)S(1)} %add.34), channel_id=1, source_target_pairs={{0,4},{1,5},{2,6},{3,7},{4,0},{5,1},{6,2},{7,3},{8,12},{9,13},{10,... | collective-permute-start | bytes 56 | tf_op jit(solution)/shard_map/ppermute | solution.py:58
  69.6 3.6 %collective-permute-start.11 = (f32[4]{0:T(128)S(1)}, f32[4]{0:T(128)S(1)}, u32[]{:S(2)}, u32[]{:S(2)}) collective-permute-start(f32[4]{0:T(128)S(1)} %add.35), channel_id=1, source_target_pairs={{0,8},{1,9},{2,10},{3,11},{4,12},{5,13},{6,14},{7,15},{8,0},{9,1},... | collective-permute-start | bytes 56 | tf_op jit(solution)/shard_map/ppermute | solution.py:58
  73.2 5.1 %collective-permute-start.12 = (f32[4]{0:T(128)S(1)}, f32[4]{0:T(128)S(1)}, u32[]{:S(2)}, u32[]{:S(2)}) collective-permute-start(f32[4]{0:T(128)S(1)} %add.36), channel_id=1, source_target_pairs={{0,16},{1,17},{2,18},{3,19},{4,20},{5,21},{6,22},{7,23},{8,24},{9,... | collective-permute-start | bytes 56 | tf_op jit(solution)/shard_map/ppermute | solution.py:58
  78.3 4.4 %collective-permute-start.13 = (f32[4]{0:T(128)S(1)}, f32[4]{0:T(128)S(1)}, u32[]{:S(2)}, u32[]{:S(2)}) collective-permute-start(f32[4]{0:T(128)S(1)} %add.37), channel_id=1, source_target_pairs={{0,32},{32,0},{64,96},{96,64},{128,160},{160,128},{192,224},{224,1... | collective-permute-start | bytes 56 | tf_op jit(solution)/shard_map/ppermute | solution.py:58
  82.7 9.2 %collective-permute-start.14 = (f32[4]{0:T(128)S(1)}, f32[4]{0:T(128)S(1)}, u32[]{:S(2)}, u32[]{:S(2)}) collective-permute-start(f32[4]{0:T(128)S(1)} %add.38), channel_id=1, source_target_pairs={{0,64},{32,96},{64,0},{96,32},{128,192},{160,224},{192,128},{224,1... | collective-permute-start | bytes 56 | tf_op jit(solution)/shard_map/ppermute | solution.py:58
  91.9 7.5 %collective-permute-start.15 = (f32[4]{0:T(128)S(1)}, f32[4]{0:T(128)S(1)}, u32[]{:S(2)}, u32[]{:S(2)}) collective-permute-start(f32[4]{0:T(128)S(1)} %add.39), channel_id=1, source_target_pairs={{0,128},{32,160},{64,192},{96,224},{128,0},{160,32},{192,64},{224,... | collective-permute-start | bytes 56 | tf_op jit(solution)/shard_map/ppermute | solution.py:58
  99.9 7.7 %copy-start.1 = (f32[2]{0:T(128)S(1)}, f32[2]{0:T(128)}, u32[]{:S(2)}) copy-start(f32[2]{0:T(128)} %multiply_add_fusion.s_ref) | copy-start | bytes 28

commit v4 on v2

--- a/solution.py
+++ b/solution.py
@@ -151,24 +151,22 @@
         h = f["thick"][n]
         u, v = f["vel"][n]
         fu, fv = h * f["slope"][0], h * f["slope"][1]
+        states = []
         for _ in range(SWEEPS):
             u, v = sweep_fwd(nb, u, v, h, cov, fric, fu, fv)
-        out.append((u, v))
+            states.append((u, v))
+        out.append(states)
     return out
 
 
-def backward_all(nb, f, steps, scales, g):
+def backward_all(nb, f, steps, scales, g, saved):
     cov, grounded, don_e, don_s, fric = statics(f)
     su, sv = f["slope"][0], f["slope"][1]
     beta = jnp.zeros_like(g)
     for n in reversed(range(steps)):
         h = f["thick"][n]
-        u, v = f["vel"][n]
-        fu, fv = h * su, h * sv
-        states = []
-        for _ in range(SWEEPS):
-            states.append((u, v))
-            u, v = sweep_fwd(nb, u, v, h, cov, fric, fu, fv)
+        states = [f["vel"][n]] + [saved(n, k) for k in range(SWEEPS - 1)]
+        u, v = saved(n, SWEEPS - 1)
         ou, ov = f["obs"][n]
         inv = 1.0 / scales[n]
         bu, bv, h_bar = transport_bwd(nb, u, v, h, cov, don_e, don_s, g)
@@ -225,16 +223,21 @@
 
 
 def forward_kernel(steps, rows, cols):
-    def kernel(f_ref, o_ref):
+    def kernel(f_ref, o_ref, w_ref):
         nb = make_nb(pltpu.roll)
         loader = RefLoader(f_ref, steps)
         out = forward_all(nb, loader, steps)
+        for n, states in enumerate(out):
+            for k, (u, v) in enumerate(states):
+                w_ref[2 * (n * SWEEPS + k)] = u
+                w_ref[2 * (n * SWEEPS + k) + 1] = v
         grounded = (loader["mask"][:rows, :cols] > 1.5).astype(jnp.float32)
 
         def total(x):
             return jnp.broadcast_to(jnp.sum(jnp.sum(x, axis=0, keepdims=True), axis=1, keepdims=True), o_ref.shape[1:])
 
-        for n, (u, v) in enumerate(out):
+        for n, states in enumerate(out):
+            u, v = states[-1]
             ou, ov = loader["obs"][n]
             ou, ov = ou[:rows, :cols], ov[:rows, :cols]
             du, dv = u[:rows, :cols] - ou, v[:rows, :cols] - ov
@@ -245,11 +248,15 @@
 
 
 def backward_kernel(steps, rows, cols):
-    def kernel(s_ref, f_ref, beta_ref, g_ref):
+    def kernel(s_ref, f_ref, w_ref, beta_ref, g_ref):
         nb = make_nb(pltpu.roll)
         loader = RefLoader(f_ref, steps)
         scales = [s_ref[n] for n in range(steps)]
-        beta, g = backward_all(nb, loader, steps, scales, loader["adj"])
+
+        def saved(n, k):
+            return w_ref[2 * (n * SWEEPS + k)], w_ref[2 * (n * SWEEPS + k) + 1]
+
+        beta, g = backward_all(nb, loader, steps, scales, loader["adj"], saved)
         beta_ref[...] = beta[:rows, :cols]
         g_ref[...] = g[:rows, :cols]
 
@@ -285,21 +292,25 @@
 
 
 def run_forward(fields, steps, rows, cols):
+    _, patch_rows, patch_cols = fields.shape
     return pl.pallas_call(
         forward_kernel(steps, rows, cols),
-        out_shape=jax.ShapeDtypeStruct((2 * steps, 8, LANES), jnp.float32),
+        out_shape=(
+            jax.ShapeDtypeStruct((2 * steps, 8, LANES), jnp.float32),
+            jax.ShapeDtypeStruct((2 * SWEEPS * steps, patch_rows, patch_cols), jnp.float32),
+        ),
         in_specs=[pl.BlockSpec(memory_space=pltpu.VMEM)],
-        out_specs=pl.BlockSpec(memory_space=pltpu.VMEM),
+        out_specs=(pl.BlockSpec(memory_space=pltpu.VMEM),) * 2,
     )(fields)
 
 
-def run_backward(scales, fields, steps, rows, cols):
+def run_backward(scales, fields, states, steps, rows, cols):
     return pl.pallas_call(
         backward_kernel(steps, rows, cols),
         out_shape=(jax.ShapeDtypeStruct((rows, cols), jnp.float32),) * 2,
-        in_specs=[pl.BlockSpec(memory_space=pltpu.SMEM), pl.BlockSpec(memory_space=pltpu.VMEM)],
+        in_specs=[pl.BlockSpec(memory_space=pltpu.SMEM)] + [pl.BlockSpec(memory_space=pltpu.VMEM)] * 2,
         out_specs=(pl.BlockSpec(memory_space=pltpu.VMEM),) * 2,
-    )(scales, fields)
+    )(scales, fields, states)
 
 
 def on_device(
@@ -326,14 +337,15 @@
         thickness_adjoint,
     )
     wide = wrapped_patch(fields, HALO)
-    local_sums = run_forward(wide, steps, rows, cols)[:, 0, 0]
+    sums, states = run_forward(wide, steps, rows, cols)
+    local_sums = sums[:, 0, 0]
     totals = butterfly_sum(local_sums, ("gx", "gy"))
     cell_count = rows * cols * lax.axis_size("gy") * lax.axis_size("gx")
     scales = totals[:steps] / cell_count + EPSILON
     misfit = jnp.zeros((), f32)
     for n in reversed(range(steps)):
         misfit = misfit + totals[steps + n] / cell_count / scales[n]
-    grads = run_backward(scales, wide, steps, rows, cols)
+    grads = run_backward(scales, wide, states, steps, rows, cols)
     return (grads[0], grads[1], misfit)
 
 

time: 86.7 us -> 87.4 us (level)
  Pallas kernels: 14.2 us -> 15.5 us
    pallas_call x1, Pallas kernels: 4.4 us -> 5.38 us  [run_forward(): pl.pallas_call(forward_kernel(steps, rows, cols), out_shape=(jax.ShapeDty...]
where the time goes in v4:
time: 87.4 us; the launch traced here: 87 us
  waiting for transfers between devices  32.8 us (38%)
  starting transfers between devices  26.6 us (30%)
  Pallas kernels  15.5 us (18%)
  local copies, waits for them, and re-layouts  4.55 us (5%)
  between operations  4.43 us (5%)
  other arithmetic  3.07 us (4%)
    ppermute x8, waiting for transfers between devices, butterfly_sum(): lax.ppermute(values, axis, [(i, i ^ stride) for i in range(count)])  21.7 us
    ppermute x8, starting transfers between devices, butterfly_sum(): lax.ppermute(values, axis, [(i, i ^ stride) for i in range(count)])  15.4 us
    pallas_call x1, Pallas kernels, run_backward(): pl.pallas_call(backward_kernel(steps, rows, cols), out_shape=(jax.ShapeDt...  7.94 us
    ppermute x2, waiting for transfers between devices, wrapped_patch(): lax.ppermute(lax.slice_in_dim(block, block.shape[dim] - width, None, axis...  6.92 us
    ppermute x2, starting transfers between devices, wrapped_patch(): lax.ppermute(lax.slice_in_dim(block, block.shape[dim] - width, None, axis...  6.49 us
    pallas_call x1, Pallas kernels, run_forward(): pl.pallas_call(forward_kernel(steps, rows, cols), out_shape=(jax.ShapeDty...  5.38 us
    ppermute x2, starting transfers between devices, wrapped_patch(): lax.ppermute(lax.slice_in_dim(block, 0, width, axis=dim), axis, backward)  4.76 us
    ppermute x2, waiting for transfers between devices, wrapped_patch(): lax.ppermute(lax.slice_in_dim(block, 0, width, axis=dim), axis, backward)  4.26 us
  transfers between devices with their start and end apart: 12, of which 11 were waited for; matrix products, arithmetic and copies ran while one was open for 1% of the time, Pallas kernels for 0%

profile of v4, /device:TPU:24, one launch (start us, length us, event | category | flops | bytes accessed | tf_op | source)
XLA Modules:
  0.0 87.0 jit_solution(13689467214123183255)
XLA Ops:
  0.6 2.2 %shard_map.103 = f32[16,64,256]{2,1,0:T(8,128)} custom-call(bf16[2,64,256]{2,1,0:T(8,128)(2,1)} %thick_ref.1, bf16[2,2,64,256]{3,2,1,0:T(8,128)(2,1)} %vel_ref.1, bf16[2,64,256]{2,1,0:T(8,128)(2,1)} %slope_ref.1, f32[64,256]{1,0:T(8,128)} %beta_ref.1, s32[64,256]{1,0:T(8,128)} %mask_ref.1, s32[64,256]{1,0:T(8,128)} %flags_ref.1, ...), custom_call_target="tpu_custom_call" | custom-call | tf_op jit(solution)/shard_map/pallas_call | solution.py:286
  2.8 1.1 %fusion.1 = (f32[16,12,256]{2,1,0:T(8,128)S(1)}, f32[16,12,256]{2,1,0:T(8,128)S(1)}) fusion(f32[16,64,256]{2,1,0:T(8,128)} %shard_map.103), kind=kLoop, calls=%fused_computation.5 | loop fusion | bytes 786432 | tf_op jit(solution)/shard_map/slice | solution.py:22
  3.9 1.3 %collective-permute-start = (f32[16,12,256]{2,1,0:T(8,128)S(1)}, f32[16,12,256]{2,1,0:T(8,128)S(1)}, u32[]{:S(2)}, u32[]{:S(2)}) collective-permute-start(f32[16,12,256]{2,1,0:T(8,128)S(1)} %get-tuple-element.13), channel_id=1, source_target_pairs={{32,0},{64,32},{96,64},{128,96},{160,128},{192,160},{224,192},{33,... | collective-permute-start | bytes 589832 | tf_op jit(solution)/shard_map/ppermute | solution.py:22
  5.2 4.6 %collective-permute-start.1 = (f32[16,12,256]{2,1,0:T(8,128)S(1)}, f32[16,12,256]{2,1,0:T(8,128)S(1)}, u32[]{:S(2)}, u32[]{:S(2)}) collective-permute-start(f32[16,12,256]{2,1,0:T(8,128)S(1)} %get-tuple-element.14), channel_id=1, source_target_pairs={{0,32},{32,64},{64,96},{96,128},{128,160},{160,192},{192,224},{1,3... | collective-permute-start | bytes 589832 | tf_op jit(solution)/shard_map/ppermute | solution.py:19
  9.8 4.3 %collective-permute-done = f32[16,12,256]{2,1,0:T(8,128)S(1)} collective-permute-done((f32[16,12,256]{2,1,0:T(8,128)S(1)}, f32[16,12,256]{2,1,0:T(8,128)S(1)}, u32[]{:S(2)}, u32[]{:S(2)}) %collective-permute-start) | collective-permute-done | bytes 196640 | tf_op jit(solution)/shard_map/ppermute | solution.py:22
  14.0 1.2 %collective-permute-done.1 = f32[16,12,256]{2,1,0:T(8,128)S(1)} collective-permute-done((f32[16,12,256]{2,1,0:T(8,128)S(1)}, f32[16,12,256]{2,1,0:T(8,128)S(1)}, u32[]{:S(2)}, u32[]{:S(2)}) %collective-permute-start.1) | collective-permute-done | bytes 196640 | tf_op jit(solution)/shard_map/ppermute | solution.py:19
  15.2 1.4 %pad_maximum_fusion.1 = f32[16,88,256]{2,1,0:T(8,128)S(1)} fusion(f32[16,12,256]{2,1,0:T(8,128)S(1)} %collective-permute-done.1, f32[16,12,256]{2,1,0:T(8,128)S(1)} %collective-permute-done, f32[16,64,256]{2,1,0:T(8,128)} %shard_map.103), kind=kLoop, calls=%fused_computation.1 | loop fusion | flops 720896 | bytes 2883584 | tf_op jit(solution)/shard_map/concatenate | solution.py:24
  16.6 0.3 fusion
  16.8 0.0 copy-start
  16.8 0.3 copy.11
  17.1 3.5 %collective-permute-start.2 = (f32[16,88,12]{1,0,2:T(8,128)S(1)}, f32[16,88,12]{1,0,2:T(8,128)S(1)}, u32[]{:S(2)}, u32[]{:S(2)}) collective-permute-start(f32[16,88,12]{1,0,2:T(8,128)S(1)} %copy.11), channel_id=1, source_target_pairs={{1,0},{2,1},{3,2},{4,3},{5,4},{6,5},{7,6},{8,7},{9,8},{10,9},{11,1... | collective-permute-start | bytes 202760 | tf_op jit(solution)/shard_map/ppermute | solution.py:22
  20.6 0.3 copy.12
  20.8 1.9 %collective-permute-start.3 = (f32[16,88,12]{1,0,2:T(8,128)S(1)}, f32[16,88,12]{1,0,2:T(8,128)S(1)}, u32[]{:S(2)}, u32[]{:S(2)}) collective-permute-start(f32[16,88,12]{1,0,2:T(8,128)S(1)} %copy.12), channel_id=1, source_target_pairs={{0,1},{1,2},{2,3},{3,4},{4,5},{5,6},{6,7},{7,8},{8,9},{9,10},{10,1... | collective-permute-start | bytes 202760 | tf_op jit(solution)/shard_map/ppermute | solution.py:19
  22.8 0.1 pad.4.clone
  22.8 0.0 collective-permute-done.2
  22.8 0.3 copy.13
  23.1 5.7 %collective-permute-done.3 = f32[16,88,12]{1,0,2:T(8,128)S(1)} collective-permute-done((f32[16,88,12]{1,0,2:T(8,128)S(1)}, f32[16,88,12]{1,0,2:T(8,128)S(1)}, u32[]{:S(2)}, u32[]{:S(2)}) %collective-permute-start.3) | collective-permute-done | bytes 67616 | tf_op jit(solution)/shard_map/ppermute | solution.py:19
  28.9 0.3 copy.14
  29.2 0.0 copy-done
  29.2 1.7 %pad_maximum_fusion.f_ref = f32[16,88,384]{2,1,0:T(8,128)} fusion(f32[16,88,12]{2,1,0:T(8,128)S(1)} %copy.14, f32[16,88,12]{2,1,0:T(8,128)S(1)} %copy.13, f32[16,12,256]{2,1,0:T(8,128)S(1)} %collective-permute-done.1, f32[16,12,256]{2,1,0:T(8,128)S(1)} %collective-permute-done, f32[16,64,256]{2,1,0:T(8,128)S(1)} %copy-done, f32[384]{0:T(512)S(1)} %pad.4.clone), kind=kLoop, calls=%fused_computation | loop fusion | flops 2703360 | bytes 3741184 | tf_op jit(solution)/shard_map/concatenate | solution.py:28
  30.8 5.4 %shard_map.104 = (f32[4,8,128]{2,1,0:T(8,128)}, f32[12,88,384]{2,1,0:T(8,128)}) custom-call(f32[16,88,384]{2,1,0:T(8,128)} %pad_maximum_fusion.f_ref), custom_call_target="tpu_custom_call" | custom-call | tf_op jit(solution)/shard_map/pallas_call | solution.py:296
  36.2 0.8 slice_reduce_fusion
  37.1 0.1 collective-permute-start.4
  37.1 1.1 %collective-permute-done.4 = f32[4]{0:T(128)S(1)} collective-permute-done((f32[4]{0:T(128)S(1)}, f32[4]{0:T(128)S(1)}, u32[]{:S(2)}, u32[]{:S(2)}) %collective-permute-start.4) | collective-permute-done | bytes 48 | tf_op jit(solution)/shard_map/ppermute | solution.py:40
  38.3 0.0 collective-permute-start.5
  38.3 3.6 %collective-permute-done.5 = f32[4]{0:T(128)S(1)} collective-permute-done((f32[4]{0:T(128)S(1)}, f32[4]{0:T(128)S(1)}, u32[]{:S(2)}, u32[]{:S(2)}) %collective-permute-start.5) | collective-permute-done | bytes 48 | tf_op jit(solution)/shard_map/ppermute | solution.py:40
  41.9 0.0 collective-permute-start.6
  41.9 5.1 %collective-permute-done.6 = f32[4]{0:T(128)S(1)} collective-permute-done((f32[4]{0:T(128)S(1)}, f32[4]{0:T(128)S(1)}, u32[]{:S(2)}, u32[]{:S(2)}) %collective-permute-start.6) | collective-permute-done | bytes 48 | tf_op jit(solution)/shard_map/ppermute | solution.py:40
  46.9 0.4 collective-permute-start.7
  47.4 3.1 %collective-permute-done.7 = f32[4]{0:T(128)S(1)} collective-permute-done((f32[4]{0:T(128)S(1)}, f32[4]{0:T(128)S(1)}, u32[]{:S(2)}, u32[]{:S(2)}) %collective-permute-start.7) | collective-permute-done | bytes 48 | tf_op jit(solution)/shard_map/ppermute | solution.py:40
  50.5 0.9 %collective-permute-start.8 = (f32[4]{0:T(128)S(1)}, f32[4]{0:T(128)S(1)}, u32[]{:S(2)}, u32[]{:S(2)}) collective-permute-start(f32[4]{0:T(128)S(1)} %add.36), channel_id=1, source_target_pairs={{0,16},{1,17},{2,18},{3,19},{4,20},{5,21},{6,22},{7,23},{8,24},{9,... | collective-permute-start | bytes 56 | tf_op jit(solution)/shard_map/ppermute | solution.py:40
  51.5 4.1 %collective-permute-done.8 = f32[4]{0:T(128)S(1)} collective-permute-done((f32[4]{0:T(128)S(1)}, f32[4]{0:T(128)S(1)}, u32[]{:S(2)}, u32[]{:S(2)}) %collective-permute-start.8) | collective-permute-done | bytes 48 | tf_op jit(solution)/shard_map/ppermute | solution.py:40
  55.6 2.5 %collective-permute-start.9 = (f32[4]{0:T(128)S(1)}, f32[4]{0:T(128)S(1)}, u32[]{:S(2)}, u32[]{:S(2)}) collective-permute-start(f32[4]{0:T(128)S(1)} %add.37), channel_id=1, source_target_pairs={{0,32},{32,0},{64,96},{96,64},{128,160},{160,128},{192,224},{224,1... | collective-permute-start | bytes 56 | tf_op jit(solution)/shard_map/ppermute | solution.py:40
  58.1 1.5 %collective-permute-done.9 = f32[4]{0:T(128)S(1)} collective-permute-done((f32[4]{0:T(128)S(1)}, f32[4]{0:T(128)S(1)}, u32[]{:S(2)}, u32[]{:S(2)}) %collective-permute-start.9) | collective-permute-done | bytes 48 | tf_op jit(solution)/shard_map/ppermute | solution.py:40
  59.6 3.9 %collective-permute-start.10 = (f32[4]{0:T(128)S(1)}, f32[4]{0:T(128)S(1)}, u32[]{:S(2)}, u32[]{:S(2)}) collective-permute-start(f32[4]{0:T(128)S(1)} %add.38), channel_id=1, source_target_pairs={{0,64},{32,96},{64,0},{96,32},{128,192},{160,224},{192,128},{224,1... | collective-permute-start | bytes 56 | tf_op jit(solution)/shard_map/ppermute | solution.py:40
  63.5 1.5 %collective-permute-done.10 = f32[4]{0:T(128)S(1)} collective-permute-done((f32[4]{0:T(128)S(1)}, f32[4]{0:T(128)S(1)}, u32[]{:S(2)}, u32[]{:S(2)}) %collective-permute-start.10) | collective-permute-done | bytes 48 | tf_op jit(solution)/shard_map/ppermute | solution.py:40
  65.1 7.5 %collective-permute-start.11 = (f32[4]{0:T(128)S(1)}, f32[4]{0:T(128)S(1)}, u32[]{:S(2)}, u32[]{:S(2)}) collective-permute-start(f32[4]{0:T(128)S(1)} %add.39), channel_id=1, source_target_pairs={{0,128},{32,160},{64,192},{96,224},{128,0},{160,32},{192,64},{224,... | collective-permute-start | bytes 56 | tf_op jit(solution)/shard_map/ppermute | solution.py:40
  72.6 1.5 %collective-permute-done.11 = f32[4]{0:T(128)S(1)} collective-permute-done((f32[4]{0:T(128)S(1)}, f32[4]{0:T(128)S(1)}, u32[]{:S(2)}, u32[]{:S(2)}) %collective-permute-start.11) | collective-permute-done | bytes 48 | tf_op jit(solution)/shard_map/ppermute | solution.py:40
  74.2 0.0 copy-start.1
  74.2 0.6 fusion.3
  74.8 0.6 fusion.2
  75.4 0.0 copy-done.1
  75.4 7.9 %shard_map.105 = (f32[64,256]{1,0:T(8,128)}, f32[64,256]{1,0:T(8,128)}) custom-call(f32[2]{0:T(128)} %copy-done.1, f32[16,88,384]{2,1,0:T(8,128)} %pad_maximum_fusion.f_ref, f32[12,88,384]{2,1,0:T(8,128)} %get-tuple-element.8.w_ref), custom_call_target="tpu_custom_call" | custom-call | tf_op jit(solution)/shard_map/pallas_call | solution.py:308
  (10 shorter events, 0.0 us)
Async XLA Ops:
  3.9 10.1 %collective-permute-start = (f32[16,12,256]{2,1,0:T(8,128)S(1)}, f32[16,12,256]{2,1,0:T(8,128)S(1)}, u32[]{:S(2)}, u32[]{:S(2)}) collective-permute-start(f32[16,12,256]{2,1,0:T(8,128)S(1)} %get-tuple-element.13), channel_id=1, source_target_pairs={{32,0},{64,32},{96,64},{128,96},{160,128},{192,160},{224,192},{33,... | collective-permute-start | bytes 589832 | tf_op jit(solution)/shard_map/ppermute | solution.py:22
  5.2 10.0 %collective-permute-start.1 = (f32[16,12,256]{2,1,0:T(8,128)S(1)}, f32[16,12,256]{2,1,0:T(8,128)S(1)}, u32[]{:S(2)}, u32[]{:S(2)}) collective-permute-start(f32[16,12,256]{2,1,0:T(8,128)S(1)} %get-tuple-element.14), channel_id=1, source_target_pairs={{0,32},{32,64},{64,96},{96,128},{128,160},{160,192},{192,224},{1,3... | collective-permute-start | bytes 589832 | tf_op jit(solution)/shard_map/ppermute | solution.py:19
  16.8 12.3 %copy-start = (f32[16,64,256]{2,1,0:T(8,128)S(1)}, f32[16,64,256]{2,1,0:T(8,128)}, u32[]{:S(2)}) copy-start(f32[16,64,256]{2,1,0:T(8,128)} %shard_map.103) | copy-start | bytes 3145732
  17.1 5.8 %collective-permute-start.2 = (f32[16,88,12]{1,0,2:T(8,128)S(1)}, f32[16,88,12]{1,0,2:T(8,128)S(1)}, u32[]{:S(2)}, u32[]{:S(2)}) collective-permute-start(f32[16,88,12]{1,0,2:T(8,128)S(1)} %copy.11), channel_id=1, source_target_pairs={{1,0},{2,1},{3,2},{4,3},{5,4},{6,5},{7,6},{8,7},{9,8},{10,9},{11,1... | collective-permute-start | bytes 202760 | tf_op jit(solution)/shard_map/ppermute | solution.py:22
  20.8 8.1 %collective-permute-start.3 = (f32[16,88,12]{1,0,2:T(8,128)S(1)}, f32[16,88,12]{1,0,2:T(8,128)S(1)}, u32[]{:S(2)}, u32[]{:S(2)}) collective-permute-start(f32[16,88,12]{1,0,2:T(8,128)S(1)} %copy.12), channel_id=1, source_target_pairs={{0,1},{1,2},{2,3},{3,4},{4,5},{5,6},{6,7},{7,8},{8,9},{9,10},{10,1... | collective-permute-start | bytes 202760 | tf_op jit(solution)/shard_map/ppermute | solution.py:19
  37.1 1.2 %collective-permute-start.4 = (f32[4]{0:T(128)S(1)}, f32[4]{0:T(128)S(1)}, u32[]{:S(2)}, u32[]{:S(2)}) collective-permute-start(f32[4]{0:T(128)S(1)} %slice_reduce_fusion), channel_id=1, source_target_pairs={{0,1},{1,0},{2,3},{3,2},{4,5},{5,4},{6,7},{7,6},{8,9},{9,8},{10,11... | collective-permute-start | bytes 56 | tf_op jit(solution)/shard_map/ppermute | solution.py:40
  38.3 3.6 %collective-permute-start.5 = (f32[4]{0:T(128)S(1)}, f32[4]{0:T(128)S(1)}, u32[]{:S(2)}, u32[]{:S(2)}) collective-permute-start(f32[4]{0:T(128)S(1)} %add.33), channel_id=1, source_target_pairs={{0,2},{1,3},{2,0},{3,1},{4,6},{5,7},{6,4},{7,5},{8,10},{9,11},{10,... | collective-permute-start | bytes 56 | tf_op jit(solution)/shard_map/ppermute | solution.py:40
  41.9 5.1 %collective-permute-start.6 = (f32[4]{0:T(128)S(1)}, f32[4]{0:T(128)S(1)}, u32[]{:S(2)}, u32[]{:S(2)}) collective-permute-start(f32[4]{0:T(128)S(1)} %add.34), channel_id=1, source_target_pairs={{0,4},{1,5},{2,6},{3,7},{4,0},{5,1},{6,2},{7,3},{8,12},{9,13},{10,... | collective-permute-start | bytes 56 | tf_op jit(solution)/shard_map/ppermute | solution.py:40
  46.9 3.6 %collective-permute-start.7 = (f32[4]{0:T(128)S(1)}, f32[4]{0:T(128)S(1)}, u32[]{:S(2)}, u32[]{:S(2)}) collective-permute-start(f32[4]{0:T(128)S(1)} %add.35), channel_id=1, source_target_pairs={{0,8},{1,9},{2,10},{3,11},{4,12},{5,13},{6,14},{7,15},{8,0},{9,1},... | collective-permute-start | bytes 56 | tf_op jit(solution)/shard_map/ppermute | solution.py:40
  50.5 5.1 %collective-permute-start.8 = (f32[4]{0:T(128)S(1)}, f32[4]{0:T(128)S(1)}, u32[]{:S(2)}, u32[]{:S(2)}) collective-permute-start(f32[4]{0:T(128)S(1)} %add.36), channel_id=1, source_target_pairs={{0,16},{1,17},{2,18},{3,19},{4,20},{5,21},{6,22},{7,23},{8,24},{9,... | collective-permute-start | bytes 56 | tf_op jit(solution)/shard_map/ppermute | solution.py:40
  55.6 4.0 %collective-permute-start.9 = (f32[4]{0:T(128)S(1)}, f32[4]{0:T(128)S(1)}, u32[]{:S(2)}, u32[]{:S(2)}) collective-permute-start(f32[4]{0:T(128)S(1)} %add.37), channel_id=1, source_target_pairs={{0,32},{32,0},{64,96},{96,64},{128,160},{160,128},{192,224},{224,1... | collective-permute-start | bytes 56 | tf_op jit(solution)/shard_map/ppermute | solution.py:40
  59.6 5.5 %collective-permute-start.10 = (f32[4]{0:T(128)S(1)}, f32[4]{0:T(128)S(1)}, u32[]{:S(2)}, u32[]{:S(2)}) collective-permute-start(f32[4]{0:T(128)S(1)} %add.38), channel_id=1, source_target_pairs={{0,64},{32,96},{64,0},{96,32},{128,192},{160,224},{192,128},{224,1... | collective-permute-start | bytes 56 | tf_op jit(solution)/shard_map/ppermute | solution.py:40
  65.1 9.1 %collective-permute-start.11 = (f32[4]{0:T(128)S(1)}, f32[4]{0:T(128)S(1)}, u32[]{:S(2)}, u32[]{:S(2)}) collective-permute-start(f32[4]{0:T(128)S(1)} %add.39), channel_id=1, source_target_pairs={{0,128},{32,160},{64,192},{96,224},{128,0},{160,32},{192,64},{224,... | collective-permute-start | bytes 56 | tf_op jit(solution)/shard_map/ppermute | solution.py:40
  74.2 1.2 %copy-start.1 = (f32[2]{0:T(128)}, f32[2]{0:T(128)S(1)}, u32[]{:S(2)}) copy-start(f32[2]{0:T(128)S(1)} %multiply_add_fusion.s_ref) | copy-start | bytes 28

commit v5 on v2

--- a/solution.py
+++ b/solution.py
@@ -232,7 +232,7 @@
         grounded = (loader["mask"][:rows, :cols] > 1.5).astype(jnp.float32)
 
         def total(x):
-            return jnp.broadcast_to(jnp.sum(jnp.sum(x, axis=0, keepdims=True), axis=1, keepdims=True), o_ref.shape[1:])
+            return jnp.sum(x)
 
         for n, (u, v) in enumerate(out):
             ou, ov = loader["obs"][n]
@@ -244,11 +244,15 @@
     return kernel
 
 
-def backward_kernel(steps, rows, cols):
-    def kernel(s_ref, f_ref, beta_ref, g_ref):
+def backward_kernel(steps, rows, cols, cell_count):
+    def kernel(s_ref, f_ref, beta_ref, g_ref, m_ref):
         nb = make_nb(pltpu.roll)
         loader = RefLoader(f_ref, steps)
-        scales = [s_ref[n] for n in range(steps)]
+        scales = [s_ref[n] / cell_count + EPSILON for n in range(steps)]
+        misfit = s_ref[2 * steps - 1] / cell_count / scales[steps - 1]
+        for n in reversed(range(steps - 1)):
+            misfit = misfit + s_ref[steps + n] / cell_count / scales[n]
+        m_ref[0] = misfit
         beta, g = backward_all(nb, loader, steps, scales, loader["adj"])
         beta_ref[...] = beta[:rows, :cols]
         g_ref[...] = g[:rows, :cols]
@@ -287,19 +291,20 @@
 def run_forward(fields, steps, rows, cols):
     return pl.pallas_call(
         forward_kernel(steps, rows, cols),
-        out_shape=jax.ShapeDtypeStruct((2 * steps, 8, LANES), jnp.float32),
+        out_shape=jax.ShapeDtypeStruct((2 * steps,), jnp.float32),
         in_specs=[pl.BlockSpec(memory_space=pltpu.VMEM)],
-        out_specs=pl.BlockSpec(memory_space=pltpu.VMEM),
+        out_specs=pl.BlockSpec(memory_space=pltpu.SMEM),
     )(fields)
 
 
-def run_backward(scales, fields, steps, rows, cols):
+def run_backward(totals, fields, steps, rows, cols, cell_count):
     return pl.pallas_call(
-        backward_kernel(steps, rows, cols),
-        out_shape=(jax.ShapeDtypeStruct((rows, cols), jnp.float32),) * 2,
+        backward_kernel(steps, rows, cols, cell_count),
+        out_shape=(jax.ShapeDtypeStruct((rows, cols), jnp.float32),) * 2
+        + (jax.ShapeDtypeStruct((1,), jnp.float32),),
         in_specs=[pl.BlockSpec(memory_space=pltpu.SMEM), pl.BlockSpec(memory_space=pltpu.VMEM)],
-        out_specs=(pl.BlockSpec(memory_space=pltpu.VMEM),) * 2,
-    )(scales, fields)
+        out_specs=(pl.BlockSpec(memory_space=pltpu.VMEM),) * 2 + (pl.BlockSpec(memory_space=pltpu.SMEM),),
+    )(totals, fields)
 
 
 def on_device(
@@ -326,15 +331,11 @@
         thickness_adjoint,
     )
     wide = wrapped_patch(fields, HALO)
-    local_sums = run_forward(wide, steps, rows, cols)[:, 0, 0]
+    local_sums = run_forward(wide, steps, rows, cols)
     totals = butterfly_sum(local_sums, ("gx", "gy"))
     cell_count = rows * cols * lax.axis_size("gy") * lax.axis_size("gx")
-    scales = totals[:steps] / cell_count + EPSILON
-    misfit = jnp.zeros((), f32)
-    for n in reversed(range(steps)):
-        misfit = misfit + totals[steps + n] / cell_count / scales[n]
-    grads = run_backward(scales, wide, steps, rows, cols)
-    return (grads[0], grads[1], misfit)
+    beta_gradient, thickness_gradient, misfit = run_backward(totals, wide, steps, rows, cols, cell_count)
+    return (beta_gradient, thickness_gradient, misfit.reshape(()))
 
 
 def solution(mesh):

time: 86.7 us -> 81.8 us (0.943)
  between operations: 4.47 us -> 0.91 us
  local copies, waits for them, and re-layouts: 4.53 us -> 2.48 us
    slice x3 -> x0, local copies, waits for them, and re-layouts: 2.04 us -> none  [the longest x2 1.21 us: on_device(): misfit = misfit + totals[steps + n] / cell_count / scales[n]]
    add x8, other arithmetic: 0.03 us -> 1.26 us  [butterfly_sum(): values + lax.ppermute(values, axis, [(i, i ^ stride) for i in range(count)])]
where the time goes in v5:
time: 81.8 us; the launch traced here: 81.4 us
  waiting for transfers between devices  33 us (40%)
  starting transfers between devices  26.6 us (33%)
  Pallas kernels  14.1 us (17%)
  other arithmetic  4.31 us (5%)
  local copies, waits for them, and re-layouts  2.48 us (3%)
  between operations  0.91 us (1%)
    ppermute x8, waiting for transfers between devices, butterfly_sum(): lax.ppermute(values, axis, [(i, i ^ stride) for i in range(count)])  21.8 us
    ppermute x8, starting transfers between devices, butterfly_sum(): lax.ppermute(values, axis, [(i, i ^ stride) for i in range(count)])  15.4 us
    pallas_call x1, Pallas kernels, run_backward(): pl.pallas_call(backward_kernel(steps, rows, cols, cell_count), out_shape=...  7.63 us
    ppermute x2, waiting for transfers between devices, wrapped_patch(): lax.ppermute(lax.slice_in_dim(block, block.shape[dim] - width, None, axis...  6.92 us
    ppermute x2, starting transfers between devices, wrapped_patch(): lax.ppermute(lax.slice_in_dim(block, block.shape[dim] - width, None, axis...  6.49 us
    ppermute x2, starting transfers between devices, wrapped_patch(): lax.ppermute(lax.slice_in_dim(block, 0, width, axis=dim), axis, backward)  4.76 us
    pallas_call x1, Pallas kernels, run_forward(): pl.pallas_call(forward_kernel(steps, rows, cols), out_shape=jax.ShapeDtyp...  4.29 us
    ppermute x2, waiting for transfers between devices, wrapped_patch(): lax.ppermute(lax.slice_in_dim(block, 0, width, axis=dim), axis, backward)  4.26 us
  transfers between devices with their start and end apart: 12, of which 11 were waited for; matrix products, arithmetic and copies ran while one was open for 1% of the time, Pallas kernels for 0%

profile of v5, /device:TPU:24, one launch (start us, length us, event | category | flops | bytes accessed | tf_op | source)
XLA Modules:
  0.0 81.4 jit_solution(9609749391794049798)
XLA Ops:
  0.6 2.2 %shard_map.103 = f32[16,64,256]{2,1,0:T(8,128)} custom-call(bf16[2,64,256]{2,1,0:T(8,128)(2,1)} %thick_ref.1, bf16[2,2,64,256]{3,2,1,0:T(8,128)(2,1)} %vel_ref.1, bf16[2,64,256]{2,1,0:T(8,128)(2,1)} %slope_ref.1, f32[64,256]{1,0:T(8,128)} %beta_ref.1, s32[64,256]{1,0:T(8,128)} %mask_ref.1, s32[64,256]{1,0:T(8,128)} %flags_ref.1, ...), custom_call_target="tpu_custom_call" | custom-call | tf_op jit(solution)/shard_map/pallas_call | solution.py:283
  2.8 1.1 %fusion.1 = (f32[16,12,256]{2,1,0:T(8,128)S(1)}, f32[16,12,256]{2,1,0:T(8,128)S(1)}) fusion(f32[16,64,256]{2,1,0:T(8,128)} %shard_map.103), kind=kLoop, calls=%fused_computation.3 | loop fusion | bytes 786432 | tf_op jit(solution)/shard_map/slice | solution.py:22
  3.9 1.3 %collective-permute-start = (f32[16,12,256]{2,1,0:T(8,128)S(1)}, f32[16,12,256]{2,1,0:T(8,128)S(1)}, u32[]{:S(2)}, u32[]{:S(2)}) collective-permute-start(f32[16,12,256]{2,1,0:T(8,128)S(1)} %get-tuple-element.11), channel_id=1, source_target_pairs={{32,0},{64,32},{96,64},{128,96},{160,128},{192,160},{224,192},{33,... | collective-permute-start | bytes 589832 | tf_op jit(solution)/shard_map/ppermute | solution.py:22
  5.2 4.6 %collective-permute-start.1 = (f32[16,12,256]{2,1,0:T(8,128)S(1)}, f32[16,12,256]{2,1,0:T(8,128)S(1)}, u32[]{:S(2)}, u32[]{:S(2)}) collective-permute-start(f32[16,12,256]{2,1,0:T(8,128)S(1)} %get-tuple-element.12), channel_id=1, source_target_pairs={{0,32},{32,64},{64,96},{96,128},{128,160},{160,192},{192,224},{1,3... | collective-permute-start | bytes 589832 | tf_op jit(solution)/shard_map/ppermute | solution.py:19
  9.8 4.3 %collective-permute-done = f32[16,12,256]{2,1,0:T(8,128)S(1)} collective-permute-done((f32[16,12,256]{2,1,0:T(8,128)S(1)}, f32[16,12,256]{2,1,0:T(8,128)S(1)}, u32[]{:S(2)}, u32[]{:S(2)}) %collective-permute-start) | collective-permute-done | bytes 196640 | tf_op jit(solution)/shard_map/ppermute | solution.py:22
  14.0 1.2 %collective-permute-done.1 = f32[16,12,256]{2,1,0:T(8,128)S(1)} collective-permute-done((f32[16,12,256]{2,1,0:T(8,128)S(1)}, f32[16,12,256]{2,1,0:T(8,128)S(1)}, u32[]{:S(2)}, u32[]{:S(2)}) %collective-permute-start.1) | collective-permute-done | bytes 196640 | tf_op jit(solution)/shard_map/ppermute | solution.py:19
  15.2 1.4 %pad_maximum_fusion.1 = f32[16,88,256]{2,1,0:T(8,128)S(1)} fusion(f32[16,12,256]{2,1,0:T(8,128)S(1)} %collective-permute-done.1, f32[16,12,256]{2,1,0:T(8,128)S(1)} %collective-permute-done, f32[16,64,256]{2,1,0:T(8,128)} %shard_map.103), kind=kLoop, calls=%fused_computation.1 | loop fusion | flops 720896 | bytes 2883584 | tf_op jit(solution)/shard_map/concatenate | solution.py:24
  16.6 0.3 fusion
  16.8 0.0 copy-start
  16.8 0.3 copy.11
  17.1 3.5 %collective-permute-start.2 = (f32[16,88,12]{1,0,2:T(8,128)S(1)}, f32[16,88,12]{1,0,2:T(8,128)S(1)}, u32[]{:S(2)}, u32[]{:S(2)}) collective-permute-start(f32[16,88,12]{1,0,2:T(8,128)S(1)} %copy.11), channel_id=1, source_target_pairs={{1,0},{2,1},{3,2},{4,3},{5,4},{6,5},{7,6},{8,7},{9,8},{10,9},{11,1... | collective-permute-start | bytes 202760 | tf_op jit(solution)/shard_map/ppermute | solution.py:22
  20.5 0.3 copy.12
  20.8 1.9 %collective-permute-start.3 = (f32[16,88,12]{1,0,2:T(8,128)S(1)}, f32[16,88,12]{1,0,2:T(8,128)S(1)}, u32[]{:S(2)}, u32[]{:S(2)}) collective-permute-start(f32[16,88,12]{1,0,2:T(8,128)S(1)} %copy.12), channel_id=1, source_target_pairs={{0,1},{1,2},{2,3},{3,4},{4,5},{5,6},{6,7},{7,8},{8,9},{9,10},{10,1... | collective-permute-start | bytes 202760 | tf_op jit(solution)/shard_map/ppermute | solution.py:19
  22.8 0.1 pad.4.clone
  22.8 0.0 collective-permute-done.2
  22.8 0.3 copy.13
  23.1 5.7 %collective-permute-done.3 = f32[16,88,12]{1,0,2:T(8,128)S(1)} collective-permute-done((f32[16,88,12]{1,0,2:T(8,128)S(1)}, f32[16,88,12]{1,0,2:T(8,128)S(1)}, u32[]{:S(2)}, u32[]{:S(2)}) %collective-permute-start.3) | collective-permute-done | bytes 67616 | tf_op jit(solution)/shard_map/ppermute | solution.py:19
  28.9 0.3 copy.14
  29.1 0.0 copy-done
  29.2 1.7 %pad_maximum_fusion.f_ref = f32[16,88,384]{2,1,0:T(8,128)} fusion(f32[16,88,12]{2,1,0:T(8,128)S(1)} %copy.14, f32[16,88,12]{2,1,0:T(8,128)S(1)} %copy.13, f32[16,12,256]{2,1,0:T(8,128)S(1)} %collective-permute-done.1, f32[16,12,256]{2,1,0:T(8,128)S(1)} %collective-permute-done, f32[16,64,256]{2,1,0:T(8,128)S(1)} %copy-done, f32[384]{0:T(512)S(1)} %pad.4.clone), kind=kLoop, calls=%fused_computation | loop fusion | flops 2703360 | bytes 3741184 | tf_op jit(solution)/shard_map/concatenate | solution.py:28
  30.8 4.3 %shard_map.104 = f32[4]{0:T(128)} custom-call(f32[16,88,384]{2,1,0:T(8,128)} %pad_maximum_fusion.f_ref), custom_call_target="tpu_custom_call" | custom-call | tf_op jit(solution)/shard_map/pallas_call | solution.py:292
  35.1 0.1 collective-permute-start.4
  35.2 1.3 %collective-permute-done.4 = f32[4]{0:T(128)S(1)} collective-permute-done((f32[4]{0:T(128)}, f32[4]{0:T(128)S(1)}, u32[]{:S(2)}, u32[]{:S(2)}) %collective-permute-start.4) | collective-permute-done | bytes 48 | tf_op jit(solution)/shard_map/ppermute | solution.py:40
  36.5 0.7 add.24
  37.2 0.0 collective-permute-start.5
  37.2 3.6 %collective-permute-done.5 = f32[4]{0:T(128)S(1)} collective-permute-done((f32[4]{0:T(128)S(1)}, f32[4]{0:T(128)S(1)}, u32[]{:S(2)}, u32[]{:S(2)}) %collective-permute-start.5) | collective-permute-done | bytes 48 | tf_op jit(solution)/shard_map/ppermute | solution.py:40
  40.8 0.0 collective-permute-start.6
  40.8 5.1 %collective-permute-done.6 = f32[4]{0:T(128)S(1)} collective-permute-done((f32[4]{0:T(128)S(1)}, f32[4]{0:T(128)S(1)}, u32[]{:S(2)}, u32[]{:S(2)}) %collective-permute-start.6) | collective-permute-done | bytes 48 | tf_op jit(solution)/shard_map/ppermute | solution.py:40
  45.8 0.4 collective-permute-start.7
  46.3 3.1 %collective-permute-done.7 = f32[4]{0:T(128)S(1)} collective-permute-done((f32[4]{0:T(128)S(1)}, f32[4]{0:T(128)S(1)}, u32[]{:S(2)}, u32[]{:S(2)}) %collective-permute-start.7) | collective-permute-done | bytes 48 | tf_op jit(solution)/shard_map/ppermute | solution.py:40
  49.4 0.9 %collective-permute-start.8 = (f32[4]{0:T(128)S(1)}, f32[4]{0:T(128)S(1)}, u32[]{:S(2)}, u32[]{:S(2)}) collective-permute-start(f32[4]{0:T(128)S(1)} %add.27), channel_id=1, source_target_pairs={{0,16},{1,17},{2,18},{3,19},{4,20},{5,21},{6,22},{7,23},{8,24},{9,... | collective-permute-start | bytes 56 | tf_op jit(solution)/shard_map/ppermute | solution.py:40
  50.3 4.1 %collective-permute-done.8 = f32[4]{0:T(128)S(1)} collective-permute-done((f32[4]{0:T(128)S(1)}, f32[4]{0:T(128)S(1)}, u32[]{:S(2)}, u32[]{:S(2)}) %collective-permute-start.8) | collective-permute-done | bytes 48 | tf_op jit(solution)/shard_map/ppermute | solution.py:40
  54.5 2.5 %collective-permute-start.9 = (f32[4]{0:T(128)S(1)}, f32[4]{0:T(128)S(1)}, u32[]{:S(2)}, u32[]{:S(2)}) collective-permute-start(f32[4]{0:T(128)S(1)} %add.28), channel_id=1, source_target_pairs={{0,32},{32,0},{64,96},{96,64},{128,160},{160,128},{192,224},{224,1... | collective-permute-start | bytes 56 | tf_op jit(solution)/shard_map/ppermute | solution.py:40
  57.0 1.5 %collective-permute-done.9 = f32[4]{0:T(128)S(1)} collective-permute-done((f32[4]{0:T(128)S(1)}, f32[4]{0:T(128)S(1)}, u32[]{:S(2)}, u32[]{:S(2)}) %collective-permute-start.9) | collective-permute-done | bytes 48 | tf_op jit(solution)/shard_map/ppermute | solution.py:40
  58.5 3.9 %collective-permute-start.10 = (f32[4]{0:T(128)S(1)}, f32[4]{0:T(128)S(1)}, u32[]{:S(2)}, u32[]{:S(2)}) collective-permute-start(f32[4]{0:T(128)S(1)} %add.29), channel_id=1, source_target_pairs={{0,64},{32,96},{64,0},{96,32},{128,192},{160,224},{192,128},{224,1... | collective-permute-start | bytes 56 | tf_op jit(solution)/shard_map/ppermute | solution.py:40
  62.4 1.5 %collective-permute-done.10 = f32[4]{0:T(128)S(1)} collective-permute-done((f32[4]{0:T(128)S(1)}, f32[4]{0:T(128)S(1)}, u32[]{:S(2)}, u32[]{:S(2)}) %collective-permute-start.10) | collective-permute-done | bytes 48 | tf_op jit(solution)/shard_map/ppermute | solution.py:40
  64.0 7.5 %collective-permute-start.11 = (f32[4]{0:T(128)S(1)}, f32[4]{0:T(128)S(1)}, u32[]{:S(2)}, u32[]{:S(2)}) collective-permute-start(f32[4]{0:T(128)S(1)} %add.30), channel_id=1, source_target_pairs={{0,128},{32,160},{64,192},{96,224},{128,0},{160,32},{192,64},{224,... | collective-permute-start | bytes 56 | tf_op jit(solution)/shard_map/ppermute | solution.py:40
  71.5 1.5 %collective-permute-done.11 = f32[4]{0:T(128)S(1)} collective-permute-done((f32[4]{0:T(128)S(1)}, f32[4]{0:T(128)S(1)}, u32[]{:S(2)}, u32[]{:S(2)}) %collective-permute-start.11) | collective-permute-done | bytes 48 | tf_op jit(solution)/shard_map/ppermute | solution.py:40
  73.0 0.6 add.31.s_ref
  73.6 7.6 %shard_map.105 = (f32[64,256]{1,0:T(8,128)}, f32[64,256]{1,0:T(8,128)}, f32[1]{0:T(128)}) custom-call(f32[4]{0:T(128)} %add.31.s_ref, f32[16,88,384]{2,1,0:T(8,128)} %pad_maximum_fusion.f_ref), custom_call_target="tpu_custom_call" | custom-call | tf_op jit(solution)/shard_map/pallas_call | solution.py:301
  (7 shorter events, 0.0 us)
Async XLA Ops:
  3.9 10.1 %collective-permute-start = (f32[16,12,256]{2,1,0:T(8,128)S(1)}, f32[16,12,256]{2,1,0:T(8,128)S(1)}, u32[]{:S(2)}, u32[]{:S(2)}) collective-permute-start(f32[16,12,256]{2,1,0:T(8,128)S(1)} %get-tuple-element.11), channel_id=1, source_target_pairs={{32,0},{64,32},{96,64},{128,96},{160,128},{192,160},{224,192},{33,... | collective-permute-start | bytes 589832 | tf_op jit(solution)/shard_map/ppermute | solution.py:22
  5.2 10.0 %collective-permute-start.1 = (f32[16,12,256]{2,1,0:T(8,128)S(1)}, f32[16,12,256]{2,1,0:T(8,128)S(1)}, u32[]{:S(2)}, u32[]{:S(2)}) collective-permute-start(f32[16,12,256]{2,1,0:T(8,128)S(1)} %get-tuple-element.12), channel_id=1, source_target_pairs={{0,32},{32,64},{64,96},{96,128},{128,160},{160,192},{192,224},{1,3... | collective-permute-start | bytes 589832 | tf_op jit(solution)/shard_map/ppermute | solution.py:19
  16.8 12.3 %copy-start = (f32[16,64,256]{2,1,0:T(8,128)S(1)}, f32[16,64,256]{2,1,0:T(8,128)}, u32[]{:S(2)}) copy-start(f32[16,64,256]{2,1,0:T(8,128)} %shard_map.103) | copy-start | bytes 3145732
  17.1 5.8 %collective-permute-start.2 = (f32[16,88,12]{1,0,2:T(8,128)S(1)}, f32[16,88,12]{1,0,2:T(8,128)S(1)}, u32[]{:S(2)}, u32[]{:S(2)}) collective-permute-start(f32[16,88,12]{1,0,2:T(8,128)S(1)} %copy.11), channel_id=1, source_target_pairs={{1,0},{2,1},{3,2},{4,3},{5,4},{6,5},{7,6},{8,7},{9,8},{10,9},{11,1... | collective-permute-start | bytes 202760 | tf_op jit(solution)/shard_map/ppermute | solution.py:22
  20.8 8.1 %collective-permute-start.3 = (f32[16,88,12]{1,0,2:T(8,128)S(1)}, f32[16,88,12]{1,0,2:T(8,128)S(1)}, u32[]{:S(2)}, u32[]{:S(2)}) collective-permute-start(f32[16,88,12]{1,0,2:T(8,128)S(1)} %copy.12), channel_id=1, source_target_pairs={{0,1},{1,2},{2,3},{3,4},{4,5},{5,6},{6,7},{7,8},{8,9},{9,10},{10,1... | collective-permute-start | bytes 202760 | tf_op jit(solution)/shard_map/ppermute | solution.py:19
  35.1 1.4 %collective-permute-start.4 = (f32[4]{0:T(128)}, f32[4]{0:T(128)S(1)}, u32[]{:S(2)}, u32[]{:S(2)}) collective-permute-start(f32[4]{0:T(128)} %shard_map.104), channel_id=1, source_target_pairs={{0,1},{1,0},{2,3},{3,2},{4,5},{5,4},{6,7},{7,6},{8,9},{9,8},{10,11... | collective-permute-start | bytes 56 | tf_op jit(solution)/shard_map/ppermute | solution.py:40
  37.2 3.6 %collective-permute-start.5 = (f32[4]{0:T(128)S(1)}, f32[4]{0:T(128)S(1)}, u32[]{:S(2)}, u32[]{:S(2)}) collective-permute-start(f32[4]{0:T(128)S(1)} %add.24), channel_id=1, source_target_pairs={{0,2},{1,3},{2,0},{3,1},{4,6},{5,7},{6,4},{7,5},{8,10},{9,11},{10,... | collective-permute-start | bytes 56 | tf_op jit(solution)/shard_map/ppermute | solution.py:40
  40.8 5.1 %collective-permute-start.6 = (f32[4]{0:T(128)S(1)}, f32[4]{0:T(128)S(1)}, u32[]{:S(2)}, u32[]{:S(2)}) collective-permute-start(f32[4]{0:T(128)S(1)} %add.25), channel_id=1, source_target_pairs={{0,4},{1,5},{2,6},{3,7},{4,0},{5,1},{6,2},{7,3},{8,12},{9,13},{10,... | collective-permute-start | bytes 56 | tf_op jit(solution)/shard_map/ppermute | solution.py:40
  45.8 3.6 %collective-permute-start.7 = (f32[4]{0:T(128)S(1)}, f32[4]{0:T(128)S(1)}, u32[]{:S(2)}, u32[]{:S(2)}) collective-permute-start(f32[4]{0:T(128)S(1)} %add.26), channel_id=1, source_target_pairs={{0,8},{1,9},{2,10},{3,11},{4,12},{5,13},{6,14},{7,15},{8,0},{9,1},... | collective-permute-start | bytes 56 | tf_op jit(solution)/shard_map/ppermute | solution.py:40
  49.4 5.1 %collective-permute-start.8 = (f32[4]{0:T(128)S(1)}, f32[4]{0:T(128)S(1)}, u32[]{:S(2)}, u32[]{:S(2)}) collective-permute-start(f32[4]{0:T(128)S(1)} %add.27), channel_id=1, source_target_pairs={{0,16},{1,17},{2,18},{3,19},{4,20},{5,21},{6,22},{7,23},{8,24},{9,... | collective-permute-start | bytes 56 | tf_op jit(solution)/shard_map/ppermute | solution.py:40
  54.5 4.0 %collective-permute-start.9 = (f32[4]{0:T(128)S(1)}, f32[4]{0:T(128)S(1)}, u32[]{:S(2)}, u32[]{:S(2)}) collective-permute-start(f32[4]{0:T(128)S(1)} %add.28), channel_id=1, source_target_pairs={{0,32},{32,0},{64,96},{96,64},{128,160},{160,128},{192,224},{224,1... | collective-permute-start | bytes 56 | tf_op jit(solution)/shard_map/ppermute | solution.py:40
  58.5 5.5 %collective-permute-start.10 = (f32[4]{0:T(128)S(1)}, f32[4]{0:T(128)S(1)}, u32[]{:S(2)}, u32[]{:S(2)}) collective-permute-start(f32[4]{0:T(128)S(1)} %add.29), channel_id=1, source_target_pairs={{0,64},{32,96},{64,0},{96,32},{128,192},{160,224},{192,128},{224,1... | collective-permute-start | bytes 56 | tf_op jit(solution)/shard_map/ppermute | solution.py:40
  64.0 9.1 %collective-permute-start.11 = (f32[4]{0:T(128)S(1)}, f32[4]{0:T(128)S(1)}, u32[]{:S(2)}, u32[]{:S(2)}) collective-permute-start(f32[4]{0:T(128)S(1)} %add.30), channel_id=1, source_target_pairs={{0,128},{32,160},{64,192},{96,224},{128,0},{160,32},{192,64},{224,... | collective-permute-start | bytes 56 | tf_op jit(solution)/shard_map/ppermute | solution.py:40

commit v6 on v5

--- a/solution.py
+++ b/solution.py
@@ -10,16 +10,20 @@
 LANES = 128
 
 
-def wrapped_patch(block, width):
+def wrapped_patch(block, width, first_rows, last_rows):
     pieces = {}
     for axis, dim in (("gy", 1), ("gx", 2)):
         count = lax.axis_size(axis)
         forward = [(i, i + 1) for i in range(count - 1)]
         backward = [(target, source) for source, target in forward]
-        before = lax.ppermute(
-            lax.slice_in_dim(block, block.shape[dim] - width, None, axis=dim), axis, forward
-        )
-        after = lax.ppermute(lax.slice_in_dim(block, 0, width, axis=dim), axis, backward)
+        if dim == 1:
+            before = lax.ppermute(last_rows, axis, forward)
+            after = lax.ppermute(first_rows, axis, backward)
+        else:
+            before = lax.ppermute(
+                lax.slice_in_dim(block, block.shape[dim] - width, None, axis=dim), axis, forward
+            )
+            after = lax.ppermute(lax.slice_in_dim(block, 0, width, axis=dim), axis, backward)
         if dim == 1:
             block = jnp.concatenate([block, after, before], axis=dim)
         else:
@@ -261,7 +265,7 @@
 
 
 def pack_kernel(steps):
-    def kernel(thick_ref, vel_ref, slope_ref, beta_ref, mask_ref, flags_ref, obs_ref, adj_ref, o_ref):
+    def kernel(thick_ref, vel_ref, slope_ref, beta_ref, mask_ref, flags_ref, obs_ref, adj_ref, o_ref, top_ref, bottom_ref):
         f32 = jnp.float32
         o_ref[0] = mask_ref[...].astype(f32)
         o_ref[1] = flags_ref[...].astype(f32)
@@ -274,17 +278,25 @@
                 o_ref[5 + steps + 2 * n + c] = vel_ref[n, c].astype(f32)
                 o_ref[5 + 3 * steps + 2 * n + c] = obs_ref[n, c].astype(f32)
         o_ref[5 + 5 * steps] = adj_ref[...]
+        width = top_ref.shape[1]
+        top_ref[...] = o_ref[:, :width, :]
+        bottom_ref[...] = o_ref[:, o_ref.shape[1] - width :, :]
 
     return kernel
 
 
-def run_pack(*arrays):
+def run_pack(width, *arrays):
     steps, rows, cols = arrays[0].shape
+    fields = 6 + 5 * steps
     return pl.pallas_call(
         pack_kernel(steps),
-        out_shape=jax.ShapeDtypeStruct((6 + 5 * steps, rows, cols), jnp.float32),
+        out_shape=(
+            jax.ShapeDtypeStruct((fields, rows, cols), jnp.float32),
+            jax.ShapeDtypeStruct((fields, width, cols), jnp.float32),
+            jax.ShapeDtypeStruct((fields, width, cols), jnp.float32),
+        ),
         in_specs=[pl.BlockSpec(memory_space=pltpu.VMEM)] * len(arrays),
-        out_specs=pl.BlockSpec(memory_space=pltpu.VMEM),
+        out_specs=(pl.BlockSpec(memory_space=pltpu.VMEM),) * 3,
     )(*arrays)
 
 
@@ -320,7 +332,8 @@
     steps = saved_thickness.shape[0]
     rows, cols = basal_beta.shape
     f32 = jnp.float32
-    fields = run_pack(
+    fields, first_rows, last_rows = run_pack(
+        HALO,
         saved_thickness,
         saved_velocity,
         surface_slope,
@@ -330,7 +343,7 @@
         observed_velocity,
         thickness_adjoint,
     )
-    wide = wrapped_patch(fields, HALO)
+    wide = wrapped_patch(fields, HALO, first_rows, last_rows)
     local_sums = run_forward(wide, steps, rows, cols)
     totals = butterfly_sum(local_sums, ("gx", "gy"))
     cell_count = rows * cols * lax.axis_size("gy") * lax.axis_size("gx")

time: 81.8 us -> 81 us (level)
  local copies, waits for them, and re-layouts: 2.48 us -> 1.41 us
    ppermute x0 -> x2, starting transfers between devices: none -> 5.84 us  [the longest x1 4.56 us: wrapped_patch(): before = lax.ppermute(last_rows, axis, forward)]
    ppermute x0 -> x2, waiting for transfers between devices: none -> 5.75 us  [the longest x1 4.46 us: wrapped_patch(): after = lax.ppermute(first_rows, axis, backward)]
    ppermute x2 -> x1, starting transfers between devices: 6.49 us -> 1.93 us  [wrapped_patch(): lax.ppermute(lax.slice_in_dim(block, block.shape[dim] - width, None, axis...]
    ppermute x2 -> x1, waiting for transfers between devices: 4.26 us -> 0.01 us  [wrapped_patch(): lax.ppermute(lax.slice_in_dim(block, 0, width, axis=dim), axis, backward)]
    ppermute x2 -> x1, starting transfers between devices: 4.76 us -> 3.47 us  [wrapped_patch(): lax.ppermute(lax.slice_in_dim(block, 0, width, axis=dim), axis, backward)]
    ppermute x2 -> x1, waiting for transfers between devices: 6.92 us -> 5.74 us  [wrapped_patch(): lax.ppermute(lax.slice_in_dim(block, block.shape[dim] - width, None, axis...]
    slice x3 -> x2, local copies, waits for them, and re-layouts: 1.57 us -> 0.5 us  [wrapped_patch(): lax.slice_in_dim(block, 0, width, axis=dim)]
where the time goes in v6:
time: 81 us; the launch traced here: 80.7 us
  waiting for transfers between devices  33.3 us (41%)
  starting transfers between devices  26.5 us (33%)
  Pallas kernels  14.3 us (18%)
  other arithmetic  4.31 us (5%)
  local copies, waits for them, and re-layouts  1.41 us (2%)
  between operations  0.9 us (1%)
    ppermute x8, waiting for transfers between devices, butterfly_sum(): lax.ppermute(values, axis, [(i, i ^ stride) for i in range(count)])  21.8 us
    ppermute x8, starting transfers between devices, butterfly_sum(): lax.ppermute(values, axis, [(i, i ^ stride) for i in range(count)])  15.3 us
    pallas_call x1, Pallas kernels, run_backward(): pl.pallas_call(backward_kernel(steps, rows, cols, cell_count), out_shape=...  7.63 us
    ppermute x1, waiting for transfers between devices, wrapped_patch(): lax.ppermute(lax.slice_in_dim(block, block.shape[dim] - width, None, axis...  5.74 us
    ppermute x1, starting transfers between devices, wrapped_patch(): before = lax.ppermute(last_rows, axis, forward)  4.56 us
    ppermute x1, waiting for transfers between devices, wrapped_patch(): after = lax.ppermute(first_rows, axis, backward)  4.46 us
    pallas_call x1, Pallas kernels, run_forward(): pl.pallas_call(forward_kernel(steps, rows, cols), out_shape=jax.ShapeDtyp...  4.29 us
    ppermute x1, starting transfers between devices, wrapped_patch(): lax.ppermute(lax.slice_in_dim(block, 0, width, axis=dim), axis, backward)  3.47 us
  transfers between devices with their start and end apart: 12, of which 11 were waited for; matrix products, arithmetic and copies ran while one was open for 1% of the time, Pallas kernels for 0%

profile of v6, /device:TPU:24, one launch (start us, length us, event | category | flops | bytes accessed | tf_op | source)
XLA Modules:
  0.0 80.7 jit_solution(11313770593756513315)
XLA Ops:
  0.6 2.3 %shard_map.103 = (f32[16,64,256]{2,1,0:T(8,128)}, f32[16,12,256]{2,1,0:T(8,128)}, f32[16,12,256]{2,1,0:T(8,128)}) custom-call(bf16[2,64,256]{2,1,0:T(8,128)(2,1)} %thick_ref.1, bf16[2,2,64,256]{3,2,1,0:T(8,128)(2,1)} %vel_ref.1, bf16[2,64,256]{2,1,0:T(8,128)(2,1)} %slope_ref.1, f32[64,256]{1,0:T(8,128)} %beta_ref.1, s32[64,256]{1,0:T(8,128)} %mask_ref.1, ...), custom_call_target="tpu_custom_call" | custom-call | tf_op jit(solution)/shard_map/pallas_call | solution.py:291
  3.0 1.3 %collective-permute-start = (f32[16,12,256]{2,1,0:T(8,128)}, f32[16,12,256]{2,1,0:T(8,128)S(1)}, u32[]{:S(2)}, u32[]{:S(2)}) collective-permute-start(f32[16,12,256]{2,1,0:T(8,128)} %get-tuple-element.10), channel_id=1, source_target_pairs={{32,0},{64,32},{96,64},{128,96},{160,128},{192,160},{224,192},{33,... | collective-permute-start | bytes 589832 | tf_op jit(solution)/shard_map/ppermute | solution.py:21
  4.3 4.6 %collective-permute-start.1 = (f32[16,12,256]{2,1,0:T(8,128)}, f32[16,12,256]{2,1,0:T(8,128)S(1)}, u32[]{:S(2)}, u32[]{:S(2)}) collective-permute-start(f32[16,12,256]{2,1,0:T(8,128)} %get-tuple-element.11), channel_id=1, source_target_pairs={{0,32},{32,64},{64,96},{96,128},{128,160},{160,192},{192,224},{1,3... | collective-permute-start | bytes 589832 | tf_op jit(solution)/shard_map/ppermute | solution.py:20
  8.8 4.5 %collective-permute-done = f32[16,12,256]{2,1,0:T(8,128)S(1)} collective-permute-done((f32[16,12,256]{2,1,0:T(8,128)}, f32[16,12,256]{2,1,0:T(8,128)S(1)}, u32[]{:S(2)}, u32[]{:S(2)}) %collective-permute-start) | collective-permute-done | bytes 196640 | tf_op jit(solution)/shard_map/ppermute | solution.py:21
  13.3 1.3 %collective-permute-done.1 = f32[16,12,256]{2,1,0:T(8,128)S(1)} collective-permute-done((f32[16,12,256]{2,1,0:T(8,128)}, f32[16,12,256]{2,1,0:T(8,128)S(1)}, u32[]{:S(2)}, u32[]{:S(2)}) %collective-permute-start.1) | collective-permute-done | bytes 196640 | tf_op jit(solution)/shard_map/ppermute | solution.py:20
  14.6 1.4 %pad_maximum_fusion.1 = f32[16,88,256]{2,1,0:T(8,128)S(1)} fusion(f32[16,12,256]{2,1,0:T(8,128)S(1)} %collective-permute-done.1, f32[16,12,256]{2,1,0:T(8,128)S(1)} %collective-permute-done, f32[16,64,256]{2,1,0:T(8,128)} %get-tuple-element.9), kind=kLoop, calls=%fused_computation.1 | loop fusion | flops 720896 | bytes 2883584 | tf_op jit(solution)/shard_map/concatenate | solution.py:28
  15.9 0.3 fusion
  16.2 0.0 copy-start
  16.2 0.3 copy.11
  16.5 3.5 %collective-permute-start.2 = (f32[16,88,12]{1,0,2:T(8,128)S(1)}, f32[16,88,12]{1,0,2:T(8,128)S(1)}, u32[]{:S(2)}, u32[]{:S(2)}) collective-permute-start(f32[16,88,12]{1,0,2:T(8,128)S(1)} %copy.11), channel_id=1, source_target_pairs={{1,0},{2,1},{3,2},{4,3},{5,4},{6,5},{7,6},{8,7},{9,8},{10,9},{11,1... | collective-permute-start | bytes 202760 | tf_op jit(solution)/shard_map/ppermute | solution.py:26
  19.9 0.3 copy.12
  20.2 1.9 %collective-permute-start.3 = (f32[16,88,12]{1,0,2:T(8,128)S(1)}, f32[16,88,12]{1,0,2:T(8,128)S(1)}, u32[]{:S(2)}, u32[]{:S(2)}) collective-permute-start(f32[16,88,12]{1,0,2:T(8,128)S(1)} %copy.12), channel_id=1, source_target_pairs={{0,1},{1,2},{2,3},{3,4},{4,5},{5,6},{6,7},{7,8},{8,9},{9,10},{10,1... | collective-permute-start | bytes 202760 | tf_op jit(solution)/shard_map/ppermute | solution.py:23
  22.1 0.1 pad.4.clone
  22.2 0.0 collective-permute-done.2
  22.2 0.3 copy.13
  22.5 5.7 %collective-permute-done.3 = f32[16,88,12]{1,0,2:T(8,128)S(1)} collective-permute-done((f32[16,88,12]{1,0,2:T(8,128)S(1)}, f32[16,88,12]{1,0,2:T(8,128)S(1)}, u32[]{:S(2)}, u32[]{:S(2)}) %collective-permute-start.3) | collective-permute-done | bytes 67616 | tf_op jit(solution)/shard_map/ppermute | solution.py:23
  28.2 0.3 copy.14
  28.5 0.0 copy-done
  28.5 1.7 %pad_maximum_fusion.f_ref = f32[16,88,384]{2,1,0:T(8,128)} fusion(f32[16,88,12]{2,1,0:T(8,128)S(1)} %copy.14, f32[16,88,12]{2,1,0:T(8,128)S(1)} %copy.13, f32[16,12,256]{2,1,0:T(8,128)S(1)} %collective-permute-done.1, f32[16,12,256]{2,1,0:T(8,128)S(1)} %collective-permute-done, f32[16,64,256]{2,1,0:T(8,128)S(1)} %copy-done, f32[384]{0:T(512)S(1)} %pad.4.clone), kind=kLoop, calls=%fused_computation | loop fusion | flops 2703360 | bytes 3741184 | tf_op jit(solution)/shard_map/concatenate | solution.py:32
  30.2 4.3 %shard_map.104 = f32[4]{0:T(128)} custom-call(f32[16,88,384]{2,1,0:T(8,128)} %pad_maximum_fusion.f_ref), custom_call_target="tpu_custom_call" | custom-call | tf_op jit(solution)/shard_map/pallas_call | solution.py:304
  34.5 0.1 collective-permute-start.4
  34.6 1.3 %collective-permute-done.4 = f32[4]{0:T(128)S(1)} collective-permute-done((f32[4]{0:T(128)}, f32[4]{0:T(128)S(1)}, u32[]{:S(2)}, u32[]{:S(2)}) %collective-permute-start.4) | collective-permute-done | bytes 48 | tf_op jit(solution)/shard_map/ppermute | solution.py:44
  35.9 0.7 add.24
  36.6 0.0 collective-permute-start.5
  36.6 3.6 %collective-permute-done.5 = f32[4]{0:T(128)S(1)} collective-permute-done((f32[4]{0:T(128)S(1)}, f32[4]{0:T(128)S(1)}, u32[]{:S(2)}, u32[]{:S(2)}) %collective-permute-start.5) | collective-permute-done | bytes 48 | tf_op jit(solution)/shard_map/ppermute | solution.py:44
  40.1 0.0 collective-permute-start.6
  40.1 5.1 %collective-permute-done.6 = f32[4]{0:T(128)S(1)} collective-permute-done((f32[4]{0:T(128)S(1)}, f32[4]{0:T(128)S(1)}, u32[]{:S(2)}, u32[]{:S(2)}) %collective-permute-start.6) | collective-permute-done | bytes 48 | tf_op jit(solution)/shard_map/ppermute | solution.py:44
  45.2 0.4 collective-permute-start.7
  45.7 3.1 %collective-permute-done.7 = f32[4]{0:T(128)S(1)} collective-permute-done((f32[4]{0:T(128)S(1)}, f32[4]{0:T(128)S(1)}, u32[]{:S(2)}, u32[]{:S(2)}) %collective-permute-start.7) | collective-permute-done | bytes 48 | tf_op jit(solution)/shard_map/ppermute | solution.py:44
  48.8 0.9 %collective-permute-start.8 = (f32[4]{0:T(128)S(1)}, f32[4]{0:T(128)S(1)}, u32[]{:S(2)}, u32[]{:S(2)}) collective-permute-start(f32[4]{0:T(128)S(1)} %add.27), channel_id=1, source_target_pairs={{0,16},{1,17},{2,18},{3,19},{4,20},{5,21},{6,22},{7,23},{8,24},{9,... | collective-permute-start | bytes 56 | tf_op jit(solution)/shard_map/ppermute | solution.py:44
  49.7 4.1 %collective-permute-done.8 = f32[4]{0:T(128)S(1)} collective-permute-done((f32[4]{0:T(128)S(1)}, f32[4]{0:T(128)S(1)}, u32[]{:S(2)}, u32[]{:S(2)}) %collective-permute-start.8) | collective-permute-done | bytes 48 | tf_op jit(solution)/shard_map/ppermute | solution.py:44
  53.9 2.4 %collective-permute-start.9 = (f32[4]{0:T(128)S(1)}, f32[4]{0:T(128)S(1)}, u32[]{:S(2)}, u32[]{:S(2)}) collective-permute-start(f32[4]{0:T(128)S(1)} %add.28), channel_id=1, source_target_pairs={{0,32},{32,0},{64,96},{96,64},{128,160},{160,128},{192,224},{224,1... | collective-permute-start | bytes 56 | tf_op jit(solution)/shard_map/ppermute | solution.py:44
  56.2 1.5 %collective-permute-done.9 = f32[4]{0:T(128)S(1)} collective-permute-done((f32[4]{0:T(128)S(1)}, f32[4]{0:T(128)S(1)}, u32[]{:S(2)}, u32[]{:S(2)}) %collective-permute-start.9) | collective-permute-done | bytes 48 | tf_op jit(solution)/shard_map/ppermute | solution.py:44
  57.8 4.0 %collective-permute-start.10 = (f32[4]{0:T(128)S(1)}, f32[4]{0:T(128)S(1)}, u32[]{:S(2)}, u32[]{:S(2)}) collective-permute-start(f32[4]{0:T(128)S(1)} %add.29), channel_id=1, source_target_pairs={{0,64},{32,96},{64,0},{96,32},{128,192},{160,224},{192,128},{224,1... | collective-permute-start | bytes 56 | tf_op jit(solution)/shard_map/ppermute | solution.py:44
  61.8 1.5 %collective-permute-done.10 = f32[4]{0:T(128)S(1)} collective-permute-done((f32[4]{0:T(128)S(1)}, f32[4]{0:T(128)S(1)}, u32[]{:S(2)}, u32[]{:S(2)}) %collective-permute-start.10) | collective-permute-done | bytes 48 | tf_op jit(solution)/shard_map/ppermute | solution.py:44
  63.4 7.4 %collective-permute-start.11 = (f32[4]{0:T(128)S(1)}, f32[4]{0:T(128)S(1)}, u32[]{:S(2)}, u32[]{:S(2)}) collective-permute-start(f32[4]{0:T(128)S(1)} %add.30), channel_id=1, source_target_pairs={{0,128},{32,160},{64,192},{96,224},{128,0},{160,32},{192,64},{224,... | collective-permute-start | bytes 56 | tf_op jit(solution)/shard_map/ppermute | solution.py:44
  70.8 1.5 %collective-permute-done.11 = f32[4]{0:T(128)S(1)} collective-permute-done((f32[4]{0:T(128)S(1)}, f32[4]{0:T(128)S(1)}, u32[]{:S(2)}, u32[]{:S(2)}) %collective-permute-start.11) | collective-permute-done | bytes 48 | tf_op jit(solution)/shard_map/ppermute | solution.py:44
  72.3 0.6 add.31.s_ref
  72.9 7.6 %shard_map.105 = (f32[64,256]{1,0:T(8,128)}, f32[64,256]{1,0:T(8,128)}, f32[1]{0:T(128)}) custom-call(f32[4]{0:T(128)} %add.31.s_ref, f32[16,88,384]{2,1,0:T(8,128)} %pad_maximum_fusion.f_ref), custom_call_target="tpu_custom_call" | custom-call | tf_op jit(solution)/shard_map/pallas_call | solution.py:313
  (7 shorter events, 0.0 us)
Async XLA Ops:
  3.0 10.3 %collective-permute-start = (f32[16,12,256]{2,1,0:T(8,128)}, f32[16,12,256]{2,1,0:T(8,128)S(1)}, u32[]{:S(2)}, u32[]{:S(2)}) collective-permute-start(f32[16,12,256]{2,1,0:T(8,128)} %get-tuple-element.10), channel_id=1, source_target_pairs={{32,0},{64,32},{96,64},{128,96},{160,128},{192,160},{224,192},{33,... | collective-permute-start | bytes 589832 | tf_op jit(solution)/shard_map/ppermute | solution.py:21
  4.3 10.3 %collective-permute-start.1 = (f32[16,12,256]{2,1,0:T(8,128)}, f32[16,12,256]{2,1,0:T(8,128)S(1)}, u32[]{:S(2)}, u32[]{:S(2)}) collective-permute-start(f32[16,12,256]{2,1,0:T(8,128)} %get-tuple-element.11), channel_id=1, source_target_pairs={{0,32},{32,64},{64,96},{96,128},{128,160},{160,192},{192,224},{1,3... | collective-permute-start | bytes 589832 | tf_op jit(solution)/shard_map/ppermute | solution.py:20
  16.2 12.3 %copy-start = (f32[16,64,256]{2,1,0:T(8,128)S(1)}, f32[16,64,256]{2,1,0:T(8,128)}, u32[]{:S(2)}) copy-start(f32[16,64,256]{2,1,0:T(8,128)} %get-tuple-element.9) | copy-start | bytes 3145732
  16.5 5.8 %collective-permute-start.2 = (f32[16,88,12]{1,0,2:T(8,128)S(1)}, f32[16,88,12]{1,0,2:T(8,128)S(1)}, u32[]{:S(2)}, u32[]{:S(2)}) collective-permute-start(f32[16,88,12]{1,0,2:T(8,128)S(1)} %copy.11), channel_id=1, source_target_pairs={{1,0},{2,1},{3,2},{4,3},{5,4},{6,5},{7,6},{8,7},{9,8},{10,9},{11,1... | collective-permute-start | bytes 202760 | tf_op jit(solution)/shard_map/ppermute | solution.py:26
  20.2 8.1 %collective-permute-start.3 = (f32[16,88,12]{1,0,2:T(8,128)S(1)}, f32[16,88,12]{1,0,2:T(8,128)S(1)}, u32[]{:S(2)}, u32[]{:S(2)}) collective-permute-start(f32[16,88,12]{1,0,2:T(8,128)S(1)} %copy.12), channel_id=1, source_target_pairs={{0,1},{1,2},{2,3},{3,4},{4,5},{5,6},{6,7},{7,8},{8,9},{9,10},{10,1... | collective-permute-start | bytes 202760 | tf_op jit(solution)/shard_map/ppermute | solution.py:23
  34.5 1.4 %collective-permute-start.4 = (f32[4]{0:T(128)}, f32[4]{0:T(128)S(1)}, u32[]{:S(2)}, u32[]{:S(2)}) collective-permute-start(f32[4]{0:T(128)} %shard_map.104), channel_id=1, source_target_pairs={{0,1},{1,0},{2,3},{3,2},{4,5},{5,4},{6,7},{7,6},{8,9},{9,8},{10,11... | collective-permute-start | bytes 56 | tf_op jit(solution)/shard_map/ppermute | solution.py:44
  36.6 3.6 %collective-permute-start.5 = (f32[4]{0:T(128)S(1)}, f32[4]{0:T(128)S(1)}, u32[]{:S(2)}, u32[]{:S(2)}) collective-permute-start(f32[4]{0:T(128)S(1)} %add.24), channel_id=1, source_target_pairs={{0,2},{1,3},{2,0},{3,1},{4,6},{5,7},{6,4},{7,5},{8,10},{9,11},{10,... | collective-permute-start | bytes 56 | tf_op jit(solution)/shard_map/ppermute | solution.py:44
  40.1 5.1 %collective-permute-start.6 = (f32[4]{0:T(128)S(1)}, f32[4]{0:T(128)S(1)}, u32[]{:S(2)}, u32[]{:S(2)}) collective-permute-start(f32[4]{0:T(128)S(1)} %add.25), channel_id=1, source_target_pairs={{0,4},{1,5},{2,6},{3,7},{4,0},{5,1},{6,2},{7,3},{8,12},{9,13},{10,... | collective-permute-start | bytes 56 | tf_op jit(solution)/shard_map/ppermute | solution.py:44
  45.2 3.6 %collective-permute-start.7 = (f32[4]{0:T(128)S(1)}, f32[4]{0:T(128)S(1)}, u32[]{:S(2)}, u32[]{:S(2)}) collective-permute-start(f32[4]{0:T(128)S(1)} %add.26), channel_id=1, source_target_pairs={{0,8},{1,9},{2,10},{3,11},{4,12},{5,13},{6,14},{7,15},{8,0},{9,1},... | collective-permute-start | bytes 56 | tf_op jit(solution)/shard_map/ppermute | solution.py:44
  48.8 5.1 %collective-permute-start.8 = (f32[4]{0:T(128)S(1)}, f32[4]{0:T(128)S(1)}, u32[]{:S(2)}, u32[]{:S(2)}) collective-permute-start(f32[4]{0:T(128)S(1)} %add.27), channel_id=1, source_target_pairs={{0,16},{1,17},{2,18},{3,19},{4,20},{5,21},{6,22},{7,23},{8,24},{9,... | collective-permute-start | bytes 56 | tf_op jit(solution)/shard_map/ppermute | solution.py:44
  53.9 3.9 %collective-permute-start.9 = (f32[4]{0:T(128)S(1)}, f32[4]{0:T(128)S(1)}, u32[]{:S(2)}, u32[]{:S(2)}) collective-permute-start(f32[4]{0:T(128)S(1)} %add.28), channel_id=1, source_target_pairs={{0,32},{32,0},{64,96},{96,64},{128,160},{160,128},{192,224},{224,1... | collective-permute-start | bytes 56 | tf_op jit(solution)/shard_map/ppermute | solution.py:44
  57.8 5.6 %collective-permute-start.10 = (f32[4]{0:T(128)S(1)}, f32[4]{0:T(128)S(1)}, u32[]{:S(2)}, u32[]{:S(2)}) collective-permute-start(f32[4]{0:T(128)S(1)} %add.29), channel_id=1, source_target_pairs={{0,64},{32,96},{64,0},{96,32},{128,192},{160,224},{192,128},{224,1... | collective-permute-start | bytes 56 | tf_op jit(solution)/shard_map/ppermute | solution.py:44
  63.4 9.0 %collective-permute-start.11 = (f32[4]{0:T(128)S(1)}, f32[4]{0:T(128)S(1)}, u32[]{:S(2)}, u32[]{:S(2)}) collective-permute-start(f32[4]{0:T(128)S(1)} %add.30), channel_id=1, source_target_pairs={{0,128},{32,160},{64,192},{96,224},{128,0},{160,32},{192,64},{224,... | collective-permute-start | bytes 56 | tf_op jit(solution)/shard_map/ppermute | solution.py:44

commit v7 on v6

--- a/solution.py
+++ b/solution.py
@@ -43,6 +43,27 @@
         while stride < count:
             values = values + lax.ppermute(values, axis, [(i, i ^ stride) for i in range(count)])
             stride *= 2
+    return values
+
+
+def radix_sum(values, axis, radices):
+    count = lax.axis_size(axis)
+    stride = 1
+    for radix in radices:
+        digit = (lax.axis_index(axis) // stride) % radix
+        received = [values]
+        for shift in range(1, radix):
+            pairs = []
+            for i in range(count):
+                own = (i // stride) % radix
+                pairs.append((i + (((own + shift) % radix) - own) * stride, i))
+            received.append(lax.ppermute(values, axis, pairs))
+        stacked = jnp.stack(received)
+        ordered = stacked[(jnp.arange(radix) - digit) % radix]
+        values = ordered[0]
+        for k in range(1, radix):
+            values = values + ordered[k]
+        stride *= radix
     return values
 
 
@@ -345,7 +366,10 @@
     )
     wide = wrapped_patch(fields, HALO, first_rows, last_rows)
     local_sums = run_forward(wide, steps, rows, cols)
-    totals = butterfly_sum(local_sums, ("gx", "gy"))
+    if lax.axis_size("gx") == 32 and lax.axis_size("gy") == 8:
+        totals = radix_sum(radix_sum(local_sums, "gx", (2, 4, 4)), "gy", (2, 4))
+    else:
+        totals = butterfly_sum(local_sums, ("gx", "gy"))
     cell_count = rows * cols * lax.axis_size("gy") * lax.axis_size("gx")
     beta_gradient, thickness_gradient, misfit = run_backward(totals, wide, steps, rows, cols, cell_count)
     return (beta_gradient, thickness_gradient, misfit.reshape(()))

time: 81 us -> 82.2 us (1.015)
  waiting for transfers between devices: 33.3 us -> 21.8 us
  starting transfers between devices: 26.5 us -> 36 us
  local copies, waits for them, and re-layouts: 1.41 us -> 4.2 us
    ppermute x8 -> x11, waiting for transfers between devices: 21.8 us -> 11.5 us  [radix_sum(): received.append(lax.ppermute(values, axis, pairs))]
    ppermute x8 -> x11, starting transfers between devices: 15.3 us -> 23.1 us  [radix_sum(): received.append(lax.ppermute(values, axis, pairs))]
    ppermute x1, waiting for transfers between devices: 5.74 us -> 0.08 us  [wrapped_patch(): lax.ppermute(lax.slice_in_dim(block, block.shape[dim] - width, None, axis...]
    ppermute x1, waiting for transfers between devices: 1.29 us -> 4.22 us  [wrapped_patch(): before = lax.ppermute(last_rows, axis, forward)]
    gather x0 -> x5, local copies, waits for them, and re-layouts: none -> 2.79 us  [radix_sum(): ordered = stacked[(jnp.arange(radix) - digit) % radix]]
    ppermute x1, starting transfers between devices: 3.47 us -> 5.76 us  [wrapped_patch(): lax.ppermute(lax.slice_in_dim(block, 0, width, axis=dim), axis, backward)]
    ppermute x1, waiting for transfers between devices: 0.01 us -> 1.81 us  [wrapped_patch(): lax.ppermute(lax.slice_in_dim(block, 0, width, axis=dim), axis, backward)]
  transfers between devices with their start and end apart: 12 -> 15, of which waited for: 11 -> 12; matrix products, arithmetic and copies ran while one was open for 1% -> 1% of each run, Pallas kernels for 0% -> 0%
where the time goes in v7:
time: 82.2 us; the launch traced here: 81.7 us
  starting transfers between devices  36 us (44%)
  waiting for transfers between devices  21.8 us (27%)
  Pallas kernels  14.2 us (17%)
  other arithmetic  4.42 us (5%)
  local copies, waits for them, and re-layouts  4.2 us (5%)
  between operations  1.09 us (1%)
    ppermute x11, starting transfers between devices, radix_sum(): received.append(lax.ppermute(values, axis, pairs))  23.1 us
    ppermute x11, waiting for transfers between devices, radix_sum(): received.append(lax.ppermute(values, axis, pairs))  11.5 us
    pallas_call x1, Pallas kernels, run_backward(): pl.pallas_call(backward_kernel(steps, rows, cols, cell_count), out_shape=...  7.63 us
    ppermute x1, starting transfers between devices, wrapped_patch(): lax.ppermute(lax.slice_in_dim(block, 0, width, axis=dim), axis, backward)  5.76 us
    pallas_call x1, Pallas kernels, run_forward(): pl.pallas_call(forward_kernel(steps, rows, cols), out_shape=jax.ShapeDtyp...  4.29 us
    ppermute x1, waiting for transfers between devices, wrapped_patch(): before = lax.ppermute(last_rows, axis, forward)  4.22 us
    ppermute x1, waiting for transfers between devices, wrapped_patch(): after = lax.ppermute(first_rows, axis, backward)  4.19 us
    ppermute x1, starting transfers between devices, wrapped_patch(): before = lax.ppermute(last_rows, axis, forward)  3.82 us
  transfers between devices with their start and end apart: 15, of which 12 were waited for; matrix products, arithmetic and copies ran while one was open for 1% of the time, Pallas kernels for 0%

profile of v7, /device:TPU:24, one launch (start us, length us, event | category | flops | bytes accessed | tf_op | source)
XLA Modules:
  0.0 81.7 jit_solution(11921566260914035354)
XLA Ops:
  0.6 2.3 %shard_map.103 = (f32[16,64,256]{2,1,0:T(8,128)}, f32[16,12,256]{2,1,0:T(8,128)}, f32[16,12,256]{2,1,0:T(8,128)}) custom-call(bf16[2,64,256]{2,1,0:T(8,128)(2,1)} %thick_ref.1, bf16[2,2,64,256]{3,2,1,0:T(8,128)(2,1)} %vel_ref.1, bf16[2,64,256]{2,1,0:T(8,128)(2,1)} %slope_ref.1, f32[64,256]{1,0:T(8,128)} %beta_ref.1, s32[64,256]{1,0:T(8,128)} %mask_ref.1, ...), custom_call_target="tpu_custom_call" | custom-call | tf_op jit(solution)/shard_map/pallas_call | solution.py:312
  3.0 3.8 %collective-permute-start.1 = (f32[16,12,256]{2,1,0:T(8,128)}, f32[16,12,256]{2,1,0:T(8,128)S(1)}, u32[]{:S(2)}, u32[]{:S(2)}) collective-permute-start(f32[16,12,256]{2,1,0:T(8,128)} %get-tuple-element.11), channel_id=1, source_target_pairs={{0,32},{32,64},{64,96},{96,128},{128,160},{160,192},{192,224},{1,3... | collective-permute-start | bytes 589832 | tf_op jit(solution)/shard_map/ppermute | solution.py:20
  6.8 1.3 %collective-permute-start = (f32[16,12,256]{2,1,0:T(8,128)}, f32[16,12,256]{2,1,0:T(8,128)S(1)}, u32[]{:S(2)}, u32[]{:S(2)}) collective-permute-start(f32[16,12,256]{2,1,0:T(8,128)} %get-tuple-element.10), channel_id=1, source_target_pairs={{32,0},{64,32},{96,64},{128,96},{160,128},{192,160},{224,192},{33,... | collective-permute-start | bytes 589832 | tf_op jit(solution)/shard_map/ppermute | solution.py:21
  8.3 0.1 pad.20.clone
  8.4 4.2 %collective-permute-done.1 = f32[16,12,256]{2,1,0:T(8,128)S(1)} collective-permute-done((f32[16,12,256]{2,1,0:T(8,128)}, f32[16,12,256]{2,1,0:T(8,128)S(1)}, u32[]{:S(2)}, u32[]{:S(2)}) %collective-permute-start.1) | collective-permute-done | bytes 196640 | tf_op jit(solution)/shard_map/ppermute | solution.py:20
  12.6 4.2 %collective-permute-done = f32[16,12,256]{2,1,0:T(8,128)S(1)} collective-permute-done((f32[16,12,256]{2,1,0:T(8,128)}, f32[16,12,256]{2,1,0:T(8,128)S(1)}, u32[]{:S(2)}, u32[]{:S(2)}) %collective-permute-start) | collective-permute-done | bytes 196640 | tf_op jit(solution)/shard_map/ppermute | solution.py:21
  16.8 1.4 %pad_maximum_fusion.1 = f32[16,88,256]{2,1,0:T(8,128)S(1)} fusion(f32[16,12,256]{2,1,0:T(8,128)S(1)} %collective-permute-done.1, f32[16,12,256]{2,1,0:T(8,128)S(1)} %collective-permute-done, f32[16,64,256]{2,1,0:T(8,128)} %get-tuple-element.9), kind=kLoop, calls=%fused_computation.6 | loop fusion | flops 720896 | bytes 2883584 | tf_op jit(solution)/shard_map/concatenate | solution.py:28
  18.2 0.3 fusion.10
  18.4 0.0 copy-start
  18.5 0.3 copy.12
  18.7 2.1 %collective-permute-start.3 = (f32[16,88,12]{1,0,2:T(8,128)S(1)}, f32[16,88,12]{1,0,2:T(8,128)S(1)}, u32[]{:S(2)}, u32[]{:S(2)}) collective-permute-start(f32[16,88,12]{1,0,2:T(8,128)S(1)} %copy.12), channel_id=1, source_target_pairs={{0,1},{1,2},{2,3},{3,4},{4,5},{5,6},{6,7},{7,8},{8,9},{9,10},{10,1... | collective-permute-start | bytes 202760 | tf_op jit(solution)/shard_map/ppermute | solution.py:23
  20.8 0.3 copy.11
  21.0 5.8 %collective-permute-start.2 = (f32[16,88,12]{1,0,2:T(8,128)S(1)}, f32[16,88,12]{1,0,2:T(8,128)S(1)}, u32[]{:S(2)}, u32[]{:S(2)}) collective-permute-start(f32[16,88,12]{1,0,2:T(8,128)S(1)} %copy.11), channel_id=1, source_target_pairs={{1,0},{2,1},{3,2},{4,3},{5,4},{6,5},{7,6},{8,7},{9,8},{10,9},{11,1... | collective-permute-start | bytes 202760 | tf_op jit(solution)/shard_map/ppermute | solution.py:26
  26.8 0.1 collective-permute-done.3
  26.9 0.3 copy.14
  27.2 1.8 %collective-permute-done.2 = f32[16,88,12]{1,0,2:T(8,128)S(1)} collective-permute-done((f32[16,88,12]{1,0,2:T(8,128)S(1)}, f32[16,88,12]{1,0,2:T(8,128)S(1)}, u32[]{:S(2)}, u32[]{:S(2)}) %collective-permute-start.2) | collective-permute-done | bytes 67616 | tf_op jit(solution)/shard_map/ppermute | solution.py:26
  29.0 0.3 copy.13
  29.3 0.0 copy-done
  29.3 1.7 %pad_maximum_fusion.f_ref = f32[16,88,384]{2,1,0:T(8,128)} fusion(f32[16,88,12]{2,1,0:T(8,128)S(1)} %copy.14, f32[16,88,12]{2,1,0:T(8,128)S(1)} %copy.13, f32[16,12,256]{2,1,0:T(8,128)S(1)} %collective-permute-done.1, f32[16,12,256]{2,1,0:T(8,128)S(1)} %collective-permute-done, f32[16,64,256]{2,1,0:T(8,128)S(1)} %copy-done, f32[384]{0:T(512)S(1)} %pad.20.clone), kind=kLoop, calls=%fused_computation.5 | loop fusion | flops 2703360 | bytes 3741184 | tf_op jit(solution)/shard_map/concatenate | solution.py:32
  31.0 4.3 %shard_map.104 = f32[4]{0:T(128)} custom-call(f32[16,88,384]{2,1,0:T(8,128)} %pad_maximum_fusion.f_ref), custom_call_target="tpu_custom_call" | custom-call | tf_op jit(solution)/shard_map/pallas_call | solution.py:325
  35.3 0.1 collective-permute-start.4
  35.4 1.3 %collective-permute-done.4 = f32[4]{0:T(128)S(1)} collective-permute-done((f32[4]{0:T(128)}, f32[4]{0:T(128)S(1)}, u32[]{:S(2)}, u32[]{:S(2)}) %collective-permute-start.4) | collective-permute-done | bytes 48 | tf_op jit(solution)/shard_map/ppermute | solution.py:60
  36.6 0.7 pad_maximum_fusion.5
  37.3 0.6 gather_fusion
  37.9 0.8 collective-permute-start.7
  38.7 1.4 %collective-permute-start.6 = (f32[4]{0:T(128)S(1)}, f32[4]{0:T(128)S(1)}, u32[]{:S(2)}, u32[]{:S(2)}) collective-permute-start(f32[4]{0:T(128)S(1)} %fusion.14), channel_id=1, source_target_pairs={{4,0},{5,1},{6,2},{7,3},{0,4},{1,5},{2,6},{3,7},{12,8},{13,9},{14,... | collective-permute-start | bytes 56 | tf_op jit(solution)/shard_map/ppermute | solution.py:60
  40.1 2.5 %collective-permute-start.5 = (f32[4]{0:T(128)S(1)}, f32[4]{0:T(128)S(1)}, u32[]{:S(2)}, u32[]{:S(2)}) collective-permute-start(f32[4]{0:T(128)S(1)} %fusion.14), channel_id=1, source_target_pairs={{2,0},{3,1},{4,2},{5,3},{6,4},{7,5},{0,6},{1,7},{10,8},{11,9},{12,... | collective-permute-start | bytes 56 | tf_op jit(solution)/shard_map/ppermute | solution.py:60
  42.6 0.2 collective-permute-done.7
  42.7 1.0 %collective-permute-done.6 = f32[4]{0:T(128)S(1)} collective-permute-done((f32[4]{0:T(128)S(1)}, f32[4]{0:T(128)S(1)}, u32[]{:S(2)}, u32[]{:S(2)}) %collective-permute-start.6) | collective-permute-done | bytes 48 | tf_op jit(solution)/shard_map/ppermute | solution.py:60
  43.8 0.1 collective-permute-done.5
  43.9 0.6 gather_fusion.1
  44.4 3.5 %collective-permute-start.10 = (f32[4]{0:T(128)S(1)}, f32[4]{0:T(128)S(1)}, u32[]{:S(2)}, u32[]{:S(2)}) collective-permute-start(f32[4]{0:T(128)S(1)} %fusion.13), channel_id=1, source_target_pairs={{24,0},{25,1},{26,2},{27,3},{28,4},{29,5},{30,6},{31,7},{0,8},{1,9... | collective-permute-start | bytes 56 | tf_op jit(solution)/shard_map/ppermute | solution.py:60
  48.0 2.3 %collective-permute-start.9 = (f32[4]{0:T(128)S(1)}, f32[4]{0:T(128)S(1)}, u32[]{:S(2)}, u32[]{:S(2)}) collective-permute-start(f32[4]{0:T(128)S(1)} %fusion.13), channel_id=1, source_target_pairs={{16,0},{17,1},{18,2},{19,3},{20,4},{21,5},{22,6},{23,7},{24,8},{25... | collective-permute-start | bytes 56 | tf_op jit(solution)/shard_map/ppermute | solution.py:60
  50.3 0.1 collective-permute-start.8
  50.4 0.0 collective-permute-done.10
  50.4 2.6 %collective-permute-done.9 = f32[4]{0:T(128)S(1)} collective-permute-done((f32[4]{0:T(128)S(1)}, f32[4]{0:T(128)S(1)}, u32[]{:S(2)}, u32[]{:S(2)}) %collective-permute-start.9) | collective-permute-done | bytes 48 | tf_op jit(solution)/shard_map/ppermute | solution.py:60
  53.1 2.0 %collective-permute-done.8 = f32[4]{0:T(128)S(1)} collective-permute-done((f32[4]{0:T(128)S(1)}, f32[4]{0:T(128)S(1)}, u32[]{:S(2)}, u32[]{:S(2)}) %collective-permute-start.8) | collective-permute-done | bytes 48 | tf_op jit(solution)/shard_map/ppermute | solution.py:60
  55.1 0.6 gather_fusion.2
  55.6 2.0 %collective-permute-start.11 = (f32[4]{0:T(128)S(1)}, f32[4]{0:T(128)S(1)}, u32[]{:S(2)}, u32[]{:S(2)}) collective-permute-start(f32[4]{0:T(128)S(1)} %fusion.12), channel_id=1, source_target_pairs={{32,0},{0,32},{96,64},{64,96},{160,128},{128,160},{224,192},{192,2... | collective-permute-start | bytes 56 | tf_op jit(solution)/shard_map/ppermute | solution.py:60
  57.7 1.7 %collective-permute-done.11 = f32[4]{0:T(128)S(1)} collective-permute-done((f32[4]{0:T(128)S(1)}, f32[4]{0:T(128)S(1)}, u32[]{:S(2)}, u32[]{:S(2)}) %collective-permute-start.11) | collective-permute-done | bytes 48 | tf_op jit(solution)/shard_map/ppermute | solution.py:60
  59.3 0.6 gather_fusion.3
  59.9 5.5 %collective-permute-start.14 = (f32[4]{0:T(128)S(1)}, f32[4]{0:T(128)S(1)}, u32[]{:S(2)}, u32[]{:S(2)}) collective-permute-start(f32[4]{0:T(128)S(1)} %fusion.11), channel_id=1, source_target_pairs={{192,0},{224,32},{0,64},{32,96},{64,128},{96,160},{128,192},{160,2... | collective-permute-start | bytes 56 | tf_op jit(solution)/shard_map/ppermute | solution.py:60
  65.4 2.2 %collective-permute-start.13 = (f32[4]{0:T(128)S(1)}, f32[4]{0:T(128)S(1)}, u32[]{:S(2)}, u32[]{:S(2)}) collective-permute-start(f32[4]{0:T(128)S(1)} %fusion.11), channel_id=1, source_target_pairs={{128,0},{160,32},{192,64},{224,96},{0,128},{32,160},{64,192},{96,2... | collective-permute-start | bytes 56 | tf_op jit(solution)/shard_map/ppermute | solution.py:60
  67.5 2.7 %collective-permute-start.12 = (f32[4]{0:T(128)S(1)}, f32[4]{0:T(128)S(1)}, u32[]{:S(2)}, u32[]{:S(2)}) collective-permute-start(f32[4]{0:T(128)S(1)} %fusion.11), channel_id=1, source_target_pairs={{64,0},{96,32},{128,64},{160,96},{192,128},{224,160},{0,192},{32,2... | collective-permute-start | bytes 56 | tf_op jit(solution)/shard_map/ppermute | solution.py:60
  70.2 0.0 collective-permute-done.14
  70.2 2.6 %collective-permute-done.13 = f32[4]{0:T(128)S(1)} collective-permute-done((f32[4]{0:T(128)S(1)}, f32[4]{0:T(128)S(1)}, u32[]{:S(2)}, u32[]{:S(2)}) %collective-permute-start.13) | collective-permute-done | bytes 48 | tf_op jit(solution)/shard_map/ppermute | solution.py:60
  72.8 0.0 collective-permute-done.12
  72.9 0.6 gather_fusion.4
  73.4 0.5 add_bitcast_fusion.s_ref
  73.9 7.6 %shard_map.105 = (f32[64,256]{1,0:T(8,128)}, f32[64,256]{1,0:T(8,128)}, f32[1]{0:T(128)}) custom-call(f32[4]{0:T(128)} %add_bitcast_fusion.s_ref, f32[16,88,384]{2,1,0:T(8,128)} %pad_maximum_fusion.f_ref), custom_call_target="tpu_custom_call" | custom-call | tf_op jit(solution)/shard_map/pallas_call | solution.py:334
  (23 shorter events, 0.2 us)
Async XLA Ops:
  3.0 9.7 %collective-permute-start.1 = (f32[16,12,256]{2,1,0:T(8,128)}, f32[16,12,256]{2,1,0:T(8,128)S(1)}, u32[]{:S(2)}, u32[]{:S(2)}) collective-permute-start(f32[16,12,256]{2,1,0:T(8,128)} %get-tuple-element.11), channel_id=1, source_target_pairs={{0,32},{32,64},{64,96},{96,128},{128,160},{160,192},{192,224},{1,3... | collective-permute-start | bytes 589832 | tf_op jit(solution)/shard_map/ppermute | solution.py:20
  6.8 10.0 %collective-permute-start = (f32[16,12,256]{2,1,0:T(8,128)}, f32[16,12,256]{2,1,0:T(8,128)S(1)}, u32[]{:S(2)}, u32[]{:S(2)}) collective-permute-start(f32[16,12,256]{2,1,0:T(8,128)} %get-tuple-element.10), channel_id=1, source_target_pairs={{32,0},{64,32},{96,64},{128,96},{160,128},{192,160},{224,192},{33,... | collective-permute-start | bytes 589832 | tf_op jit(solution)/shard_map/ppermute | solution.py:21
  18.4 10.8 %copy-start = (f32[16,64,256]{2,1,0:T(8,128)S(1)}, f32[16,64,256]{2,1,0:T(8,128)}, u32[]{:S(2)}) copy-start(f32[16,64,256]{2,1,0:T(8,128)} %get-tuple-element.9) | copy-start | bytes 3145732
  18.7 8.2 %collective-permute-start.3 = (f32[16,88,12]{1,0,2:T(8,128)S(1)}, f32[16,88,12]{1,0,2:T(8,128)S(1)}, u32[]{:S(2)}, u32[]{:S(2)}) collective-permute-start(f32[16,88,12]{1,0,2:T(8,128)S(1)} %copy.12), channel_id=1, source_target_pairs={{0,1},{1,2},{2,3},{3,4},{4,5},{5,6},{6,7},{7,8},{8,9},{9,10},{10,1... | collective-permute-start | bytes 202760 | tf_op jit(solution)/shard_map/ppermute | solution.py:23
  21.0 8.0 %collective-permute-start.2 = (f32[16,88,12]{1,0,2:T(8,128)S(1)}, f32[16,88,12]{1,0,2:T(8,128)S(1)}, u32[]{:S(2)}, u32[]{:S(2)}) collective-permute-start(f32[16,88,12]{1,0,2:T(8,128)S(1)} %copy.11), channel_id=1, source_target_pairs={{1,0},{2,1},{3,2},{4,3},{5,4},{6,5},{7,6},{8,7},{9,8},{10,9},{11,1... | collective-permute-start | bytes 202760 | tf_op jit(solution)/shard_map/ppermute | solution.py:26
  35.3 1.4 %collective-permute-start.4 = (f32[4]{0:T(128)}, f32[4]{0:T(128)S(1)}, u32[]{:S(2)}, u32[]{:S(2)}) collective-permute-start(f32[4]{0:T(128)} %shard_map.104), channel_id=1, source_target_pairs={{1,0},{0,1},{3,2},{2,3},{5,4},{4,5},{7,6},{6,7},{9,8},{8,9},{11,10... | collective-permute-start | bytes 56 | tf_op jit(solution)/shard_map/ppermute | solution.py:60
  37.9 4.9 %collective-permute-start.7 = (f32[4]{0:T(128)S(1)}, f32[4]{0:T(128)S(1)}, u32[]{:S(2)}, u32[]{:S(2)}) collective-permute-start(f32[4]{0:T(128)S(1)} %fusion.14), channel_id=1, source_target_pairs={{6,0},{7,1},{0,2},{1,3},{2,4},{3,5},{4,6},{5,7},{14,8},{15,9},{8,1... | collective-permute-start | bytes 56 | tf_op jit(solution)/shard_map/ppermute | solution.py:60
  38.7 5.1 %collective-permute-start.6 = (f32[4]{0:T(128)S(1)}, f32[4]{0:T(128)S(1)}, u32[]{:S(2)}, u32[]{:S(2)}) collective-permute-start(f32[4]{0:T(128)S(1)} %fusion.14), channel_id=1, source_target_pairs={{4,0},{5,1},{6,2},{7,3},{0,4},{1,5},{2,6},{3,7},{12,8},{13,9},{14,... | collective-permute-start | bytes 56 | tf_op jit(solution)/shard_map/ppermute | solution.py:60
  40.1 3.8 %collective-permute-start.5 = (f32[4]{0:T(128)S(1)}, f32[4]{0:T(128)S(1)}, u32[]{:S(2)}, u32[]{:S(2)}) collective-permute-start(f32[4]{0:T(128)S(1)} %fusion.14), channel_id=1, source_target_pairs={{2,0},{3,1},{4,2},{5,3},{6,4},{7,5},{0,6},{1,7},{10,8},{11,9},{12,... | collective-permute-start | bytes 56 | tf_op jit(solution)/shard_map/ppermute | solution.py:60
  44.4 6.0 %collective-permute-start.10 = (f32[4]{0:T(128)S(1)}, f32[4]{0:T(128)S(1)}, u32[]{:S(2)}, u32[]{:S(2)}) collective-permute-start(f32[4]{0:T(128)S(1)} %fusion.13), channel_id=1, source_target_pairs={{24,0},{25,1},{26,2},{27,3},{28,4},{29,5},{30,6},{31,7},{0,8},{1,9... | collective-permute-start | bytes 56 | tf_op jit(solution)/shard_map/ppermute | solution.py:60
  48.0 5.1 %collective-permute-start.9 = (f32[4]{0:T(128)S(1)}, f32[4]{0:T(128)S(1)}, u32[]{:S(2)}, u32[]{:S(2)}) collective-permute-start(f32[4]{0:T(128)S(1)} %fusion.13), channel_id=1, source_target_pairs={{16,0},{17,1},{18,2},{19,3},{20,4},{21,5},{22,6},{23,7},{24,8},{25... | collective-permute-start | bytes 56 | tf_op jit(solution)/shard_map/ppermute | solution.py:60
  50.3 4.8 %collective-permute-start.8 = (f32[4]{0:T(128)S(1)}, f32[4]{0:T(128)S(1)}, u32[]{:S(2)}, u32[]{:S(2)}) collective-permute-start(f32[4]{0:T(128)S(1)} %fusion.13), channel_id=1, source_target_pairs={{8,0},{9,1},{10,2},{11,3},{12,4},{13,5},{14,6},{15,7},{16,8},{17,9... | collective-permute-start | bytes 56 | tf_op jit(solution)/shard_map/ppermute | solution.py:60
  55.6 3.7 %collective-permute-start.11 = (f32[4]{0:T(128)S(1)}, f32[4]{0:T(128)S(1)}, u32[]{:S(2)}, u32[]{:S(2)}) collective-permute-start(f32[4]{0:T(128)S(1)} %fusion.12), channel_id=1, source_target_pairs={{32,0},{0,32},{96,64},{64,96},{160,128},{128,160},{224,192},{192,2... | collective-permute-start | bytes 56 | tf_op jit(solution)/shard_map/ppermute | solution.py:60
  59.9 10.3 %collective-permute-start.14 = (f32[4]{0:T(128)S(1)}, f32[4]{0:T(128)S(1)}, u32[]{:S(2)}, u32[]{:S(2)}) collective-permute-start(f32[4]{0:T(128)S(1)} %fusion.11), channel_id=1, source_target_pairs={{192,0},{224,32},{0,64},{32,96},{64,128},{96,160},{128,192},{160,2... | collective-permute-start | bytes 56 | tf_op jit(solution)/shard_map/ppermute | solution.py:60
  65.4 7.5 %collective-permute-start.13 = (f32[4]{0:T(128)S(1)}, f32[4]{0:T(128)S(1)}, u32[]{:S(2)}, u32[]{:S(2)}) collective-permute-start(f32[4]{0:T(128)S(1)} %fusion.11), channel_id=1, source_target_pairs={{128,0},{160,32},{192,64},{224,96},{0,128},{32,160},{64,192},{96,2... | collective-permute-start | bytes 56 | tf_op jit(solution)/shard_map/ppermute | solution.py:60
  67.5 5.3 %collective-permute-start.12 = (f32[4]{0:T(128)S(1)}, f32[4]{0:T(128)S(1)}, u32[]{:S(2)}, u32[]{:S(2)}) collective-permute-start(f32[4]{0:T(128)S(1)} %fusion.11), channel_id=1, source_target_pairs={{64,0},{96,32},{128,64},{160,96},{192,128},{224,160},{0,192},{32,2... | collective-permute-start | bytes 56 | tf_op jit(solution)/shard_map/ppermute | solution.py:60

commit v8 on v6

--- a/solution.py
+++ b/solution.py
@@ -11,26 +11,22 @@
 
 
 def wrapped_patch(block, width, first_rows, last_rows):
-    pieces = {}
-    for axis, dim in (("gy", 1), ("gx", 2)):
-        count = lax.axis_size(axis)
-        forward = [(i, i + 1) for i in range(count - 1)]
-        backward = [(target, source) for source, target in forward]
-        if dim == 1:
-            before = lax.ppermute(last_rows, axis, forward)
-            after = lax.ppermute(first_rows, axis, backward)
-        else:
-            before = lax.ppermute(
-                lax.slice_in_dim(block, block.shape[dim] - width, None, axis=dim), axis, forward
-            )
-            after = lax.ppermute(lax.slice_in_dim(block, 0, width, axis=dim), axis, backward)
-        if dim == 1:
-            block = jnp.concatenate([block, after, before], axis=dim)
-        else:
-            lanes = -(-(block.shape[2] + 2 * width) // LANES) * LANES
-            gap = jnp.zeros(block.shape[:2] + (lanes - block.shape[2] - 2 * width,), block.dtype)
-            block = jnp.concatenate([block, after, gap, before], axis=dim)
-    return block
+    rows_axis = lax.axis_size("gy")
+    forward = [(i, i + 1) for i in range(rows_axis - 1)]
+    backward = [(target, source) for source, target in forward]
+    north = lax.ppermute(last_rows, "gy", forward)
+    south = lax.ppermute(first_rows, "gy", backward)
+    bands = (block, south, north)
+    cols_axis = lax.axis_size("gx")
+    forward = [(i, i + 1) for i in range(cols_axis - 1)]
+    backward = [(target, source) for source, target in forward]
+    cols = block.shape[2]
+    west = lax.ppermute(jnp.concatenate([b[..., cols - width :] for b in bands], axis=1), "gx", forward)
+    east = lax.ppermute(jnp.concatenate([b[..., :width] for b in bands], axis=1), "gx", backward)
+    lanes = -(-(cols + 2 * width) // LANES) * LANES
+    middle = jnp.concatenate(bands, axis=1)
+    gap = jnp.zeros(middle.shape[:2] + (lanes - cols - 2 * width,), block.dtype)
+    return jnp.concatenate([middle, east, gap, west], axis=2)
 
 
 def butterfly_sum(values, axes):

time: 81 us -> 79.5 us (0.981)
  waiting for transfers between devices: 33.3 us -> 30.9 us
  local copies, waits for them, and re-layouts: 1.41 us -> 3.52 us
  other arithmetic: 4.31 us -> 3.17 us
    ppermute x4, waiting for transfers between devices: 11.5 us -> 9.11 us  [the longest x1 5.69 us: wrapped_patch(): lax.ppermute(jnp.concatenate([b[..., cols - width:] for b in bands], axis...]
    slice x3 -> x9, local copies, waits for them, and re-layouts: 0.76 us -> 2.87 us  [the longest x6 2.23 us: wrapped_patch(): b[..., :width]]
    concatenate x2 -> x3, other arithmetic: 3.04 us -> 1.92 us  [the longest x1 1.68 us: wrapped_patch(): return jnp.concatenate([middle, east, gap, west], axis=2)]
  transfers between devices with their start and end apart: 12 -> 12, of which waited for: 11 -> 12; matrix products, arithmetic and copies ran while one was open for 1% -> 4% of each run, Pallas kernels for 0% -> 0%
where the time goes in v8:
time: 79.5 us; the launch traced here: 79.2 us
  waiting for transfers between devices  30.9 us (39%)
  starting transfers between devices  26.4 us (33%)
  Pallas kernels  14.2 us (18%)
  local copies, waits for them, and re-layouts  3.52 us (4%)
  other arithmetic  3.17 us (4%)
  between operations  0.93 us (1%)
    ppermute x8, waiting for transfers between devices, butterfly_sum(): lax.ppermute(values, axis, [(i, i ^ stride) for i in range(count)])  21.8 us
    ppermute x8, starting transfers between devices, butterfly_sum(): lax.ppermute(values, axis, [(i, i ^ stride) for i in range(count)])  15.3 us
    pallas_call x1, Pallas kernels, run_backward(): pl.pallas_call(backward_kernel(steps, rows, cols, cell_count), out_shape=...  7.63 us
    ppermute x1, waiting for transfers between devices, wrapped_patch(): lax.ppermute(jnp.concatenate([b[..., cols - width:] for b in bands], axis...  5.69 us
    ppermute x1, starting transfers between devices, wrapped_patch(): north = lax.ppermute(last_rows, 'gy', forward)  4.56 us
    pallas_call x1, Pallas kernels, run_forward(): pl.pallas_call(forward_kernel(steps, rows, cols), out_shape=jax.ShapeDtyp...  4.29 us
    ppermute x1, starting transfers between devices, wrapped_patch(): lax.ppermute(jnp.concatenate([b[..., :width] for b in bands], axis=1), 'g...  3.33 us
    ppermute x1, waiting for transfers between devices, wrapped_patch(): south = lax.ppermute(first_rows, 'gy', backward)  2.61 us
  transfers between devices with their start and end apart: 12, of which 12 were waited for; matrix products, arithmetic and copies ran while one was open for 4% of the time, Pallas kernels for 0%

profile of v8, /device:TPU:24, one launch (start us, length us, event | category | flops | bytes accessed | tf_op | source)
XLA Modules:
  0.0 79.2 jit_solution(3216035110887155916)
XLA Ops:
  0.6 2.3 %shard_map.103 = (f32[16,64,256]{2,1,0:T(8,128)}, f32[16,12,256]{2,1,0:T(8,128)}, f32[16,12,256]{2,1,0:T(8,128)}) custom-call(bf16[2,64,256]{2,1,0:T(8,128)(2,1)} %thick_ref.1, bf16[2,2,64,256]{3,2,1,0:T(8,128)(2,1)} %vel_ref.1, bf16[2,64,256]{2,1,0:T(8,128)(2,1)} %slope_ref.1, f32[64,256]{1,0:T(8,128)} %beta_ref.1, s32[64,256]{1,0:T(8,128)} %mask_ref.1, ...), custom_call_target="tpu_custom_call" | custom-call | tf_op jit(solution)/shard_map/pallas_call | solution.py:287
  3.0 1.3 %collective-permute-start = (f32[16,12,256]{2,1,0:T(8,128)}, f32[16,12,256]{2,1,0:T(8,128)S(1)}, u32[]{:S(2)}, u32[]{:S(2)}) collective-permute-start(f32[16,12,256]{2,1,0:T(8,128)} %get-tuple-element.10), channel_id=1, source_target_pairs={{32,0},{64,32},{96,64},{128,96},{160,128},{192,160},{224,192},{33,... | collective-permute-start | bytes 589832 | tf_op jit(solution)/shard_map/ppermute | solution.py:18
  4.2 4.6 %collective-permute-start.1 = (f32[16,12,256]{2,1,0:T(8,128)}, f32[16,12,256]{2,1,0:T(8,128)S(1)}, u32[]{:S(2)}, u32[]{:S(2)}) collective-permute-start(f32[16,12,256]{2,1,0:T(8,128)} %get-tuple-element.11), channel_id=1, source_target_pairs={{0,32},{32,64},{64,96},{96,128},{128,160},{160,192},{192,224},{1,3... | collective-permute-start | bytes 589832 | tf_op jit(solution)/shard_map/ppermute | solution.py:17
  8.8 1.4 %fusion = (f32[16,64,12]{2,1,0:T(8,128)S(1)}, f32[16,64,12]{2,1,0:T(8,128)S(1)}) fusion(f32[16,64,256]{2,1,0:T(8,128)} %get-tuple-element.9), kind=kLoop, calls=%fused_computation.3 | loop fusion | bytes 196608 | tf_op jit(solution)/shard_map/slice | solution.py:25
  10.2 0.2 copy.11
  10.4 0.2 copy.14
  10.7 0.0 copy-start
  10.7 2.6 %collective-permute-done = f32[16,12,256]{2,1,0:T(8,128)S(1)} collective-permute-done((f32[16,12,256]{2,1,0:T(8,128)}, f32[16,12,256]{2,1,0:T(8,128)S(1)}, u32[]{:S(2)}, u32[]{:S(2)}) %collective-permute-start) | collective-permute-done | bytes 196640 | tf_op jit(solution)/shard_map/ppermute | solution.py:18
  13.3 0.1 fusion.1
  13.4 0.2 copy.12
  13.6 0.2 copy.15
  13.8 0.8 collective-permute-done.1
  14.6 0.1 fusion.2
  14.7 0.2 copy.13
  14.9 0.2 copy.16
  15.1 0.1 pad_maximum_fusion.1
  15.2 3.3 %collective-permute-start.2 = (f32[16,88,12]{1,0,2:T(8,128)S(1)}, f32[16,88,12]{1,0,2:T(8,128)S(1)}, u32[]{:S(2)}, u32[]{:S(2)}) collective-permute-start(f32[16,88,12]{1,0,2:T(8,128)S(1)} %pad_maximum_fusion.1), channel_id=1, source_target_pairs={{1,0},{2,1},{3,2},{4,3},{5,4},{6,5},{7,6},{8,7},{9,8},{10,9},{11,1... | collective-permute-start | bytes 202760 | tf_op jit(solution)/shard_map/ppermute | solution.py:25
  18.6 0.1 pad_maximum_fusion.2
  18.7 1.9 %collective-permute-start.3 = (f32[16,88,12]{1,0,2:T(8,128)S(1)}, f32[16,88,12]{1,0,2:T(8,128)S(1)}, u32[]{:S(2)}, u32[]{:S(2)}) collective-permute-start(f32[16,88,12]{1,0,2:T(8,128)S(1)} %pad_maximum_fusion.2), channel_id=1, source_target_pairs={{0,1},{1,2},{2,3},{3,4},{4,5},{5,6},{6,7},{7,8},{8,9},{9,10},{10,1... | collective-permute-start | bytes 202760 | tf_op jit(solution)/shard_map/ppermute | solution.py:24
  20.6 0.1 pad.4.clone
  20.7 0.1 collective-permute-done.2
  20.8 0.3 copy.17
  21.0 5.7 %collective-permute-done.3 = f32[16,88,12]{1,0,2:T(8,128)S(1)} collective-permute-done((f32[16,88,12]{1,0,2:T(8,128)S(1)}, f32[16,88,12]{1,0,2:T(8,128)S(1)}, u32[]{:S(2)}, u32[]{:S(2)}) %collective-permute-start.3) | collective-permute-done | bytes 67616 | tf_op jit(solution)/shard_map/ppermute | solution.py:24
  26.7 0.3 copy.18
  27.0 0.0 copy-done
  27.0 1.7 %pad_maximum_fusion.f_ref = f32[16,88,384]{2,1,0:T(8,128)} fusion(f32[16,88,12]{2,1,0:T(8,128)S(1)} %copy.18, f32[16,88,12]{2,1,0:T(8,128)S(1)} %copy.17, f32[16,12,256]{2,1,0:T(8,128)S(1)} %collective-permute-done.1, f32[16,12,256]{2,1,0:T(8,128)S(1)} %collective-permute-done, f32[16,64,256]{2,1,0:T(8,128)S(1)} %copy-done, f32[384]{0:T(512)S(1)} %pad.4.clone), kind=kLoop, calls=%fused_computation | loop fusion | flops 2703360 | bytes 3741184 | tf_op jit(solution)/shard_map/concatenate | solution.py:29
  28.7 4.3 %shard_map.104 = f32[4]{0:T(128)} custom-call(f32[16,88,384]{2,1,0:T(8,128)} %pad_maximum_fusion.f_ref), custom_call_target="tpu_custom_call" | custom-call | tf_op jit(solution)/shard_map/pallas_call | solution.py:300
  33.0 0.1 collective-permute-start.4
  33.1 1.3 %collective-permute-done.4 = f32[4]{0:T(128)S(1)} collective-permute-done((f32[4]{0:T(128)}, f32[4]{0:T(128)S(1)}, u32[]{:S(2)}, u32[]{:S(2)}) %collective-permute-start.4) | collective-permute-done | bytes 48 | tf_op jit(solution)/shard_map/ppermute | solution.py:40
  34.4 0.7 add.24
  35.0 0.0 collective-permute-start.5
  35.0 3.6 %collective-permute-done.5 = f32[4]{0:T(128)S(1)} collective-permute-done((f32[4]{0:T(128)S(1)}, f32[4]{0:T(128)S(1)}, u32[]{:S(2)}, u32[]{:S(2)}) %collective-permute-start.5) | collective-permute-done | bytes 48 | tf_op jit(solution)/shard_map/ppermute | solution.py:40
  38.6 0.0 collective-permute-start.6
  38.6 5.1 %collective-permute-done.6 = f32[4]{0:T(128)S(1)} collective-permute-done((f32[4]{0:T(128)S(1)}, f32[4]{0:T(128)S(1)}, u32[]{:S(2)}, u32[]{:S(2)}) %collective-permute-start.6) | collective-permute-done | bytes 48 | tf_op jit(solution)/shard_map/ppermute | solution.py:40
  43.7 0.4 collective-permute-start.7
  44.1 3.1 %collective-permute-done.7 = f32[4]{0:T(128)S(1)} collective-permute-done((f32[4]{0:T(128)S(1)}, f32[4]{0:T(128)S(1)}, u32[]{:S(2)}, u32[]{:S(2)}) %collective-permute-start.7) | collective-permute-done | bytes 48 | tf_op jit(solution)/shard_map/ppermute | solution.py:40
  47.3 0.9 %collective-permute-start.8 = (f32[4]{0:T(128)S(1)}, f32[4]{0:T(128)S(1)}, u32[]{:S(2)}, u32[]{:S(2)}) collective-permute-start(f32[4]{0:T(128)S(1)} %add.27), channel_id=1, source_target_pairs={{0,16},{1,17},{2,18},{3,19},{4,20},{5,21},{6,22},{7,23},{8,24},{9,... | collective-permute-start | bytes 56 | tf_op jit(solution)/shard_map/ppermute | solution.py:40
  48.2 4.1 %collective-permute-done.8 = f32[4]{0:T(128)S(1)} collective-permute-done((f32[4]{0:T(128)S(1)}, f32[4]{0:T(128)S(1)}, u32[]{:S(2)}, u32[]{:S(2)}) %collective-permute-start.8) | collective-permute-done | bytes 48 | tf_op jit(solution)/shard_map/ppermute | solution.py:40
  52.3 2.4 %collective-permute-start.9 = (f32[4]{0:T(128)S(1)}, f32[4]{0:T(128)S(1)}, u32[]{:S(2)}, u32[]{:S(2)}) collective-permute-start(f32[4]{0:T(128)S(1)} %add.28), channel_id=1, source_target_pairs={{0,32},{32,0},{64,96},{96,64},{128,160},{160,128},{192,224},{224,1... | collective-permute-start | bytes 56 | tf_op jit(solution)/shard_map/ppermute | solution.py:40
  54.7 1.5 %collective-permute-done.9 = f32[4]{0:T(128)S(1)} collective-permute-done((f32[4]{0:T(128)S(1)}, f32[4]{0:T(128)S(1)}, u32[]{:S(2)}, u32[]{:S(2)}) %collective-permute-start.9) | collective-permute-done | bytes 48 | tf_op jit(solution)/shard_map/ppermute | solution.py:40
  56.3 4.0 %collective-permute-start.10 = (f32[4]{0:T(128)S(1)}, f32[4]{0:T(128)S(1)}, u32[]{:S(2)}, u32[]{:S(2)}) collective-permute-start(f32[4]{0:T(128)S(1)} %add.29), channel_id=1, source_target_pairs={{0,64},{32,96},{64,0},{96,32},{128,192},{160,224},{192,128},{224,1... | collective-permute-start | bytes 56 | tf_op jit(solution)/shard_map/ppermute | solution.py:40
  60.3 1.5 %collective-permute-done.10 = f32[4]{0:T(128)S(1)} collective-permute-done((f32[4]{0:T(128)S(1)}, f32[4]{0:T(128)S(1)}, u32[]{:S(2)}, u32[]{:S(2)}) %collective-permute-start.10) | collective-permute-done | bytes 48 | tf_op jit(solution)/shard_map/ppermute | solution.py:40
  61.8 7.4 %collective-permute-start.11 = (f32[4]{0:T(128)S(1)}, f32[4]{0:T(128)S(1)}, u32[]{:S(2)}, u32[]{:S(2)}) collective-permute-start(f32[4]{0:T(128)S(1)} %add.30), channel_id=1, source_target_pairs={{0,128},{32,160},{64,192},{96,224},{128,0},{160,32},{192,64},{224,... | collective-permute-start | bytes 56 | tf_op jit(solution)/shard_map/ppermute | solution.py:40
  69.3 1.5 %collective-permute-done.11 = f32[4]{0:T(128)S(1)} collective-permute-done((f32[4]{0:T(128)S(1)}, f32[4]{0:T(128)S(1)}, u32[]{:S(2)}, u32[]{:S(2)}) %collective-permute-start.11) | collective-permute-done | bytes 48 | tf_op jit(solution)/shard_map/ppermute | solution.py:40
  70.8 0.6 add.31.s_ref
  71.4 7.6 %shard_map.105 = (f32[64,256]{1,0:T(8,128)}, f32[64,256]{1,0:T(8,128)}, f32[1]{0:T(128)}) custom-call(f32[4]{0:T(128)} %add.31.s_ref, f32[16,88,384]{2,1,0:T(8,128)} %pad_maximum_fusion.f_ref), custom_call_target="tpu_custom_call" | custom-call | tf_op jit(solution)/shard_map/pallas_call | solution.py:309
  (7 shorter events, 0.0 us)
Async XLA Ops:
  3.0 10.3 %collective-permute-start = (f32[16,12,256]{2,1,0:T(8,128)}, f32[16,12,256]{2,1,0:T(8,128)S(1)}, u32[]{:S(2)}, u32[]{:S(2)}) collective-permute-start(f32[16,12,256]{2,1,0:T(8,128)} %get-tuple-element.10), channel_id=1, source_target_pairs={{32,0},{64,32},{96,64},{128,96},{160,128},{192,160},{224,192},{33,... | collective-permute-start | bytes 589832 | tf_op jit(solution)/shard_map/ppermute | solution.py:18
  4.2 10.3 %collective-permute-start.1 = (f32[16,12,256]{2,1,0:T(8,128)}, f32[16,12,256]{2,1,0:T(8,128)S(1)}, u32[]{:S(2)}, u32[]{:S(2)}) collective-permute-start(f32[16,12,256]{2,1,0:T(8,128)} %get-tuple-element.11), channel_id=1, source_target_pairs={{0,32},{32,64},{64,96},{96,128},{128,160},{160,192},{192,224},{1,3... | collective-permute-start | bytes 589832 | tf_op jit(solution)/shard_map/ppermute | solution.py:17
  10.7 16.4 %copy-start = (f32[16,64,256]{2,1,0:T(8,128)S(1)}, f32[16,64,256]{2,1,0:T(8,128)}, u32[]{:S(2)}) copy-start(f32[16,64,256]{2,1,0:T(8,128)} %get-tuple-element.9) | copy-start | bytes 3145732
  15.2 5.5 %collective-permute-start.2 = (f32[16,88,12]{1,0,2:T(8,128)S(1)}, f32[16,88,12]{1,0,2:T(8,128)S(1)}, u32[]{:S(2)}, u32[]{:S(2)}) collective-permute-start(f32[16,88,12]{1,0,2:T(8,128)S(1)} %pad_maximum_fusion.1), channel_id=1, source_target_pairs={{1,0},{2,1},{3,2},{4,3},{5,4},{6,5},{7,6},{8,7},{9,8},{10,9},{11,1... | collective-permute-start | bytes 202760 | tf_op jit(solution)/shard_map/ppermute | solution.py:25
  18.7 8.0 %collective-permute-start.3 = (f32[16,88,12]{1,0,2:T(8,128)S(1)}, f32[16,88,12]{1,0,2:T(8,128)S(1)}, u32[]{:S(2)}, u32[]{:S(2)}) collective-permute-start(f32[16,88,12]{1,0,2:T(8,128)S(1)} %pad_maximum_fusion.2), channel_id=1, source_target_pairs={{0,1},{1,2},{2,3},{3,4},{4,5},{5,6},{6,7},{7,8},{8,9},{9,10},{10,1... | collective-permute-start | bytes 202760 | tf_op jit(solution)/shard_map/ppermute | solution.py:24
  33.0 1.4 %collective-permute-start.4 = (f32[4]{0:T(128)}, f32[4]{0:T(128)S(1)}, u32[]{:S(2)}, u32[]{:S(2)}) collective-permute-start(f32[4]{0:T(128)} %shard_map.104), channel_id=1, source_target_pairs={{0,1},{1,0},{2,3},{3,2},{4,5},{5,4},{6,7},{7,6},{8,9},{9,8},{10,11... | collective-permute-start | bytes 56 | tf_op jit(solution)/shard_map/ppermute | solution.py:40
  35.0 3.6 %collective-permute-start.5 = (f32[4]{0:T(128)S(1)}, f32[4]{0:T(128)S(1)}, u32[]{:S(2)}, u32[]{:S(2)}) collective-permute-start(f32[4]{0:T(128)S(1)} %add.24), channel_id=1, source_target_pairs={{0,2},{1,3},{2,0},{3,1},{4,6},{5,7},{6,4},{7,5},{8,10},{9,11},{10,... | collective-permute-start | bytes 56 | tf_op jit(solution)/shard_map/ppermute | solution.py:40
  38.6 5.1 %collective-permute-start.6 = (f32[4]{0:T(128)S(1)}, f32[4]{0:T(128)S(1)}, u32[]{:S(2)}, u32[]{:S(2)}) collective-permute-start(f32[4]{0:T(128)S(1)} %add.25), channel_id=1, source_target_pairs={{0,4},{1,5},{2,6},{3,7},{4,0},{5,1},{6,2},{7,3},{8,12},{9,13},{10,... | collective-permute-start | bytes 56 | tf_op jit(solution)/shard_map/ppermute | solution.py:40
  43.7 3.6 %collective-permute-start.7 = (f32[4]{0:T(128)S(1)}, f32[4]{0:T(128)S(1)}, u32[]{:S(2)}, u32[]{:S(2)}) collective-permute-start(f32[4]{0:T(128)S(1)} %add.26), channel_id=1, source_target_pairs={{0,8},{1,9},{2,10},{3,11},{4,12},{5,13},{6,14},{7,15},{8,0},{9,1},... | collective-permute-start | bytes 56 | tf_op jit(solution)/shard_map/ppermute | solution.py:40
  47.3 5.1 %collective-permute-start.8 = (f32[4]{0:T(128)S(1)}, f32[4]{0:T(128)S(1)}, u32[]{:S(2)}, u32[]{:S(2)}) collective-permute-start(f32[4]{0:T(128)S(1)} %add.27), channel_id=1, source_target_pairs={{0,16},{1,17},{2,18},{3,19},{4,20},{5,21},{6,22},{7,23},{8,24},{9,... | collective-permute-start | bytes 56 | tf_op jit(solution)/shard_map/ppermute | solution.py:40
  52.3 3.9 %collective-permute-start.9 = (f32[4]{0:T(128)S(1)}, f32[4]{0:T(128)S(1)}, u32[]{:S(2)}, u32[]{:S(2)}) collective-permute-start(f32[4]{0:T(128)S(1)} %add.28), channel_id=1, source_target_pairs={{0,32},{32,0},{64,96},{96,64},{128,160},{160,128},{192,224},{224,1... | collective-permute-start | bytes 56 | tf_op jit(solution)/shard_map/ppermute | solution.py:40
  56.3 5.6 %collective-permute-start.10 = (f32[4]{0:T(128)S(1)}, f32[4]{0:T(128)S(1)}, u32[]{:S(2)}, u32[]{:S(2)}) collective-permute-start(f32[4]{0:T(128)S(1)} %add.29), channel_id=1, source_target_pairs={{0,64},{32,96},{64,0},{96,32},{128,192},{160,224},{192,128},{224,1... | collective-permute-start | bytes 56 | tf_op jit(solution)/shard_map/ppermute | solution.py:40
  61.8 9.0 %collective-permute-start.11 = (f32[4]{0:T(128)S(1)}, f32[4]{0:T(128)S(1)}, u32[]{:S(2)}, u32[]{:S(2)}) collective-permute-start(f32[4]{0:T(128)S(1)} %add.30), channel_id=1, source_target_pairs={{0,128},{32,160},{64,192},{96,224},{128,0},{160,32},{192,64},{224,... | collective-permute-start | bytes 56 | tf_op jit(solution)/shard_map/ppermute | solution.py:40
